TPU v7x, 256 devices: a whole 4x4x8 slice. The times are simulated.
256 devices in a mesh: region: 8 (over z), row: 32 (over y, x, core).
Axes of the slice: x: 4, y: 4, z: 8, core: 2. Of those that a mesh axis runs over, the one named last changes fastest.
Arguments:
- state0: float32 [32, 131072], P(None, ('region', 'row')), may hold values from -6 to 6
- drive: bfloat16 [32, 131072], P(None, ('region', 'row')), may hold values from -6 to 6
- cotangent: float32 [32, 131072], P(None, ('region', 'row')), may hold values from -6 to 6
- excitatory: int32 [131072], P(('region', 'row')), may hold values 0 or 1
- tile_vals: bfloat16 [1024, 24, 128, 128], P(('region', 'row')), may hold values from 0.0039978027 to 0.039794922
- tile_cols: int32 [1024, 24], P(('region', 'row')), may hold values from 0 to 159
- tile_count: int32 [1024], P(('region', 'row')), may hold values from 1 to 24, as said below
- boundary_rows: int32 [8, 32, 8, 16], P('region', 'row'), may hold values from 0 to 511, as said below
- u_factor: bfloat16 [32, 131072], P(None, ('region', 'row')), may hold values from -1 to 1
- v_factor: bfloat16 [32, 131072], P(None, ('region', 'row')), may hold values from -0.015625 to 0.015625
Outputs:
- final_state: float32 [32, 131072], P(None, ('region', 'row'))
- grad_u: float32 [32, 131072], P(None, ('region', 'row'))
- grad_v: float32 [32, 131072], P(None, ('region', 'row'))
Inputs may be any that keep to these rules, and one draw needn't show every extreme that they name: tile_count[q] tiles of row tile q are live; its tiles j >= tile_count[q] take no part; the most, 24, is reached in every draw. `boundary_rows`: the 16 rows of one list are distinct. tile_cols[q, j] numbers a tile of 128 extended columns of the group of row tile q.
All inputs are finite; a program needn't handle non-finite values. No bound on the sum of `excitatory` on one device may be relied on, other than what follows from the above.
Results may differ from a plain program's by a relative error of at most 0.0055.
Values may be sent and summed in bfloat16 or wider, within the bound.
No kernel may reach another device: no remote copies, remote signals or barrier semaphores. Data moves between devices by JAX's collectives and lax.ppermute only.
A program may use at most 64 MiB of HBM per device.

v0:
```python
import jax
import jax.numpy as jnp
from jax import lax
from jax.sharding import Mesh
from jax.sharding import PartitionSpec as P

STEPS = 4
ROW = ("row_0", "row_1", "row_2")
REGION_ROW = ("region", "row_0", "row_1", "row_2")


leak = 0.5


def from_each_region(chunks):
    width = chunks.shape[-1]
    padded = jnp.pad(chunks, ((0, 0), (0, 0), (0, -width % 128)))
    return lax.all_to_all(padded, "region", 0, 0, tiled=True)[..., :width]


def from_each_lane(slots):
    return lax.all_to_all(slots, ROW, 0, 0, tiled=True)


def from_every_lane(slots):
    chips = ROW[:-1]
    copies = jnp.broadcast_to(slots, (lax.axis_size(chips), *slots.shape))
    mine = lax.all_to_all(copies, chips, 0, 0, tiled=True)
    sibling = lax.ppermute(mine, ROW[-1], [(0, 1), (1, 0)])
    return jnp.stack([mine, sibling])


def split_pair(x):
    high = x.astype(jnp.bfloat16)
    low = (x - high.astype(jnp.float32)).astype(jnp.bfloat16)
    return jnp.concatenate([high, low], axis=-1)


def joined_pair(x):
    half = x.shape[-1] // 2
    return x[..., :half].astype(jnp.float32) + x[..., half:].astype(jnp.float32)


def local(
    state0,
    drive,
    cotangent,
    excitatory,
    tile_vals,
    tile_cols,
    tile_count,
    boundary_rows,
    u_factor,
    v_factor,
):
    lanes = lax.axis_size(ROW)
    groups = lax.axis_size("region")
    batch_rows, own_rows = state0.shape
    rank = v_factor.shape[0]
    own_tiles = own_rows // 128
    row_tiles = tile_vals.shape[0]
    chosen = boundary_rows.reshape(-1)
    bound_cols = chosen.shape[0]
    per_lane = own_tiles + bound_cols // 128
    tile_rows = per_lane * batch_rows
    sent = bound_cols // groups
    region_width = sent + rank
    flat_cols = tile_cols.reshape(-1)
    lane_of = flat_cols // per_lane
    cores = lax.axis_size(ROW[-1])
    side_of = (lane_of % cores != lax.axis_index(ROW[-1])).astype(jnp.int32)
    chip_of = lane_of // cores
    at_lane = flat_cols % per_lane
    live_grid = jnp.arange(tile_cols.shape[1], dtype=jnp.int32)[None, :] < tile_count[:, None]
    live_tiles = live_grid.reshape(-1)
    picks = (flat_cols[None, :] == jnp.arange(lanes * per_lane, dtype=jnp.int32)[:, None]) & live_tiles[None, :]
    picks = picks.astype(jnp.float32).reshape(lanes, per_lane, -1)
    half_rows = 16
    halves = batch_rows // half_rows
    payload_rows = tile_rows + batch_rows * 2 * rank // 128
    block_of = at_lane[:, None] * halves + jnp.arange(halves, dtype=jnp.int32)[None, :]
    picks_fwd = (
        (jnp.arange(cores, dtype=jnp.int32)[None, None, :, None, None] == side_of[:, None, None, None, None])
        & (jnp.arange(lanes // cores, dtype=jnp.int32)[None, None, None, :, None] == chip_of[:, None, None, None, None])
        & (jnp.arange(payload_rows // half_rows, dtype=jnp.int32)[None, None, None, None, :] == block_of[:, :, None, None, None])
        & live_tiles[:, None, None, None, None]
    ).astype(jnp.bfloat16)
    polarity = (2 * excitatory - 1).astype(jnp.float32)
    drive_f = drive.astype(jnp.float32)

    def forward_start(state):
        rates = jnp.tanh(state)
        signed = (polarity * rates).astype(jnp.bfloat16)
        outgoing = jnp.take(signed, chosen, axis=1).reshape(batch_rows, groups, sent)
        part_latent = jnp.dot(signed, v_factor.T, preferred_element_type=jnp.float32)
        chunks = jnp.concatenate(
            [
                jnp.moveaxis(outgoing, 1, 0).astype(jnp.float32),
                jnp.broadcast_to(part_latent, (groups, batch_rows, rank)),
            ],
            axis=2,
        )
        return rates, signed, chunks

    def forward_middle(signed, got):
        incoming = jnp.moveaxis(got[:, :, :sent], 0, 1).reshape(batch_rows, -1).astype(jnp.bfloat16)
        lane_latent = jnp.sum(got[:, :, sent:], axis=0)
        slots = jnp.concatenate(
            [
                jnp.moveaxis(signed.reshape(batch_rows, own_tiles, 128), 1, 0).reshape(-1, 128),
                incoming.reshape(batch_rows, -1),
                split_pair(lane_latent).reshape(-1, 128),
            ],
            axis=0,
        )
        return slots

    def forward_end(state, gathered):
        pair_rows = gathered[:, :, tile_rows:].reshape(lanes, batch_rows, 2 * rank)
        latent = jnp.sum(joined_pair(pair_rows), axis=0)
        stacked = gathered.reshape(*gathered.shape[:2], -1, half_rows, 128)
        blocks = jnp.einsum("shpcm,pcmrk->shrk", picks_fwd, stacked, preferred_element_type=jnp.bfloat16)
        blocks = blocks.reshape(row_tiles, -1, batch_rows, 128)
        synaptic = jnp.einsum("qjbk,qjik->bqi", blocks, tile_vals, preferred_element_type=jnp.float32)
        synaptic = synaptic.reshape(batch_rows, own_rows)
        latent_b = latent.astype(jnp.bfloat16)
        lowrank = jnp.dot(latent_b, u_factor, preferred_element_type=jnp.float32)
        return state + leak * (-state + synaptic + lowrank + drive_f), latent_b

    def adjoint_start(adjoint):
        scaled_b = (leak * adjoint).astype(jnp.bfloat16)
        part_coeff = jnp.dot(scaled_b, u_factor.T, preferred_element_type=jnp.float32)
        spread = jnp.einsum(
            "bri,rjik->brjk",
            scaled_b.reshape(batch_rows, row_tiles, 128),
            tile_vals,
            preferred_element_type=jnp.float32,
        )
        columns = jnp.einsum(
            "lts,bsk->ltbk", picks, spread.reshape(batch_rows, -1, 128), precision=lax.Precision.HIGHEST
        )
        pair_rows = split_pair(part_coeff).reshape(-1, 128)
        coeff_rows = jnp.broadcast_to(pair_rows, (lanes, *pair_rows.shape))
        tiles_rows = columns.astype(jnp.bfloat16).reshape(lanes, tile_rows, 128)
        return scaled_b, jnp.concatenate([tiles_rows, coeff_rows], axis=1)

    def adjoint_middle(got):
        everything = jnp.sum(got.astype(jnp.float32), axis=0)
        summed = everything[:tile_rows].reshape(per_lane, batch_rows, 128)
        pair_sums = everything[tile_rows:].reshape(batch_rows, 2 * rank)
        group_coeff = pair_sums[:, :rank] + pair_sums[:, rank:]
        own_part = jnp.moveaxis(summed[:own_tiles], 0, 1).reshape(batch_rows, own_rows)
        border = summed[own_tiles:].reshape(batch_rows, groups, sent)
        chunks = jnp.concatenate(
            [jnp.moveaxis(border, 1, 0), jnp.broadcast_to(group_coeff, (groups, batch_rows, rank))], axis=2
        )
        return own_part, chunks

    def adjoint_end(adjoint, own_part, back, rates):
        returned = jnp.moveaxis(back[:, :, :sent], 0, 1).reshape(batch_rows, -1)
        coeffs_b = jnp.sum(back[:, :, sent:], axis=0).astype(jnp.bfloat16)
        through = own_part.at[:, chosen].add(returned)
        total_signed = through + jnp.dot(coeffs_b, v_factor, preferred_element_type=jnp.float32)
        adjoint = (1.0 - leak) * adjoint + (1.0 - rates * rates) * polarity * total_signed
        return adjoint, coeffs_b

    def both_regions(first, second):
        got = from_each_region(jnp.concatenate([first, second], axis=2))
        return got[:, :, :region_width], got[:, :, region_width:]

    rates_of, signed_of, latent_of, scaled_of, coeffs_of = {}, {}, {}, {}, {}
    state = state0
    rates_of[0], signed_of[0], chunks = forward_start(state)
    got = from_each_region(chunks)
    scaled_of[3], lane_parts = adjoint_start(cotangent)
    got_last = from_each_lane(lane_parts)
    gathered = from_every_lane(forward_middle(signed_of[0], got))
    state, latent_of[0] = forward_end(state, gathered)
    own_last, chunks_last = adjoint_middle(got_last)
    rates_of[1], signed_of[1], chunks = forward_start(state)
    got, back_last = both_regions(chunks, chunks_last)
    gathered = from_every_lane(forward_middle(signed_of[1], got))
    state, latent_of[1] = forward_end(state, gathered)
    rates_of[2], signed_of[2], chunks = forward_start(state)
    got = from_each_region(chunks)
    gathered = from_every_lane(forward_middle(signed_of[2], got))
    state, latent_of[2] = forward_end(state, gathered)
    rates_of[3], signed_of[3], chunks_f3 = forward_start(state)
    adjoint, coeffs_of[3] = adjoint_end(cotangent, own_last, back_last, rates_of[3])
    scaled_of[2], lane_parts = adjoint_start(adjoint)
    own_part, chunks = adjoint_middle(from_each_lane(lane_parts))
    got_f3, back = both_regions(chunks_f3, chunks)
    adjoint, coeffs_of[2] = adjoint_end(adjoint, own_part, back, rates_of[2])
    scaled_of[1], lane_parts = adjoint_start(adjoint)
    gathered_f3 = from_every_lane(forward_middle(signed_of[3], got_f3))
    got = from_each_lane(lane_parts)
    final_state, latent_of[3] = forward_end(state, gathered_f3)
    own_part, chunks = adjoint_middle(got)
    adjoint, coeffs_of[1] = adjoint_end(adjoint, own_part, from_each_region(chunks), rates_of[1])
    scaled_of[0], lane_parts = adjoint_start(adjoint)
    own_part, chunks = adjoint_middle(from_each_lane(lane_parts))
    adjoint, coeffs_of[0] = adjoint_end(adjoint, own_part, from_each_region(chunks), rates_of[0])
    grad_u = jnp.zeros((rank, own_rows), jnp.float32)
    grad_v = jnp.zeros((rank, own_rows), jnp.float32)
    for moment in reversed(range(STEPS)):
        grad_u = grad_u + jnp.dot(latent_of[moment].T, scaled_of[moment], preferred_element_type=jnp.float32)
        grad_v = grad_v + jnp.dot(coeffs_of[moment].T, signed_of[moment], preferred_element_type=jnp.float32)
    return (final_state, grad_u, grad_v)


def solution(mesh):
    finer = Mesh(
        mesh.devices.reshape(mesh.shape["region"], 4, 4, 2), ("region", "row_0", "row_1", "row_2")
    )
    in_specs = (
        P(None, REGION_ROW),
        P(None, REGION_ROW),
        P(None, REGION_ROW),
        P(REGION_ROW),
        P(REGION_ROW, None, None, None),
        P(REGION_ROW, None),
        P(REGION_ROW),
        P("region", ROW, None, None),
        P(None, REGION_ROW),
        P(None, REGION_ROW),
    )
    out_specs = (P(None, REGION_ROW), P(None, REGION_ROW), P(None, REGION_ROW))
    return jax.shard_map(local, mesh=finer, in_specs=in_specs, out_specs=out_specs, check_vma=False)
```

profile of v0, /device:TPU:9, one launch (start us, length us, event | category | flops | bytes accessed | tf_op | source)
XLA Modules:
  0.0 376.3 jit_solution(1513962569909645488)
XLA Ops:
  5.9 8.2 %all-to-all-start = ((f32[8,32,128]{2,1,0:T(8,128)}), f32[8,32,128]{2,1,0:T(8,128)S(1)}, u32[]{:S(2)}, u32[]{:S(2)}) async-start(f32[8,32,128]{2,1,0:T(8,128)} %select_maximum_fusion.9), calls=%async_computation | async-start | bytes 262144 | tf_op jit(solution)/shard_map/all_to_all | solution.py:18
  16.4 1.7 fusion.78
  18.2 3.7 all-to-all-done
  23.4 6.8 %all-to-all-start.1 = ((bf16[16,176,128]{2,1,0:T(8,128)(2,1)}), bf16[16,176,128]{2,1,0:T(8,128)(2,1)}, u32[]{:S(2)}, u32[]{:S(2)}) async-start(bf16[16,176,128]{2,1,0:T(8,128)(2,1)} %broadcast_in_dim.42), calls=%async_computation.1 | async-start | bytes 1441792 | tf_op jit(solution)/shard_map/all_to_all | solution.py:28
  31.9 3.6 convolution_convert_fusion.3
  37.3 2.3 all-to-all-done.1
  39.6 9.8 %all-to-all-start.2 = ((bf16[32,176,128]{2,1,0:T(8,128)(2,1)}), bf16[32,176,128]{2,1,0:T(8,128)(2,1)}, u32[]{:S(2)}, u32[]{:S(2)}) async-start(bf16[32,176,128]{2,1,0:T(8,128)(2,1)} %pad_maximum_fusion), calls=%async_computation.2 | async-start | bytes 2883584 | tf_op jit(solution)/shard_map/all_to_all | solution.py:22
  49.9 2.2 copy.320
  52.1 17.7 %all-to-all-done.2 = bf16[32,176,128]{2,1,0:T(8,128)(2,1)} async-done(((bf16[32,176,128]{2,1,0:T(8,128)(2,1)}), bf16[32,176,128]{2,1,0:T(8,128)(2,1)}, u32[]{:S(2)}, u32[]{:S(2)}) %all-to-all-start.2) | async-done | bytes 1441824 | tf_op jit(solution)/shard_map/all_to_all | solution.py:22
  74.9 1.7 fusion.8
  76.7 1.8 convolution_bitcast_fusion.3
  84.9 1.7 select_maximum_fusion.6
  86.6 3.4 all-to-all-start.3
  90.0 9.5 %all-to-all-done.3 = f32[8,32,128]{2,1,0:T(8,128)S(1)} async-done(((f32[8,32,128]{2,1,0:T(8,128)}), f32[8,32,128]{2,1,0:T(8,128)S(1)}, u32[]{:S(2)}, u32[]{:S(2)}) %all-to-all-start.3) | async-done | bytes 131104 | tf_op jit(solution)/shard_map/all_to_all | solution.py:18
  100.3 14.9 %all_to_all.70 = bf16[16,176,128]{2,1,0:T(8,128)(2,1)S(1)} all-to-all(bf16[16,176,128]{2,1,0:T(8,128)(2,1)S(1)} %broadcast_in_dim.83), channel_id=1, replica_groups=mesh['region'=8,'row_0'=4,'row_1'=4,'row_2'=2] {'row_0','row_1'}, dimensions={0} | all-to-all | bytes 1441792 | tf_op jit(solution)/shard_map/all_to_all | solution.py:28
  115.2 2.0 collective-permute-start.1
  119.9 1.8 convolution_bitcast_fusion.2
  130.2 3.4 all-to-all-start.5
  134.2 7.7 %all-to-all-done.5 = f32[8,32,128]{2,1,0:T(8,128)S(1)} async-done(((f32[8,32,128]{2,1,0:T(8,128)}), f32[8,32,128]{2,1,0:T(8,128)S(1)}, u32[]{:S(2)}, u32[]{:S(2)}) %all-to-all-start.5) | async-done | bytes 131104 | tf_op jit(solution)/shard_map/all_to_all | solution.py:18
  146.7 15.5 %all_to_all.71 = bf16[16,176,128]{2,1,0:T(8,128)(2,1)} all-to-all(bf16[16,176,128]{2,1,0:T(8,128)(2,1)S(1)} %broadcast_in_dim.85), channel_id=1, replica_groups=mesh['region'=8,'row_0'=4,'row_1'=4,'row_2'=2] {'row_0','row_1'}, dimensions={0} | all-to-all | bytes 1441792 | tf_op jit(solution)/shard_map/all_to_all | solution.py:28
  162.2 2.5 collective-permute-start.2
  169.0 1.7 scatter_fusion
  174.7 1.8 convolution_bitcast_fusion.1
  179.3 1.7 fusion.104
  181.9 2.2 convolution_convert_fusion.2
  185.9 6.1 %all-to-all-start.7 = ((bf16[32,176,128]{2,1,0:T(8,128)(2,1)}), bf16[32,176,128]{2,1,0:T(8,128)(2,1)}, u32[]{:S(2)}, u32[]{:S(2)}) async-start(bf16[32,176,128]{2,1,0:T(8,128)(2,1)} %pad_maximum_fusion.1), calls=%async_computation.7 | async-start | bytes 2883584 | tf_op jit(solution)/shard_map/all_to_all | solution.py:22
  193.9 18.5 %all-to-all-done.7 = bf16[32,176,128]{2,1,0:T(8,128)(2,1)} async-done(((bf16[32,176,128]{2,1,0:T(8,128)(2,1)}), bf16[32,176,128]{2,1,0:T(8,128)(2,1)}, u32[]{:S(2)}, u32[]{:S(2)}) %all-to-all-start.7) | async-done | bytes 1441824 | tf_op jit(solution)/shard_map/all_to_all | solution.py:22
  219.8 1.7 select_maximum_fusion.2
  221.5 3.6 all-to-all-start.8
  226.4 8.1 %all-to-all-done.8 = f32[8,32,128]{2,1,0:T(8,128)S(1)} async-done(((f32[8,32,128]{2,1,0:T(8,128)}), f32[8,32,128]{2,1,0:T(8,128)S(1)}, u32[]{:S(2)}, u32[]{:S(2)}) %all-to-all-start.8) | async-done | bytes 131104 | tf_op jit(solution)/shard_map/all_to_all | solution.py:18
  239.5 3.1 scatter_fusion.1
  255.2 4.3 %all-to-all-start.9 = ((bf16[16,176,128]{2,1,0:T(8,128)(2,1)}), bf16[16,176,128]{2,1,0:T(8,128)(2,1)}, u32[]{:S(2)}, u32[]{:S(2)}) async-start(bf16[16,176,128]{2,1,0:T(8,128)(2,1)} %broadcast_in_dim.89), calls=%async_computation.9 | async-start | bytes 1441792 | tf_op jit(solution)/shard_map/all_to_all | solution.py:28
  260.2 2.2 convolution_convert_fusion.1
  264.2 5.8 %all-to-all-done.9 = bf16[16,176,128]{2,1,0:T(8,128)(2,1)} async-done(((bf16[16,176,128]{2,1,0:T(8,128)(2,1)}), bf16[16,176,128]{2,1,0:T(8,128)(2,1)}, u32[]{:S(2)}, u32[]{:S(2)}) %all-to-all-start.9) | async-done | bytes 720928 | tf_op jit(solution)/shard_map/all_to_all | solution.py:28
  270.0 8.5 %all-to-all-start.10 = ((bf16[32,176,128]{2,1,0:T(8,128)(2,1)}), bf16[32,176,128]{2,1,0:T(8,128)(2,1)}, u32[]{:S(2)}, u32[]{:S(2)}) async-start(bf16[32,176,128]{2,1,0:T(8,128)(2,1)} %pad_maximum_fusion.2), calls=%async_computation.10 | async-start | bytes 2883584 | tf_op jit(solution)/shard_map/all_to_all | solution.py:22
  279.9 2.2 copy.370
  282.0 16.9 %all-to-all-done.10 = bf16[32,176,128]{2,1,0:T(8,128)(2,1)} async-done(((bf16[32,176,128]{2,1,0:T(8,128)(2,1)}), bf16[32,176,128]{2,1,0:T(8,128)(2,1)}, u32[]{:S(2)}, u32[]{:S(2)}) %all-to-all-start.10) | async-done | bytes 1441824 | tf_op jit(solution)/shard_map/all_to_all | solution.py:22
  301.2 2.2 copy.371
  305.8 4.0 %all-to-all-start.11 = ((f32[8,32,128]{2,1,0:T(8,128)}), f32[8,32,128]{2,1,0:T(8,128)}, u32[]{:S(2)}, u32[]{:S(2)}) async-start(f32[8,32,128]{2,1,0:T(8,128)} %select_maximum_fusion.1), calls=%async_computation.11 | async-start | bytes 262144 | tf_op jit(solution)/shard_map/all_to_all | solution.py:18
  312.5 6.9 %all-to-all-done.11 = f32[8,32,128]{2,1,0:T(8,128)} async-done(((f32[8,32,128]{2,1,0:T(8,128)}), f32[8,32,128]{2,1,0:T(8,128)}, u32[]{:S(2)}, u32[]{:S(2)}) %all-to-all-start.11) | async-done | bytes 131104 | tf_op jit(solution)/shard_map/all_to_all | solution.py:18
  324.7 1.7 scatter_fusion.2
  329.1 2.2 convolution_convert_fusion
  333.1 6.2 %all-to-all-start.12 = ((bf16[32,176,128]{2,1,0:T(8,128)(2,1)}), bf16[32,176,128]{2,1,0:T(8,128)(2,1)}, u32[]{:S(2)}, u32[]{:S(2)}) async-start(bf16[32,176,128]{2,1,0:T(8,128)(2,1)} %pad_maximum_fusion.3), calls=%async_computation.12 | async-start | bytes 2883584 | tf_op jit(solution)/shard_map/all_to_all | solution.py:22
  340.6 1.9 fusion.17
  344.5 15.3 %all-to-all-done.12 = bf16[32,176,128]{2,1,0:T(8,128)(2,1)} async-done(((bf16[32,176,128]{2,1,0:T(8,128)(2,1)}), bf16[32,176,128]{2,1,0:T(8,128)(2,1)}, u32[]{:S(2)}, u32[]{:S(2)}) %all-to-all-start.12) | async-done | bytes 1441824 | tf_op jit(solution)/shard_map/all_to_all | solution.py:22
  362.5 3.4 all-to-all-start.13
  366.7 1.6 convolution_add_fusion.3
  368.4 7.0 %all-to-all-done.13 = f32[8,32,128]{2,1,0:T(8,128)S(1)} async-done(((f32[8,32,128]{2,1,0:T(8,128)}), f32[8,32,128]{2,1,0:T(8,128)S(1)}, u32[]{:S(2)}, u32[]{:S(2)}) %all-to-all-start.13) | async-done | bytes 131104 | tf_op jit(solution)/shard_map/all_to_all | solution.py:18
  (345 shorter events, 111.7 us)
Async XLA Ops:
  0.6 15.7 %copy-start = (bf16[4,24,128,128]{3,2,1,0:T(8,128)(2,1)S(1)}, bf16[4,24,128,128]{3,2,1,0:T(8,128)(2,1)}, u32[]{:S(2)}) copy-start(bf16[4,24,128,128]{3,2,1,0:T(8,128)(2,1)} %param.16) | copy-start | bytes 9437188
  0.6 15.6 %copy-start.1 = (bf16[32,512]{1,0:T(8,128)(2,1)S(1)}, bf16[32,512]{1,0:T(8,128)(2,1)}, u32[]{:S(2)}) copy-start(bf16[32,512]{1,0:T(8,128)(2,1)} %param.20) | copy-start | bytes 98308
  1.6 14.8 %copy-start.44 = (pred[128]{0:T(512)(128)(4,1)}, pred[128]{0:T(512)(128)(4,1)S(1)}, u32[]{:S(2)}) copy-start(pred[128]{0:T(512)(128)(4,1)S(1)} %compare_and_fusion.5) | copy-start | bytes 388
  2.3 176.9 %copy-start.24 = (f32[512]{0:T(512)}, f32[512]{0:T(512)S(1)}, u32[]{:S(2)}) copy-start(f32[512]{0:T(512)S(1)} %add_convert_fusion) | copy-start | bytes 6148
  2.3 14.0 %copy-start.43 = (s32[1024]{0:T(1024)}, s32[1024]{0:T(1024)S(1)}, u32[]{:S(2)}) copy-start(s32[1024]{0:T(1024)S(1)} %pad_clamp_fusion) | copy-start | bytes 12292
  5.9 16.0 %all-to-all-start = ((f32[8,32,128]{2,1,0:T(8,128)}), f32[8,32,128]{2,1,0:T(8,128)S(1)}, u32[]{:S(2)}, u32[]{:S(2)}) async-start(f32[8,32,128]{2,1,0:T(8,128)} %select_maximum_fusion.9), calls=%async_computation | async-start | bytes 262144 | tf_op jit(solution)/shard_map/all_to_all | solution.py:18
  23.4 16.1 %all-to-all-start.1 = ((bf16[16,176,128]{2,1,0:T(8,128)(2,1)}), bf16[16,176,128]{2,1,0:T(8,128)(2,1)}, u32[]{:S(2)}, u32[]{:S(2)}) async-start(bf16[16,176,128]{2,1,0:T(8,128)(2,1)} %broadcast_in_dim.42), calls=%async_computation.1 | async-start | bytes 1441792 | tf_op jit(solution)/shard_map/all_to_all | solution.py:28
  30.3 151.6 %copy-start.27 = (s32[32,5]{0,1:T(8,128)}, s32[32,5]{0,1:T(8,128)S(1)}, u32[]{:S(2)}) copy-start(s32[32,5]{0,1:T(8,128)S(1)} %multiply_add_fusion) | copy-start | bytes 1924
  31.0 18.3 %copy-start.38 = (s32[96]{0:T(128)}, s32[96]{0:T(128)S(1)}, u32[]{:S(2)}) copy-start(s32[96]{0:T(128)S(1)} %reshape.469) | copy-start | bytes 1156
  31.8 43.1 %copy-start.47 = (pred[96]{0:T(512)(128)(4,1)}, pred[96]{0:T(512)(128)(4,1)S(1)}, u32[]{:S(2)}) copy-start(pred[96]{0:T(512)(128)(4,1)S(1)} %lt.57) | copy-start | bytes 292
  39.6 30.2 %all-to-all-start.2 = ((bf16[32,176,128]{2,1,0:T(8,128)(2,1)}), bf16[32,176,128]{2,1,0:T(8,128)(2,1)}, u32[]{:S(2)}, u32[]{:S(2)}) async-start(bf16[32,176,128]{2,1,0:T(8,128)(2,1)} %pad_maximum_fusion), calls=%async_computation.2 | async-start | bytes 2883584 | tf_op jit(solution)/shard_map/all_to_all | solution.py:22
  49.4 25.5 %copy-start.54 = (pred[96,2,11]{0,2,1:T(8,128)(4,1)}, pred[96,2,11]{0,2,1:T(8,128)(4,1)S(1)}, u32[]{:S(2)}) copy-start(pred[96,2,11]{0,2,1:T(8,128)(4,1)S(1)} %iota_compare_fusion.2) | copy-start | bytes 6340
  49.5 24.1 %collective-permute-start = (bf16[16,176,128]{2,1,0:T(8,128)(2,1)}, bf16[16,176,128]{2,1,0:T(8,128)(2,1)}, u32[]{:S(2)}, u32[]{:S(2)}) collective-permute-start(bf16[16,176,128]{2,1,0:T(8,128)(2,1)} %all-to-all-done.1), channel_id=1, source_target_pairs={{0,1},{1,0},{2,3},{3,2},{4,5},{5,4},{6,7},{7,6},{8,9},{9,8},{10,11... | collective-permute-start | bytes 2162696 | tf_op jit(solution)/shard_map/ppermute | solution.py:29
  49.9 25.0 %copy-start.58 = (pred[96,2,16]{0,2,1:T(8,128)(4,1)}, pred[96,2,16]{0,2,1:T(8,128)(4,1)S(1)}, u32[]{:S(2)}) copy-start(pred[96,2,16]{0,2,1:T(8,128)(4,1)S(1)} %broadcast_and_fusion) | copy-start | bytes 9220
  82.8 17.4 %copy-start.5 = (bf16[32,512]{1,0:T(8,128)(2,1)}, bf16[32,512]{1,0:T(8,128)(2,1)S(1)}, u32[]{:S(2)}) copy-start(bf16[32,512]{1,0:T(8,128)(2,1)S(1)} %get-tuple-element.29) | copy-start | bytes 98308
  86.6 12.9 %all-to-all-start.3 = ((f32[8,32,128]{2,1,0:T(8,128)}), f32[8,32,128]{2,1,0:T(8,128)S(1)}, u32[]{:S(2)}, u32[]{:S(2)}) async-start(f32[8,32,128]{2,1,0:T(8,128)} %select_maximum_fusion.6), calls=%async_computation.3 | async-start | bytes 262144 | tf_op jit(solution)/shard_map/all_to_all | solution.py:18
  115.2 3.9 %collective-permute-start.1 = (bf16[16,176,128]{2,1,0:T(8,128)(2,1)S(1)}, bf16[16,176,128]{2,1,0:T(8,128)(2,1)S(1)}, u32[]{:S(2)}, u32[]{:S(2)}) collective-permute-start(bf16[16,176,128]{2,1,0:T(8,128)(2,1)S(1)} %all_to_all.70), channel_id=1, source_target_pairs={{0,1},{1,0},{2,3},{3,2},{4,5},{5,4},{6,7},{7,6},{8,9},{9,8},{10,11... | collective-permute-start | bytes 2162696 | tf_op jit(solution)/shard_map/ppermute | solution.py:29
  124.7 37.5 %copy-start.7 = (bf16[32,512]{1,0:T(8,128)(2,1)}, bf16[32,512]{1,0:T(8,128)(2,1)S(1)}, u32[]{:S(2)}) copy-start(bf16[32,512]{1,0:T(8,128)(2,1)S(1)} %get-tuple-element.31) | copy-start | bytes 98308
  130.2 11.7 %all-to-all-start.5 = ((f32[8,32,128]{2,1,0:T(8,128)}), f32[8,32,128]{2,1,0:T(8,128)S(1)}, u32[]{:S(2)}, u32[]{:S(2)}) async-start(f32[8,32,128]{2,1,0:T(8,128)} %select_maximum_fusion.5), calls=%async_computation.5 | async-start | bytes 262144 | tf_op jit(solution)/shard_map/all_to_all | solution.py:18
  144.1 22.3 %copy-start.4 = (bf16[32,512]{1,0:T(8,128)(2,1)S(1)}, bf16[32,512]{1,0:T(8,128)(2,1)}, u32[]{:S(2)}) copy-start(bf16[32,512]{1,0:T(8,128)(2,1)} %param.21) | copy-start | bytes 98308
  144.8 19.9 %copy-start.42 = (s32[1,1,8,16]{3,2,1,0:T(8,128)S(1)}, s32[1,1,8,16]{3,2,1,0:T(8,128)}, u32[]{:S(2)}) copy-start(s32[1,1,8,16]{3,2,1,0:T(8,128)} %param.19) | copy-start | bytes 1540
  144.8 20.0 %copy-start.21 = (f32[176,128]{1,0:T(8,128)S(1)}, f32[176,128]{1,0:T(8,128)}, u32[]{:S(2)}) copy-start(f32[176,128]{1,0:T(8,128)} %copy-done.20) | copy-start | bytes 270340
  162.2 10.6 %collective-permute-start.2 = (bf16[16,176,128]{2,1,0:T(8,128)(2,1)}, bf16[16,176,128]{2,1,0:T(8,128)(2,1)}, u32[]{:S(2)}, u32[]{:S(2)}) collective-permute-start(bf16[16,176,128]{2,1,0:T(8,128)(2,1)} %all_to_all.71), channel_id=1, source_target_pairs={{0,1},{1,0},{2,3},{3,2},{4,5},{5,4},{6,7},{7,6},{8,9},{9,8},{10,11... | collective-permute-start | bytes 2162696 | tf_op jit(solution)/shard_map/ppermute | solution.py:29
  164.8 7.9 %copy-start.52 = (s32[128]{0:T(128)}, s32[128]{0:T(128)S(1)}, u32[]{:S(2)}) copy-start(s32[128]{0:T(128)S(1)} %fusion.98) | copy-start | bytes 1540
  165.5 8.5 %copy-start.35 = (bf16[32,32]{0,1:T(8,128)(2,1)}, bf16[32,32]{0,1:T(8,128)(2,1)S(1)}, u32[]{:S(2)}) copy-start(bf16[32,32]{0,1:T(8,128)(2,1)S(1)} %copy.421) | copy-start | bytes 6148
  185.9 7.1 %copy-start.46 = (pred[128]{0:T(512)(128)(4,1)S(1)}, pred[128]{0:T(512)(128)(4,1)}, u32[]{:S(2)}) copy-start(pred[128]{0:T(512)(128)(4,1)} %copy-done.44) | copy-start | bytes 388
  185.9 26.5 %all-to-all-start.7 = ((bf16[32,176,128]{2,1,0:T(8,128)(2,1)}), bf16[32,176,128]{2,1,0:T(8,128)(2,1)}, u32[]{:S(2)}, u32[]{:S(2)}) async-start(bf16[32,176,128]{2,1,0:T(8,128)(2,1)} %pad_maximum_fusion.1), calls=%async_computation.7 | async-start | bytes 2883584 | tf_op jit(solution)/shard_map/all_to_all | solution.py:22
  214.6 24.9 %copy-start.53 = (s32[128]{0:T(128)S(1)}, s32[128]{0:T(128)}, u32[]{:S(2)}) copy-start(s32[128]{0:T(128)} %copy-done.52) | copy-start | bytes 1540
  219.1 24.6 %copy-start.25 = (f32[512]{0:T(512)S(1)}, f32[512]{0:T(512)}, u32[]{:S(2)}) copy-start(f32[512]{0:T(512)} %copy-done.24) | copy-start | bytes 6148
  221.5 12.9 %all-to-all-start.8 = ((f32[8,32,128]{2,1,0:T(8,128)}), f32[8,32,128]{2,1,0:T(8,128)S(1)}, u32[]{:S(2)}, u32[]{:S(2)}) async-start(f32[8,32,128]{2,1,0:T(8,128)} %select_maximum_fusion.2), calls=%async_computation.8 | async-start | bytes 262144 | tf_op jit(solution)/shard_map/all_to_all | solution.py:18
  243.7 16.4 %copy-start.10 = (f32[32,512]{1,0:T(8,128)}, f32[32,512]{1,0:T(8,128)S(1)}, u32[]{:S(2)}) copy-start(f32[32,512]{1,0:T(8,128)S(1)} %copy.378) | copy-start | bytes 196612
  244.6 15.5 %copy-start.18 = (bf16[32,512]{1,0:T(8,128)(2,1)}, bf16[32,512]{1,0:T(8,128)(2,1)S(1)}, u32[]{:S(2)}) copy-start(bf16[32,512]{1,0:T(8,128)(2,1)S(1)} %fusion.103) | copy-start | bytes 98308
  251.6 7.9 %copy-start.26 = (bf16[32,4,128]{2,1,0:T(4,128)(2,1)S(1)}, bf16[32,4,128]{2,1,0:T(4,128)(2,1)}, u32[]{:S(2)}) copy-start(bf16[32,4,128]{2,1,0:T(4,128)(2,1)} %reshape.512) | copy-start | bytes 98308
  255.2 14.8 %all-to-all-start.9 = ((bf16[16,176,128]{2,1,0:T(8,128)(2,1)}), bf16[16,176,128]{2,1,0:T(8,128)(2,1)}, u32[]{:S(2)}, u32[]{:S(2)}) async-start(bf16[16,176,128]{2,1,0:T(8,128)(2,1)} %broadcast_in_dim.89), calls=%async_computation.9 | async-start | bytes 1441792 | tf_op jit(solution)/shard_map/all_to_all | solution.py:28
  264.2 14.8 %copy-start.36 = (bf16[32,32]{0,1:T(8,128)(2,1)S(1)}, bf16[32,32]{0,1:T(8,128)(2,1)}, u32[]{:S(2)}) copy-start(bf16[32,32]{0,1:T(8,128)(2,1)} %copy-done.35) | copy-start | bytes 6148
  264.2 14.9 %copy-start.8 = (bf16[32,512]{1,0:T(8,128)(2,1)S(1)}, bf16[32,512]{1,0:T(8,128)(2,1)}, u32[]{:S(2)}) copy-start(bf16[32,512]{1,0:T(8,128)(2,1)} %copy-done.7) | copy-start | bytes 98308
  270.0 28.9 %all-to-all-start.10 = ((bf16[32,176,128]{2,1,0:T(8,128)(2,1)}), bf16[32,176,128]{2,1,0:T(8,128)(2,1)}, u32[]{:S(2)}, u32[]{:S(2)}) async-start(bf16[32,176,128]{2,1,0:T(8,128)(2,1)} %pad_maximum_fusion.2), calls=%async_computation.10 | async-start | bytes 2883584 | tf_op jit(solution)/shard_map/all_to_all | solution.py:22
  278.5 22.6 %collective-permute-start.3 = (bf16[16,176,128]{2,1,0:T(8,128)(2,1)}, bf16[16,176,128]{2,1,0:T(8,128)(2,1)}, u32[]{:S(2)}, u32[]{:S(2)}) collective-permute-start(bf16[16,176,128]{2,1,0:T(8,128)(2,1)} %all-to-all-done.9), channel_id=1, source_target_pairs={{0,1},{1,0},{2,3},{3,2},{4,5},{5,4},{6,7},{7,6},{8,9},{9,8},{10,11... | collective-permute-start | bytes 2162696 | tf_op jit(solution)/shard_map/ppermute | solution.py:29
  305.8 13.6 %all-to-all-start.11 = ((f32[8,32,128]{2,1,0:T(8,128)}), f32[8,32,128]{2,1,0:T(8,128)}, u32[]{:S(2)}, u32[]{:S(2)}) async-start(f32[8,32,128]{2,1,0:T(8,128)} %select_maximum_fusion.1), calls=%async_computation.11 | async-start | bytes 262144 | tf_op jit(solution)/shard_map/all_to_all | solution.py:18
  333.1 6.6 %copy-start.34 = (bf16[32,32]{1,0:T(8,128)(2,1)S(1)}, bf16[32,32]{1,0:T(8,128)(2,1)}, u32[]{:S(2)}) copy-start(bf16[32,32]{1,0:T(8,128)(2,1)} %copy-done.33) | copy-start | bytes 6148
  333.1 7.4 %copy-start.57 = (pred[96,2,11]{0,2,1:T(8,128)(4,1)S(1)}, pred[96,2,11]{0,2,1:T(8,128)(4,1)}, u32[]{:S(2)}) copy-start(pred[96,2,11]{0,2,1:T(8,128)(4,1)} %copy-done.54) | copy-start | bytes 6340
  333.1 7.4 %copy-start.61 = (pred[96,2,16]{0,2,1:T(8,128)(4,1)S(1)}, pred[96,2,16]{0,2,1:T(8,128)(4,1)}, u32[]{:S(2)}) copy-start(pred[96,2,16]{0,2,1:T(8,128)(4,1)} %copy-done.58) | copy-start | bytes 9220
  333.1 26.6 %all-to-all-start.12 = ((bf16[32,176,128]{2,1,0:T(8,128)(2,1)}), bf16[32,176,128]{2,1,0:T(8,128)(2,1)}, u32[]{:S(2)}, u32[]{:S(2)}) async-start(bf16[32,176,128]{2,1,0:T(8,128)(2,1)} %pad_maximum_fusion.3), calls=%async_computation.12 | async-start | bytes 2883584 | tf_op jit(solution)/shard_map/all_to_all | solution.py:22
  343.7 22.2 %copy-start.6 = (bf16[32,512]{1,0:T(8,128)(2,1)S(1)}, bf16[32,512]{1,0:T(8,128)(2,1)}, u32[]{:S(2)}) copy-start(bf16[32,512]{1,0:T(8,128)(2,1)} %copy-done.5) | copy-start | bytes 98308
  343.7 22.2 %copy-start.22 = (f32[32,512]{1,0:T(8,128)S(1)}, f32[32,512]{1,0:T(8,128)}, u32[]{:S(2)}) copy-start(f32[32,512]{1,0:T(8,128)} %convolution_add_fusion.2) | copy-start | bytes 196612
  343.7 23.0 %copy-start.32 = (bf16[32,32]{1,0:T(8,128)(2,1)S(1)}, bf16[32,32]{1,0:T(8,128)(2,1)}, u32[]{:S(2)}) copy-start(bf16[32,32]{1,0:T(8,128)(2,1)} %copy-done.31) | copy-start | bytes 6148
  344.5 31.0 %copy-start.13 = (bf16[32,512]{1,0:T(8,128)(2,1)S(1)}, bf16[32,512]{1,0:T(8,128)(2,1)}, u32[]{:S(2)}) copy-start(bf16[32,512]{1,0:T(8,128)(2,1)} %copy-done.12) | copy-start | bytes 98308
  362.5 12.9 %all-to-all-start.13 = ((f32[8,32,128]{2,1,0:T(8,128)}), f32[8,32,128]{2,1,0:T(8,128)S(1)}, u32[]{:S(2)}, u32[]{:S(2)}) async-start(f32[8,32,128]{2,1,0:T(8,128)} %select_maximum_fusion), calls=%async_computation.13 | async-start | bytes 262144 | tf_op jit(solution)/shard_map/all_to_all | solution.py:18
  (30 other events, 80.3 us)
where the time goes:
time: 381 us; the launch traced here: 376 us
  waiting for transfers between devices  121 us (32%)
  starting transfers between devices  73.1 us (19%)
  local copies, waits for them, and re-layouts  60.1 us (16%)
  other arithmetic  45.8 us (12%)
  matrix products  44.1 us (12%)
  blocking collectives  30.4 us (8%)
    all_to_all x4, waiting for transfers between devices, from_each_lane(): return lax.all_to_all(slots, ROW, 0, 0, tiled=True)  68.4 us
    all_to_all x6, waiting for transfers between devices, from_each_region(): return lax.all_to_all(padded, 'region', 0, 0, tiled=True)[..., :width]  42.8 us
    all_to_all x4, starting transfers between devices, from_each_lane(): return lax.all_to_all(slots, ROW, 0, 0, tiled=True)  30.6 us
    all_to_all x2, blocking collectives, from_every_lane(): mine = lax.all_to_all(copies, chips, 0, 0, tiled=True)  30.4 us
    all_to_all x6, starting transfers between devices, from_each_region(): return lax.all_to_all(padded, 'region', 0, 0, tiled=True)[..., :width]  25.9 us
    all_to_all x2, starting transfers between devices, from_every_lane(): mine = lax.all_to_all(copies, chips, 0, 0, tiled=True)  11.1 us
    another operation x8, local copies, waits for them, and re-layouts, from_every_lane(): return jnp.stack([mine, sibling])  10.8 us
    dot_general x4, matrix products, adjoint_start(): jnp.einsum('lts,bsk->ltbk', picks, spread.reshape(batch_rows, -1, 128), p...  10.2 us
  transfers between devices with their start and end apart: 16, of which 13 were waited for; matrix products, arithmetic and copies ran while one was open for 13% of the time, Pallas kernels for 0%

commit v1 on v0

--- a/solution.py
+++ b/solution.py
@@ -85,17 +85,19 @@
         & (jnp.arange(payload_rows // half_rows, dtype=jnp.int32)[None, None, None, None, :] == block_of[:, :, None, None, None])
         & live_tiles[:, None, None, None, None]
     ).astype(jnp.bfloat16)
+    border_to_row = (chosen[:, None] == jnp.arange(own_rows, dtype=jnp.int32)[None, :]).astype(jnp.float32)
+    row_to_border = border_to_row.T.astype(jnp.bfloat16).reshape(own_rows, groups, sent)
     polarity = (2 * excitatory - 1).astype(jnp.float32)
     drive_f = drive.astype(jnp.float32)
 
     def forward_start(state):
         rates = jnp.tanh(state)
         signed = (polarity * rates).astype(jnp.bfloat16)
-        outgoing = jnp.take(signed, chosen, axis=1).reshape(batch_rows, groups, sent)
+        outgoing = jnp.einsum("bn,ndk->dbk", signed, row_to_border, preferred_element_type=jnp.float32)
         part_latent = jnp.dot(signed, v_factor.T, preferred_element_type=jnp.float32)
         chunks = jnp.concatenate(
             [
-                jnp.moveaxis(outgoing, 1, 0).astype(jnp.float32),
+                outgoing,
                 jnp.broadcast_to(part_latent, (groups, batch_rows, rank)),
             ],
             axis=2,
@@ -159,7 +161,7 @@
     def adjoint_end(adjoint, own_part, back, rates):
         returned = jnp.moveaxis(back[:, :, :sent], 0, 1).reshape(batch_rows, -1)
         coeffs_b = jnp.sum(back[:, :, sent:], axis=0).astype(jnp.bfloat16)
-        through = own_part.at[:, chosen].add(returned)
+        through = own_part + jnp.dot(returned, border_to_row, precision=lax.Precision.HIGHEST)
         total_signed = through + jnp.dot(coeffs_b, v_factor, preferred_element_type=jnp.float32)
         adjoint = (1.0 - leak) * adjoint + (1.0 - rates * rates) * polarity * total_signed
         return adjoint, coeffs_b

time: 381 us -> 355 us (0.932)
  local copies, waits for them, and re-layouts: 60.1 us -> 42 us
  other arithmetic: 45.8 us -> 32.4 us
  matrix products: 44.1 us -> 49.3 us
    dot_general x0 -> x7, matrix products: none -> 6.94 us  [the longest x3 4.02 us: adjoint_end(): jnp.dot(returned, border_to_row, precision=lax.Precision.HIGHEST)]
    scatter-add x3 -> x0, other arithmetic: 6.46 us -> none  [adjoint_end(): through = own_part.at[:, chosen].add(returned)]
    gather x4 -> x0, local copies, waits for them, and re-layouts: 3.83 us -> none  [forward_start(): jnp.take(signed, chosen, axis=1).reshape(batch_rows, groups, sent)]
where the time goes in v1:
time: 355 us; the launch traced here: 351 us
  waiting for transfers between devices  122 us (34%)
  starting transfers between devices  73 us (21%)
  matrix products  49.3 us (14%)
  local copies, waits for them, and re-layouts  42 us (12%)
  other arithmetic  32.4 us (9%)
  blocking collectives  30.5 us (9%)
    all_to_all x4, waiting for transfers between devices, from_each_lane(): return lax.all_to_all(slots, ROW, 0, 0, tiled=True)  69.2 us
    all_to_all x6, waiting for transfers between devices, from_each_region(): return lax.all_to_all(padded, 'region', 0, 0, tiled=True)[..., :width]  41.8 us
    all_to_all x4, starting transfers between devices, from_each_lane(): return lax.all_to_all(slots, ROW, 0, 0, tiled=True)  30.6 us
    all_to_all x2, blocking collectives, from_every_lane(): mine = lax.all_to_all(copies, chips, 0, 0, tiled=True)  30.5 us
    all_to_all x6, starting transfers between devices, from_each_region(): return lax.all_to_all(padded, 'region', 0, 0, tiled=True)[..., :width]  25.8 us
    all_to_all x2, starting transfers between devices, from_every_lane(): mine = lax.all_to_all(copies, chips, 0, 0, tiled=True)  11.2 us
    another operation x8, local copies, waits for them, and re-layouts, from_every_lane(): return jnp.stack([mine, sibling])  10.8 us
    dot_general x4, matrix products, adjoint_start(): jnp.einsum('lts,bsk->ltbk', picks, spread.reshape(batch_rows, -1, 128), p...  10.2 us
  transfers between devices with their start and end apart: 16, of which 13 were waited for; matrix products, arithmetic and copies ran while one was open for 13% of the time, Pallas kernels for 0%

profile of v1, /device:TPU:9, one launch (start us, length us, event | category | flops | bytes accessed | tf_op | source)
XLA Modules:
  0.0 351.1 jit_solution(17481849159222249309)
XLA Ops:
  5.2 8.2 %all-to-all-start = ((f32[8,32,128]{2,1,0:T(8,128)}), f32[8,32,128]{2,1,0:T(8,128)S(1)}, u32[]{:S(2)}, u32[]{:S(2)}) async-start(f32[8,32,128]{2,1,0:T(8,128)} %select_maximum_fusion.9), calls=%async_computation | async-start | bytes 262144 | tf_op jit(solution)/shard_map/all_to_all | solution.py:18
  15.8 1.7 fusion.97
  17.7 3.4 all-to-all-done
  22.7 6.8 %all-to-all-start.1 = ((bf16[16,176,128]{2,1,0:T(8,128)(2,1)}), bf16[16,176,128]{2,1,0:T(8,128)(2,1)}, u32[]{:S(2)}, u32[]{:S(2)}) async-start(bf16[16,176,128]{2,1,0:T(8,128)(2,1)} %broadcast_in_dim.33), calls=%async_computation.1 | async-start | bytes 1441792 | tf_op jit(solution)/shard_map/all_to_all | solution.py:28
  29.8 3.5 %convolution_convert_fusion.3 = bf16[32,5,32,128]{3,0,2,1:T(8,128)(2,1)S(1)} fusion(f32[32,96,128]{2,0,1:T(8,128)} %bitcast.315, s32[32,5]{0,1:T(8,128)S(1)} %multiply_add_fusion, s32[96]{0:T(128)S(1)} %reshape.429, pred[96]{0:T(512)(128)(4,1)S(1)} %lt.39), kind=kOutput, calls=%fused_computation.7 | convolution fusion | flops 755660800 | bytes 2884704 | tf_op jit(solution)/shard_map/lts,bsk->ltbk/dot_general | solution.py:141
  35.1 3.7 %all-to-all-done.1 = bf16[16,176,128]{2,1,0:T(8,128)(2,1)} async-done(((bf16[16,176,128]{2,1,0:T(8,128)(2,1)}), bf16[16,176,128]{2,1,0:T(8,128)(2,1)}, u32[]{:S(2)}, u32[]{:S(2)}) %all-to-all-start.1) | async-done | bytes 720928 | tf_op jit(solution)/shard_map/all_to_all | solution.py:28
  38.8 9.8 %all-to-all-start.2 = ((bf16[32,176,128]{2,1,0:T(8,128)(2,1)}), bf16[32,176,128]{2,1,0:T(8,128)(2,1)}, u32[]{:S(2)}, u32[]{:S(2)}) async-start(bf16[32,176,128]{2,1,0:T(8,128)(2,1)} %pad_maximum_fusion), calls=%async_computation.2 | async-start | bytes 2883584 | tf_op jit(solution)/shard_map/all_to_all | solution.py:22
  49.2 2.2 copy.273
  51.4 17.7 %all-to-all-done.2 = bf16[32,176,128]{2,1,0:T(8,128)(2,1)} async-done(((bf16[32,176,128]{2,1,0:T(8,128)(2,1)}), bf16[32,176,128]{2,1,0:T(8,128)(2,1)}, u32[]{:S(2)}, u32[]{:S(2)}) %all-to-all-start.2) | async-done | bytes 1441824 | tf_op jit(solution)/shard_map/all_to_all | solution.py:22
  74.1 1.7 fusion.8
  75.9 1.8 convolution_bitcast_fusion.6
  80.5 1.6 multiply_convert_fusion.2
  84.0 1.7 select_maximum_fusion.6
  85.7 3.4 all-to-all-start.3
  89.1 9.5 %all-to-all-done.3 = f32[8,32,128]{2,1,0:T(8,128)S(1)} async-done(((f32[8,32,128]{2,1,0:T(8,128)}), f32[8,32,128]{2,1,0:T(8,128)S(1)}, u32[]{:S(2)}, u32[]{:S(2)}) %all-to-all-start.3) | async-done | bytes 131104 | tf_op jit(solution)/shard_map/all_to_all | solution.py:18
  99.9 14.9 %all_to_all.70 = bf16[16,176,128]{2,1,0:T(8,128)(2,1)S(1)} all-to-all(bf16[16,176,128]{2,1,0:T(8,128)(2,1)S(1)} %broadcast_in_dim.72), channel_id=1, replica_groups=mesh['region'=8,'row_0'=4,'row_1'=4,'row_2'=2] {'row_0','row_1'}, dimensions={0} | all-to-all | bytes 1441792 | tf_op jit(solution)/shard_map/all_to_all | solution.py:28
  114.9 2.0 collective-permute-start.1
  117.1 1.6 collective-permute-done.1
  119.6 1.8 convolution_bitcast_fusion.4
  127.8 3.5 %all-to-all-start.5 = ((f32[8,32,128]{2,1,0:T(8,128)}), f32[8,32,128]{2,1,0:T(8,128)S(1)}, u32[]{:S(2)}, u32[]{:S(2)}) async-start(f32[8,32,128]{2,1,0:T(8,128)} %select_maximum_fusion.5), calls=%async_computation.5 | async-start | bytes 262144 | tf_op jit(solution)/shard_map/all_to_all | solution.py:18
  132.0 7.6 %all-to-all-done.5 = f32[8,32,128]{2,1,0:T(8,128)S(1)} async-done(((f32[8,32,128]{2,1,0:T(8,128)}), f32[8,32,128]{2,1,0:T(8,128)S(1)}, u32[]{:S(2)}, u32[]{:S(2)}) %all-to-all-start.5) | async-done | bytes 131104 | tf_op jit(solution)/shard_map/all_to_all | solution.py:18
  142.5 15.6 %all_to_all.71 = bf16[16,176,128]{2,1,0:T(8,128)(2,1)} all-to-all(bf16[16,176,128]{2,1,0:T(8,128)(2,1)S(1)} %broadcast_in_dim.74), channel_id=1, replica_groups=mesh['region'=8,'row_0'=4,'row_1'=4,'row_2'=2] {'row_0','row_1'}, dimensions={0} | all-to-all | bytes 1441792 | tf_op jit(solution)/shard_map/all_to_all | solution.py:28
  158.1 2.4 collective-permute-start.2
  162.7 1.8 convolution_add_fusion.12
  167.8 1.8 convolution_bitcast_fusion.2
  174.0 1.7 fusion.123
  176.6 2.2 convolution_convert_fusion.2
  180.6 6.1 %all-to-all-start.7 = ((bf16[32,176,128]{2,1,0:T(8,128)(2,1)}), bf16[32,176,128]{2,1,0:T(8,128)(2,1)}, u32[]{:S(2)}, u32[]{:S(2)}) async-start(bf16[32,176,128]{2,1,0:T(8,128)(2,1)} %pad_maximum_fusion.1), calls=%async_computation.7 | async-start | bytes 2883584 | tf_op jit(solution)/shard_map/all_to_all | solution.py:22
  187.7 19.3 %all-to-all-done.7 = bf16[32,176,128]{2,1,0:T(8,128)(2,1)} async-done(((bf16[32,176,128]{2,1,0:T(8,128)(2,1)}), bf16[32,176,128]{2,1,0:T(8,128)(2,1)}, u32[]{:S(2)}, u32[]{:S(2)}) %all-to-all-start.7) | async-done | bytes 1441824 | tf_op jit(solution)/shard_map/all_to_all | solution.py:22
  213.4 3.4 all-to-all-start.8
  219.6 6.7 %all-to-all-done.8 = f32[8,32,128]{2,1,0:T(8,128)S(1)} async-done(((f32[8,32,128]{2,1,0:T(8,128)}), f32[8,32,128]{2,1,0:T(8,128)S(1)}, u32[]{:S(2)}, u32[]{:S(2)}) %all-to-all-start.8) | async-done | bytes 131104 | tf_op jit(solution)/shard_map/all_to_all | solution.py:18
  229.7 1.7 fusion.124
  235.2 4.4 %all-to-all-start.9 = ((bf16[16,176,128]{2,1,0:T(8,128)(2,1)}), bf16[16,176,128]{2,1,0:T(8,128)(2,1)}, u32[]{:S(2)}, u32[]{:S(2)}) async-start(bf16[16,176,128]{2,1,0:T(8,128)(2,1)} %broadcast_in_dim.78), calls=%async_computation.9 | async-start | bytes 1441792 | tf_op jit(solution)/shard_map/all_to_all | solution.py:28
  240.2 2.2 convolution_convert_fusion.1
  244.2 5.8 %all-to-all-done.9 = bf16[16,176,128]{2,1,0:T(8,128)(2,1)} async-done(((bf16[16,176,128]{2,1,0:T(8,128)(2,1)}), bf16[16,176,128]{2,1,0:T(8,128)(2,1)}, u32[]{:S(2)}, u32[]{:S(2)}) %all-to-all-start.9) | async-done | bytes 720928 | tf_op jit(solution)/shard_map/all_to_all | solution.py:28
  250.0 8.5 %all-to-all-start.10 = ((bf16[32,176,128]{2,1,0:T(8,128)(2,1)}), bf16[32,176,128]{2,1,0:T(8,128)(2,1)}, u32[]{:S(2)}, u32[]{:S(2)}) async-start(bf16[32,176,128]{2,1,0:T(8,128)(2,1)} %pad_maximum_fusion.2), calls=%async_computation.10 | async-start | bytes 2883584 | tf_op jit(solution)/shard_map/all_to_all | solution.py:22
  259.9 2.2 copy.318
  262.0 16.9 %all-to-all-done.10 = bf16[32,176,128]{2,1,0:T(8,128)(2,1)} async-done(((bf16[32,176,128]{2,1,0:T(8,128)(2,1)}), bf16[32,176,128]{2,1,0:T(8,128)(2,1)}, u32[]{:S(2)}, u32[]{:S(2)}) %all-to-all-start.10) | async-done | bytes 1441824 | tf_op jit(solution)/shard_map/all_to_all | solution.py:22
  281.2 2.2 copy.319
  284.5 4.0 %all-to-all-start.11 = ((f32[8,32,128]{2,1,0:T(8,128)}), f32[8,32,128]{2,1,0:T(8,128)}, u32[]{:S(2)}, u32[]{:S(2)}) async-start(f32[8,32,128]{2,1,0:T(8,128)} %select_maximum_fusion.1), calls=%async_computation.11 | async-start | bytes 262144 | tf_op jit(solution)/shard_map/all_to_all | solution.py:18
  291.3 6.8 %all-to-all-done.11 = f32[8,32,128]{2,1,0:T(8,128)} async-done(((f32[8,32,128]{2,1,0:T(8,128)}), f32[8,32,128]{2,1,0:T(8,128)}, u32[]{:S(2)}, u32[]{:S(2)}) %all-to-all-start.11) | async-done | bytes 131104 | tf_op jit(solution)/shard_map/all_to_all | solution.py:18
  303.9 2.2 convolution_convert_fusion
  307.9 6.2 %all-to-all-start.12 = ((bf16[32,176,128]{2,1,0:T(8,128)(2,1)}), bf16[32,176,128]{2,1,0:T(8,128)(2,1)}, u32[]{:S(2)}, u32[]{:S(2)}) async-start(bf16[32,176,128]{2,1,0:T(8,128)(2,1)} %pad_maximum_fusion.3), calls=%async_computation.12 | async-start | bytes 2883584 | tf_op jit(solution)/shard_map/all_to_all | solution.py:22
  315.4 1.9 fusion.17
  319.3 15.3 %all-to-all-done.12 = bf16[32,176,128]{2,1,0:T(8,128)(2,1)} async-done(((bf16[32,176,128]{2,1,0:T(8,128)(2,1)}), bf16[32,176,128]{2,1,0:T(8,128)(2,1)}, u32[]{:S(2)}, u32[]{:S(2)}) %all-to-all-start.12) | async-done | bytes 1441824 | tf_op jit(solution)/shard_map/all_to_all | solution.py:22
  337.3 3.4 all-to-all-start.13
  340.8 1.6 convolution_add_fusion.3
  342.5 7.7 %all-to-all-done.13 = f32[8,32,128]{2,1,0:T(8,128)S(1)} async-done(((f32[8,32,128]{2,1,0:T(8,128)}), f32[8,32,128]{2,1,0:T(8,128)S(1)}, u32[]{:S(2)}, u32[]{:S(2)}) %all-to-all-start.13) | async-done | bytes 131104 | tf_op jit(solution)/shard_map/all_to_all | solution.py:18
  (312 shorter events, 87.0 us)
Async XLA Ops:
  0.6 15.2 %copy-start = (bf16[4,24,128,128]{3,2,1,0:T(8,128)(2,1)S(1)}, bf16[4,24,128,128]{3,2,1,0:T(8,128)(2,1)}, u32[]{:S(2)}) copy-start(bf16[4,24,128,128]{3,2,1,0:T(8,128)(2,1)} %param.14) | copy-start | bytes 9437188
  5.2 16.0 %all-to-all-start = ((f32[8,32,128]{2,1,0:T(8,128)}), f32[8,32,128]{2,1,0:T(8,128)S(1)}, u32[]{:S(2)}, u32[]{:S(2)}) async-start(f32[8,32,128]{2,1,0:T(8,128)} %select_maximum_fusion.9), calls=%async_computation | async-start | bytes 262144 | tf_op jit(solution)/shard_map/all_to_all | solution.py:18
  17.6 12.0 %copy-start.55 = (s32[4,24]{1,0:T(4,128)S(1)}, s32[4,24]{1,0:T(4,128)}, u32[]{:S(2)}) copy-start(s32[4,24]{1,0:T(4,128)} %param.15) | copy-start | bytes 1156
  22.7 16.1 %all-to-all-start.1 = ((bf16[16,176,128]{2,1,0:T(8,128)(2,1)}), bf16[16,176,128]{2,1,0:T(8,128)(2,1)}, u32[]{:S(2)}, u32[]{:S(2)}) async-start(bf16[16,176,128]{2,1,0:T(8,128)(2,1)} %broadcast_in_dim.33), calls=%async_computation.1 | async-start | bytes 1441792 | tf_op jit(solution)/shard_map/all_to_all | solution.py:28
  29.6 19.0 %copy-start.36 = (s32[96]{0:T(128)}, s32[96]{0:T(128)S(1)}, u32[]{:S(2)}) copy-start(s32[96]{0:T(128)S(1)} %reshape.429) | copy-start | bytes 1156
  29.7 89.2 %copy-start.40 = (pred[96]{0:T(512)(128)(4,1)}, pred[96]{0:T(512)(128)(4,1)S(1)}, u32[]{:S(2)}) copy-start(pred[96]{0:T(512)(128)(4,1)S(1)} %lt.39) | copy-start | bytes 292
  38.8 30.2 %all-to-all-start.2 = ((bf16[32,176,128]{2,1,0:T(8,128)(2,1)}), bf16[32,176,128]{2,1,0:T(8,128)(2,1)}, u32[]{:S(2)}, u32[]{:S(2)}) async-start(bf16[32,176,128]{2,1,0:T(8,128)(2,1)} %pad_maximum_fusion), calls=%async_computation.2 | async-start | bytes 2883584 | tf_op jit(solution)/shard_map/all_to_all | solution.py:22
  48.7 70.3 %copy-start.45 = (pred[96,2,11]{0,2,1:T(8,128)(4,1)}, pred[96,2,11]{0,2,1:T(8,128)(4,1)S(1)}, u32[]{:S(2)}) copy-start(pred[96,2,11]{0,2,1:T(8,128)(4,1)S(1)} %iota_compare_fusion.7) | copy-start | bytes 6340
  48.7 24.1 %collective-permute-start = (bf16[16,176,128]{2,1,0:T(8,128)(2,1)}, bf16[16,176,128]{2,1,0:T(8,128)(2,1)}, u32[]{:S(2)}, u32[]{:S(2)}) collective-permute-start(bf16[16,176,128]{2,1,0:T(8,128)(2,1)} %all-to-all-done.1), channel_id=1, source_target_pairs={{0,1},{1,0},{2,3},{3,2},{4,5},{5,4},{6,7},{7,6},{8,9},{9,8},{10,11... | collective-permute-start | bytes 2162696 | tf_op jit(solution)/shard_map/ppermute | solution.py:29
  49.2 25.0 %copy-start.51 = (pred[96,2,16]{0,2,1:T(8,128)(4,1)}, pred[96,2,16]{0,2,1:T(8,128)(4,1)S(1)}, u32[]{:S(2)}) copy-start(pred[96,2,16]{0,2,1:T(8,128)(4,1)S(1)} %broadcast_and_fusion) | copy-start | bytes 9220
  77.7 4.4 %copy-start.3 = (bf16[32,512]{1,0:T(8,128)(2,1)S(1)}, bf16[32,512]{1,0:T(8,128)(2,1)}, u32[]{:S(2)}) copy-start(bf16[32,512]{1,0:T(8,128)(2,1)} %param.19) | copy-start | bytes 98308
  82.1 17.8 %copy-start.14 = (bf16[32,512]{1,0:T(8,128)(2,1)}, bf16[32,512]{1,0:T(8,128)(2,1)S(1)}, u32[]{:S(2)}) copy-start(bf16[32,512]{1,0:T(8,128)(2,1)S(1)} %get-tuple-element.25) | copy-start | bytes 98308
  85.7 12.9 %all-to-all-start.3 = ((f32[8,32,128]{2,1,0:T(8,128)}), f32[8,32,128]{2,1,0:T(8,128)S(1)}, u32[]{:S(2)}, u32[]{:S(2)}) async-start(f32[8,32,128]{2,1,0:T(8,128)} %select_maximum_fusion.6), calls=%async_computation.3 | async-start | bytes 262144 | tf_op jit(solution)/shard_map/all_to_all | solution.py:18
  114.9 3.9 %collective-permute-start.1 = (bf16[16,176,128]{2,1,0:T(8,128)(2,1)S(1)}, bf16[16,176,128]{2,1,0:T(8,128)(2,1)S(1)}, u32[]{:S(2)}, u32[]{:S(2)}) collective-permute-start(bf16[16,176,128]{2,1,0:T(8,128)(2,1)S(1)} %all_to_all.70), channel_id=1, source_target_pairs={{0,1},{1,0},{2,3},{3,2},{4,5},{5,4},{6,7},{7,6},{8,9},{9,8},{10,11... | collective-permute-start | bytes 2162696 | tf_op jit(solution)/shard_map/ppermute | solution.py:29
  124.3 33.8 %copy-start.16 = (bf16[32,512]{1,0:T(8,128)(2,1)}, bf16[32,512]{1,0:T(8,128)(2,1)S(1)}, u32[]{:S(2)}) copy-start(bf16[32,512]{1,0:T(8,128)(2,1)S(1)} %get-tuple-element.27) | copy-start | bytes 98308
  127.8 11.8 %all-to-all-start.5 = ((f32[8,32,128]{2,1,0:T(8,128)}), f32[8,32,128]{2,1,0:T(8,128)S(1)}, u32[]{:S(2)}, u32[]{:S(2)}) async-start(f32[8,32,128]{2,1,0:T(8,128)} %select_maximum_fusion.5), calls=%async_computation.5 | async-start | bytes 262144 | tf_op jit(solution)/shard_map/all_to_all | solution.py:18
  141.4 19.1 %copy-start.49 = (s32[1,1,8,16]{3,2,1,0:T(8,128)S(1)}, s32[1,1,8,16]{3,2,1,0:T(8,128)}, u32[]{:S(2)}) copy-start(s32[1,1,8,16]{3,2,1,0:T(8,128)} %param.17) | copy-start | bytes 1540
  141.4 19.7 %copy-start.23 = (f32[176,128]{1,0:T(8,128)S(1)}, f32[176,128]{1,0:T(8,128)}, u32[]{:S(2)}) copy-start(f32[176,128]{1,0:T(8,128)} %copy-done.22) | copy-start | bytes 270340
  158.1 7.7 %collective-permute-start.2 = (bf16[16,176,128]{2,1,0:T(8,128)(2,1)}, bf16[16,176,128]{2,1,0:T(8,128)(2,1)}, u32[]{:S(2)}, u32[]{:S(2)}) collective-permute-start(bf16[16,176,128]{2,1,0:T(8,128)(2,1)} %all_to_all.71), channel_id=1, source_target_pairs={{0,1},{1,0},{2,3},{3,2},{4,5},{5,4},{6,7},{7,6},{8,9},{9,8},{10,11... | collective-permute-start | bytes 2162696 | tf_op jit(solution)/shard_map/ppermute | solution.py:29
  162.7 4.4 %copy-start.41 = (pred[96]{0:T(512)(128)(4,1)S(1)}, pred[96]{0:T(512)(128)(4,1)}, u32[]{:S(2)}) copy-start(pred[96]{0:T(512)(128)(4,1)} %copy-done.40) | copy-start | bytes 292
  169.6 4.4 %copy-start.4 = (bf16[32,512]{1,0:T(8,128)(2,1)S(1)}, bf16[32,512]{1,0:T(8,128)(2,1)}, u32[]{:S(2)}) copy-start(bf16[32,512]{1,0:T(8,128)(2,1)} %param.19) | copy-start | bytes 98308
  173.3 13.7 %copy-start.12 = (bf16[32,512]{1,0:T(8,128)(2,1)}, bf16[32,512]{1,0:T(8,128)(2,1)S(1)}, u32[]{:S(2)}) copy-start(bf16[32,512]{1,0:T(8,128)(2,1)S(1)} %get-tuple-element.31) | copy-start | bytes 98308
  180.6 6.1 %copy-start.50 = (s32[1,1,8,16]{3,2,1,0:T(8,128)S(1)}, s32[1,1,8,16]{3,2,1,0:T(8,128)}, u32[]{:S(2)}) copy-start(s32[1,1,8,16]{3,2,1,0:T(8,128)} %param.17) | copy-start | bytes 1540
  180.6 26.5 %all-to-all-start.7 = ((bf16[32,176,128]{2,1,0:T(8,128)(2,1)}), bf16[32,176,128]{2,1,0:T(8,128)(2,1)}, u32[]{:S(2)}, u32[]{:S(2)}) async-start(bf16[32,176,128]{2,1,0:T(8,128)(2,1)} %pad_maximum_fusion.1), calls=%async_computation.7 | async-start | bytes 2883584 | tf_op jit(solution)/shard_map/all_to_all | solution.py:22
  213.4 12.9 %all-to-all-start.8 = ((f32[8,32,128]{2,1,0:T(8,128)}), f32[8,32,128]{2,1,0:T(8,128)S(1)}, u32[]{:S(2)}, u32[]{:S(2)}) async-start(f32[8,32,128]{2,1,0:T(8,128)} %select_maximum_fusion.2), calls=%async_computation.8 | async-start | bytes 262144 | tf_op jit(solution)/shard_map/all_to_all | solution.py:18
  231.4 8.8 %copy-start.20 = (bf16[32,512]{1,0:T(8,128)(2,1)}, bf16[32,512]{1,0:T(8,128)(2,1)S(1)}, u32[]{:S(2)}) copy-start(bf16[32,512]{1,0:T(8,128)(2,1)S(1)} %get-tuple-element.33) | copy-start | bytes 98308
  235.2 14.8 %all-to-all-start.9 = ((bf16[16,176,128]{2,1,0:T(8,128)(2,1)}), bf16[16,176,128]{2,1,0:T(8,128)(2,1)}, u32[]{:S(2)}, u32[]{:S(2)}) async-start(bf16[16,176,128]{2,1,0:T(8,128)(2,1)} %broadcast_in_dim.78), calls=%async_computation.9 | async-start | bytes 1441792 | tf_op jit(solution)/shard_map/all_to_all | solution.py:28
  244.2 14.8 %copy-start.13 = (bf16[32,512]{1,0:T(8,128)(2,1)S(1)}, bf16[32,512]{1,0:T(8,128)(2,1)}, u32[]{:S(2)}) copy-start(bf16[32,512]{1,0:T(8,128)(2,1)} %copy-done.12) | copy-start | bytes 98308
  244.2 14.9 %copy-start.17 = (bf16[32,512]{1,0:T(8,128)(2,1)S(1)}, bf16[32,512]{1,0:T(8,128)(2,1)}, u32[]{:S(2)}) copy-start(bf16[32,512]{1,0:T(8,128)(2,1)} %copy-done.16) | copy-start | bytes 98308
  244.2 14.9 %copy-start.35 = (bf16[32,32]{0,1:T(8,128)(2,1)S(1)}, bf16[32,32]{0,1:T(8,128)(2,1)}, u32[]{:S(2)}) copy-start(bf16[32,32]{0,1:T(8,128)(2,1)} %copy.368) | copy-start | bytes 6148
  250.0 28.9 %all-to-all-start.10 = ((bf16[32,176,128]{2,1,0:T(8,128)(2,1)}), bf16[32,176,128]{2,1,0:T(8,128)(2,1)}, u32[]{:S(2)}, u32[]{:S(2)}) async-start(bf16[32,176,128]{2,1,0:T(8,128)(2,1)} %pad_maximum_fusion.2), calls=%async_computation.10 | async-start | bytes 2883584 | tf_op jit(solution)/shard_map/all_to_all | solution.py:22
  258.5 22.6 %collective-permute-start.3 = (bf16[16,176,128]{2,1,0:T(8,128)(2,1)}, bf16[16,176,128]{2,1,0:T(8,128)(2,1)}, u32[]{:S(2)}, u32[]{:S(2)}) collective-permute-start(bf16[16,176,128]{2,1,0:T(8,128)(2,1)} %all-to-all-done.9), channel_id=1, source_target_pairs={{0,1},{1,0},{2,3},{3,2},{4,5},{5,4},{6,7},{7,6},{8,9},{9,8},{10,11... | collective-permute-start | bytes 2162696 | tf_op jit(solution)/shard_map/ppermute | solution.py:29
  284.5 13.6 %all-to-all-start.11 = ((f32[8,32,128]{2,1,0:T(8,128)}), f32[8,32,128]{2,1,0:T(8,128)}, u32[]{:S(2)}, u32[]{:S(2)}) async-start(f32[8,32,128]{2,1,0:T(8,128)} %select_maximum_fusion.1), calls=%async_computation.11 | async-start | bytes 262144 | tf_op jit(solution)/shard_map/all_to_all | solution.py:18
  288.5 13.4 %copy-start.6 = (f32[32,512]{1,0:T(8,128)S(1)}, f32[32,512]{1,0:T(8,128)}, u32[]{:S(2)}) copy-start(f32[32,512]{1,0:T(8,128)} %get-tuple-element.26) | copy-start | bytes 196612
  307.9 6.3 %copy-start.11 = (bf16[32,512]{1,0:T(8,128)(2,1)S(1)}, bf16[32,512]{1,0:T(8,128)(2,1)}, u32[]{:S(2)}) copy-start(bf16[32,512]{1,0:T(8,128)(2,1)} %copy-done.10) | copy-start | bytes 98308
  307.9 6.5 %copy-start.19 = (bf16[32,512]{1,0:T(8,128)(2,1)S(1)}, bf16[32,512]{1,0:T(8,128)(2,1)}, u32[]{:S(2)}) copy-start(bf16[32,512]{1,0:T(8,128)(2,1)} %copy-done.18) | copy-start | bytes 98308
  307.9 6.5 %copy-start.33 = (bf16[32,32]{1,0:T(8,128)(2,1)S(1)}, bf16[32,32]{1,0:T(8,128)(2,1)}, u32[]{:S(2)}) copy-start(bf16[32,32]{1,0:T(8,128)(2,1)} %copy-done.32) | copy-start | bytes 6148
  307.9 6.6 %copy-start.21 = (bf16[32,512]{1,0:T(8,128)(2,1)S(1)}, bf16[32,512]{1,0:T(8,128)(2,1)}, u32[]{:S(2)}) copy-start(bf16[32,512]{1,0:T(8,128)(2,1)} %copy-done.20) | copy-start | bytes 98308
  307.9 6.6 %copy-start.31 = (bf16[32,32]{1,0:T(8,128)(2,1)S(1)}, bf16[32,32]{1,0:T(8,128)(2,1)}, u32[]{:S(2)}) copy-start(bf16[32,32]{1,0:T(8,128)(2,1)} %copy-done.30) | copy-start | bytes 6148
  307.9 7.5 %copy-start.47 = (pred[96,2,11]{0,2,1:T(8,128)(4,1)S(1)}, pred[96,2,11]{0,2,1:T(8,128)(4,1)}, u32[]{:S(2)}) copy-start(pred[96,2,11]{0,2,1:T(8,128)(4,1)} %copy-done.45) | copy-start | bytes 6340
  307.9 7.4 %copy-start.54 = (pred[96,2,16]{0,2,1:T(8,128)(4,1)S(1)}, pred[96,2,16]{0,2,1:T(8,128)(4,1)}, u32[]{:S(2)}) copy-start(pred[96,2,16]{0,2,1:T(8,128)(4,1)} %copy-done.51) | copy-start | bytes 9220
  307.9 26.7 %all-to-all-start.12 = ((bf16[32,176,128]{2,1,0:T(8,128)(2,1)}), bf16[32,176,128]{2,1,0:T(8,128)(2,1)}, u32[]{:S(2)}, u32[]{:S(2)}) async-start(bf16[32,176,128]{2,1,0:T(8,128)(2,1)} %pad_maximum_fusion.3), calls=%async_computation.12 | async-start | bytes 2883584 | tf_op jit(solution)/shard_map/all_to_all | solution.py:22
  318.5 22.2 %copy-start.15 = (bf16[32,512]{1,0:T(8,128)(2,1)S(1)}, bf16[32,512]{1,0:T(8,128)(2,1)}, u32[]{:S(2)}) copy-start(bf16[32,512]{1,0:T(8,128)(2,1)} %copy-done.14) | copy-start | bytes 98308
  318.5 22.2 %copy-start.27 = (f32[32,512]{1,0:T(8,128)S(1)}, f32[32,512]{1,0:T(8,128)}, u32[]{:S(2)}) copy-start(f32[32,512]{1,0:T(8,128)} %convolution_add_fusion.2) | copy-start | bytes 196612
  318.5 22.2 %copy-start.34 = (bf16[32,32]{0,1:T(8,128)(2,1)S(1)}, bf16[32,32]{0,1:T(8,128)(2,1)}, u32[]{:S(2)}) copy-start(bf16[32,32]{0,1:T(8,128)(2,1)} %copy.369) | copy-start | bytes 6148
  318.5 22.3 %copy-start.29 = (bf16[32,32]{1,0:T(8,128)(2,1)S(1)}, bf16[32,32]{1,0:T(8,128)(2,1)}, u32[]{:S(2)}) copy-start(bf16[32,32]{1,0:T(8,128)(2,1)} %copy-done.28) | copy-start | bytes 6148
  319.3 31.0 %copy-start.26 = (bf16[32,512]{1,0:T(8,128)(2,1)S(1)}, bf16[32,512]{1,0:T(8,128)(2,1)}, u32[]{:S(2)}) copy-start(bf16[32,512]{1,0:T(8,128)(2,1)} %copy-done.25) | copy-start | bytes 98308
  337.3 12.9 %all-to-all-start.13 = ((f32[8,32,128]{2,1,0:T(8,128)}), f32[8,32,128]{2,1,0:T(8,128)S(1)}, u32[]{:S(2)}, u32[]{:S(2)}) async-start(f32[8,32,128]{2,1,0:T(8,128)} %select_maximum_fusion), calls=%async_computation.13 | async-start | bytes 262144 | tf_op jit(solution)/shard_map/all_to_all | solution.py:18
  (24 other events, 44.4 us)

commit v2 on v1

--- a/solution.py
+++ b/solution.py
@@ -159,9 +159,11 @@
         return own_part, chunks
 
     def adjoint_end(adjoint, own_part, back, rates):
-        returned = jnp.moveaxis(back[:, :, :sent], 0, 1).reshape(batch_rows, -1)
         coeffs_b = jnp.sum(back[:, :, sent:], axis=0).astype(jnp.bfloat16)
-        through = own_part + jnp.dot(returned, border_to_row, precision=lax.Precision.HIGHEST)
+        returned = jnp.einsum(
+            "gbk,gkn->bn", back[:, :, :sent], border_to_row.reshape(groups, sent, own_rows), precision=lax.Precision.HIGHEST
+        )
+        through = own_part + returned
         total_signed = through + jnp.dot(coeffs_b, v_factor, preferred_element_type=jnp.float32)
         adjoint = (1.0 - leak) * adjoint + (1.0 - rates * rates) * polarity * total_signed
         return adjoint, coeffs_b

time: 355 us -> 350 us (0.986)
  local copies, waits for them, and re-layouts: 42 us -> 37.7 us
where the time goes in v2:
time: 350 us; the launch traced here: 347 us
  waiting for transfers between devices  122 us (35%)
  starting transfers between devices  73.4 us (21%)
  matrix products  48.5 us (14%)
  local copies, waits for them, and re-layouts  37.7 us (11%)
  other arithmetic  32.9 us (9%)
  blocking collectives  30.6 us (9%)
    all_to_all x4, waiting for transfers between devices, from_each_lane(): return lax.all_to_all(slots, ROW, 0, 0, tiled=True)  69.2 us
    all_to_all x6, waiting for transfers between devices, from_each_region(): return lax.all_to_all(padded, 'region', 0, 0, tiled=True)[..., :width]  42 us
    all_to_all x4, starting transfers between devices, from_each_lane(): return lax.all_to_all(slots, ROW, 0, 0, tiled=True)  30.6 us
    all_to_all x2, blocking collectives, from_every_lane(): mine = lax.all_to_all(copies, chips, 0, 0, tiled=True)  30.6 us
    all_to_all x6, starting transfers between devices, from_each_region(): return lax.all_to_all(padded, 'region', 0, 0, tiled=True)[..., :width]  26.3 us
    all_to_all x2, starting transfers between devices, from_every_lane(): mine = lax.all_to_all(copies, chips, 0, 0, tiled=True)  11.2 us
    another operation x8, local copies, waits for them, and re-layouts, from_every_lane(): return jnp.stack([mine, sibling])  10.8 us
    dot_general x4, matrix products, adjoint_start(): jnp.einsum('lts,bsk->ltbk', picks, spread.reshape(batch_rows, -1, 128), p...  10.2 us
  transfers between devices with their start and end apart: 16, of which 13 were waited for; matrix products, arithmetic and copies ran while one was open for 13% of the time, Pallas kernels for 0%

profile of v2, /device:TPU:9, one launch (start us, length us, event | category | flops | bytes accessed | tf_op | source)
XLA Modules:
  0.0 346.6 jit_solution(13604570735044175440)
XLA Ops:
  5.2 8.2 %all-to-all-start = ((f32[8,32,128]{2,1,0:T(8,128)}), f32[8,32,128]{2,1,0:T(8,128)S(1)}, u32[]{:S(2)}, u32[]{:S(2)}) async-start(f32[8,32,128]{2,1,0:T(8,128)} %select_maximum_fusion.9), calls=%async_computation | async-start | bytes 262144 | tf_op jit(solution)/shard_map/all_to_all | solution.py:18
  16.4 1.7 fusion.103
  18.2 2.9 all-to-all-done
  22.7 6.8 %all-to-all-start.1 = ((bf16[16,176,128]{2,1,0:T(8,128)(2,1)}), bf16[16,176,128]{2,1,0:T(8,128)(2,1)}, u32[]{:S(2)}, u32[]{:S(2)}) async-start(bf16[16,176,128]{2,1,0:T(8,128)(2,1)} %broadcast_in_dim.33), calls=%async_computation.1 | async-start | bytes 1441792 | tf_op jit(solution)/shard_map/all_to_all | solution.py:28
  30.5 3.5 %convolution_convert_fusion.3 = bf16[32,5,32,128]{3,0,2,1:T(8,128)(2,1)S(1)} fusion(f32[32,96,128]{2,0,1:T(8,128)} %bitcast.313, s32[32,5]{0,1:T(8,128)S(1)} %multiply_add_fusion, s32[96]{0:T(128)S(1)} %reshape.431, pred[96]{0:T(512)(128)(4,1)S(1)} %lt.39), kind=kOutput, calls=%fused_computation.7 | convolution fusion | flops 755660800 | bytes 2884704 | tf_op jit(solution)/shard_map/lts,bsk->ltbk/dot_general | solution.py:141
  35.8 3.0 all-to-all-done.1
  38.8 9.8 %all-to-all-start.2 = ((bf16[32,176,128]{2,1,0:T(8,128)(2,1)}), bf16[32,176,128]{2,1,0:T(8,128)(2,1)}, u32[]{:S(2)}, u32[]{:S(2)}) async-start(bf16[32,176,128]{2,1,0:T(8,128)(2,1)} %pad_maximum_fusion), calls=%async_computation.2 | async-start | bytes 2883584 | tf_op jit(solution)/shard_map/all_to_all | solution.py:22
  49.2 2.2 copy.337
  51.4 17.7 %all-to-all-done.2 = bf16[32,176,128]{2,1,0:T(8,128)(2,1)} async-done(((bf16[32,176,128]{2,1,0:T(8,128)(2,1)}), bf16[32,176,128]{2,1,0:T(8,128)(2,1)}, u32[]{:S(2)}, u32[]{:S(2)}) %all-to-all-start.2) | async-done | bytes 1441824 | tf_op jit(solution)/shard_map/all_to_all | solution.py:22
  74.2 1.7 fusion.8
  75.9 1.8 convolution_bitcast_fusion.9
  80.5 1.6 multiply_convert_fusion.2
  83.3 1.7 select_maximum_fusion.6
  85.0 3.7 %all-to-all-start.3 = ((f32[8,32,128]{2,1,0:T(8,128)}), f32[8,32,128]{2,1,0:T(8,128)S(1)}, u32[]{:S(2)}, u32[]{:S(2)}) async-start(f32[8,32,128]{2,1,0:T(8,128)} %select_maximum_fusion.6), calls=%async_computation.3 | async-start | bytes 262144 | tf_op jit(solution)/shard_map/all_to_all | solution.py:18
  88.7 9.6 %all-to-all-done.3 = f32[8,32,128]{2,1,0:T(8,128)S(1)} async-done(((f32[8,32,128]{2,1,0:T(8,128)}), f32[8,32,128]{2,1,0:T(8,128)S(1)}, u32[]{:S(2)}, u32[]{:S(2)}) %all-to-all-start.3) | async-done | bytes 131104 | tf_op jit(solution)/shard_map/all_to_all | solution.py:18
  99.6 15.0 %all_to_all.70 = bf16[16,176,128]{2,1,0:T(8,128)(2,1)S(1)} all-to-all(bf16[16,176,128]{2,1,0:T(8,128)(2,1)S(1)} %broadcast_in_dim.72), channel_id=1, replica_groups=mesh['region'=8,'row_0'=4,'row_1'=4,'row_2'=2] {'row_0','row_1'}, dimensions={0} | all-to-all | bytes 1441792 | tf_op jit(solution)/shard_map/all_to_all | solution.py:28
  114.6 2.0 collective-permute-start.1
  116.8 1.6 collective-permute-done.1
  119.3 1.8 convolution_bitcast_fusion.7
  127.5 3.5 %all-to-all-start.5 = ((f32[8,32,128]{2,1,0:T(8,128)}), f32[8,32,128]{2,1,0:T(8,128)S(1)}, u32[]{:S(2)}, u32[]{:S(2)}) async-start(f32[8,32,128]{2,1,0:T(8,128)} %select_maximum_fusion.5), calls=%async_computation.5 | async-start | bytes 262144 | tf_op jit(solution)/shard_map/all_to_all | solution.py:18
  131.7 7.6 %all-to-all-done.5 = f32[8,32,128]{2,1,0:T(8,128)S(1)} async-done(((f32[8,32,128]{2,1,0:T(8,128)}), f32[8,32,128]{2,1,0:T(8,128)S(1)}, u32[]{:S(2)}, u32[]{:S(2)}) %all-to-all-start.5) | async-done | bytes 131104 | tf_op jit(solution)/shard_map/all_to_all | solution.py:18
  142.2 15.6 %all_to_all.71 = bf16[16,176,128]{2,1,0:T(8,128)(2,1)} all-to-all(bf16[16,176,128]{2,1,0:T(8,128)(2,1)S(1)} %broadcast_in_dim.74), channel_id=1, replica_groups=mesh['region'=8,'row_0'=4,'row_1'=4,'row_2'=2] {'row_0','row_1'}, dimensions={0} | all-to-all | bytes 1441792 | tf_op jit(solution)/shard_map/all_to_all | solution.py:28
  157.8 2.4 collective-permute-start.2
  161.0 1.7 fusion.41
  166.0 1.8 convolution_bitcast_fusion.5
  172.2 1.7 fusion.129
  174.9 2.2 convolution_convert_fusion.2
  178.8 6.1 %all-to-all-start.7 = ((bf16[32,176,128]{2,1,0:T(8,128)(2,1)}), bf16[32,176,128]{2,1,0:T(8,128)(2,1)}, u32[]{:S(2)}, u32[]{:S(2)}) async-start(bf16[32,176,128]{2,1,0:T(8,128)(2,1)} %pad_maximum_fusion.1), calls=%async_computation.7 | async-start | bytes 2883584 | tf_op jit(solution)/shard_map/all_to_all | solution.py:22
  186.0 19.3 %all-to-all-done.7 = bf16[32,176,128]{2,1,0:T(8,128)(2,1)} async-done(((bf16[32,176,128]{2,1,0:T(8,128)(2,1)}), bf16[32,176,128]{2,1,0:T(8,128)(2,1)}, u32[]{:S(2)}, u32[]{:S(2)}) %all-to-all-start.7) | async-done | bytes 1441824 | tf_op jit(solution)/shard_map/all_to_all | solution.py:22
  211.6 3.4 all-to-all-start.8
  217.2 7.3 %all-to-all-done.8 = f32[8,32,128]{2,1,0:T(8,128)S(1)} async-done(((f32[8,32,128]{2,1,0:T(8,128)}), f32[8,32,128]{2,1,0:T(8,128)S(1)}, u32[]{:S(2)}, u32[]{:S(2)}) %all-to-all-start.8) | async-done | bytes 131104 | tf_op jit(solution)/shard_map/all_to_all | solution.py:18
  227.0 1.7 fusion.130
  231.9 4.4 %all-to-all-start.9 = ((bf16[16,176,128]{2,1,0:T(8,128)(2,1)}), bf16[16,176,128]{2,1,0:T(8,128)(2,1)}, u32[]{:S(2)}, u32[]{:S(2)}) async-start(bf16[16,176,128]{2,1,0:T(8,128)(2,1)} %broadcast_in_dim.78), calls=%async_computation.9 | async-start | bytes 1441792 | tf_op jit(solution)/shard_map/all_to_all | solution.py:28
  237.0 2.2 convolution_convert_fusion.1
  241.0 5.7 %all-to-all-done.9 = bf16[16,176,128]{2,1,0:T(8,128)(2,1)} async-done(((bf16[16,176,128]{2,1,0:T(8,128)(2,1)}), bf16[16,176,128]{2,1,0:T(8,128)(2,1)}, u32[]{:S(2)}, u32[]{:S(2)}) %all-to-all-start.9) | async-done | bytes 720928 | tf_op jit(solution)/shard_map/all_to_all | solution.py:28
  246.8 8.5 %all-to-all-start.10 = ((bf16[32,176,128]{2,1,0:T(8,128)(2,1)}), bf16[32,176,128]{2,1,0:T(8,128)(2,1)}, u32[]{:S(2)}, u32[]{:S(2)}) async-start(bf16[32,176,128]{2,1,0:T(8,128)(2,1)} %pad_maximum_fusion.2), calls=%async_computation.10 | async-start | bytes 2883584 | tf_op jit(solution)/shard_map/all_to_all | solution.py:22
  256.6 2.2 copy.380
  258.8 16.9 %all-to-all-done.10 = bf16[32,176,128]{2,1,0:T(8,128)(2,1)} async-done(((bf16[32,176,128]{2,1,0:T(8,128)(2,1)}), bf16[32,176,128]{2,1,0:T(8,128)(2,1)}, u32[]{:S(2)}, u32[]{:S(2)}) %all-to-all-start.10) | async-done | bytes 1441824 | tf_op jit(solution)/shard_map/all_to_all | solution.py:22
  277.9 2.2 copy.381
  281.2 4.1 %all-to-all-start.11 = ((f32[8,32,128]{2,1,0:T(8,128)}), f32[8,32,128]{2,1,0:T(8,128)}, u32[]{:S(2)}, u32[]{:S(2)}) async-start(f32[8,32,128]{2,1,0:T(8,128)} %select_maximum_fusion.1), calls=%async_computation.11 | async-start | bytes 262144 | tf_op jit(solution)/shard_map/all_to_all | solution.py:18
  288.1 6.9 %all-to-all-done.11 = f32[8,32,128]{2,1,0:T(8,128)} async-done(((f32[8,32,128]{2,1,0:T(8,128)}), f32[8,32,128]{2,1,0:T(8,128)}, u32[]{:S(2)}, u32[]{:S(2)}) %all-to-all-start.11) | async-done | bytes 131104 | tf_op jit(solution)/shard_map/all_to_all | solution.py:18
  299.4 2.2 convolution_convert_fusion
  303.4 6.2 %all-to-all-start.12 = ((bf16[32,176,128]{2,1,0:T(8,128)(2,1)}), bf16[32,176,128]{2,1,0:T(8,128)(2,1)}, u32[]{:S(2)}, u32[]{:S(2)}) async-start(bf16[32,176,128]{2,1,0:T(8,128)(2,1)} %pad_maximum_fusion.3), calls=%async_computation.12 | async-start | bytes 2883584 | tf_op jit(solution)/shard_map/all_to_all | solution.py:22
  310.8 1.9 fusion.17
  314.8 15.3 %all-to-all-done.12 = bf16[32,176,128]{2,1,0:T(8,128)(2,1)} async-done(((bf16[32,176,128]{2,1,0:T(8,128)(2,1)}), bf16[32,176,128]{2,1,0:T(8,128)(2,1)}, u32[]{:S(2)}, u32[]{:S(2)}) %all-to-all-start.12) | async-done | bytes 1441824 | tf_op jit(solution)/shard_map/all_to_all | solution.py:22
  332.7 3.4 all-to-all-start.13
  336.3 1.6 convolution_add_fusion.3
  337.9 7.7 %all-to-all-done.13 = f32[8,32,128]{2,1,0:T(8,128)S(1)} async-done(((f32[8,32,128]{2,1,0:T(8,128)}), f32[8,32,128]{2,1,0:T(8,128)S(1)}, u32[]{:S(2)}, u32[]{:S(2)}) %all-to-all-start.13) | async-done | bytes 131104 | tf_op jit(solution)/shard_map/all_to_all | solution.py:18
  (306 shorter events, 82.5 us)
Async XLA Ops:
  0.6 15.7 %copy-start = (bf16[4,24,128,128]{3,2,1,0:T(8,128)(2,1)S(1)}, bf16[4,24,128,128]{3,2,1,0:T(8,128)(2,1)}, u32[]{:S(2)}) copy-start(bf16[4,24,128,128]{3,2,1,0:T(8,128)(2,1)} %param.14) | copy-start | bytes 9437188
  5.2 16.0 %all-to-all-start = ((f32[8,32,128]{2,1,0:T(8,128)}), f32[8,32,128]{2,1,0:T(8,128)S(1)}, u32[]{:S(2)}, u32[]{:S(2)}) async-start(f32[8,32,128]{2,1,0:T(8,128)} %select_maximum_fusion.9), calls=%async_computation | async-start | bytes 262144 | tf_op jit(solution)/shard_map/all_to_all | solution.py:18
  18.1 11.5 %copy-start.55 = (s32[4,24]{1,0:T(4,128)S(1)}, s32[4,24]{1,0:T(4,128)}, u32[]{:S(2)}) copy-start(s32[4,24]{1,0:T(4,128)} %param.15) | copy-start | bytes 1156
  22.7 16.1 %all-to-all-start.1 = ((bf16[16,176,128]{2,1,0:T(8,128)(2,1)}), bf16[16,176,128]{2,1,0:T(8,128)(2,1)}, u32[]{:S(2)}, u32[]{:S(2)}) async-start(bf16[16,176,128]{2,1,0:T(8,128)(2,1)} %broadcast_in_dim.33), calls=%async_computation.1 | async-start | bytes 1441792 | tf_op jit(solution)/shard_map/all_to_all | solution.py:28
  29.6 19.0 %copy-start.38 = (s32[96]{0:T(128)}, s32[96]{0:T(128)S(1)}, u32[]{:S(2)}) copy-start(s32[96]{0:T(128)S(1)} %reshape.431) | copy-start | bytes 1156
  30.4 88.3 %copy-start.42 = (pred[96]{0:T(512)(128)(4,1)}, pred[96]{0:T(512)(128)(4,1)S(1)}, u32[]{:S(2)}) copy-start(pred[96]{0:T(512)(128)(4,1)S(1)} %lt.39) | copy-start | bytes 292
  38.8 30.2 %all-to-all-start.2 = ((bf16[32,176,128]{2,1,0:T(8,128)(2,1)}), bf16[32,176,128]{2,1,0:T(8,128)(2,1)}, u32[]{:S(2)}, u32[]{:S(2)}) async-start(bf16[32,176,128]{2,1,0:T(8,128)(2,1)} %pad_maximum_fusion), calls=%async_computation.2 | async-start | bytes 2883584 | tf_op jit(solution)/shard_map/all_to_all | solution.py:22
  48.7 25.4 %copy-start.47 = (pred[96,2,11]{0,2,1:T(8,128)(4,1)}, pred[96,2,11]{0,2,1:T(8,128)(4,1)S(1)}, u32[]{:S(2)}) copy-start(pred[96,2,11]{0,2,1:T(8,128)(4,1)S(1)} %iota_compare_fusion.7) | copy-start | bytes 6340
  48.7 24.1 %collective-permute-start = (bf16[16,176,128]{2,1,0:T(8,128)(2,1)}, bf16[16,176,128]{2,1,0:T(8,128)(2,1)}, u32[]{:S(2)}, u32[]{:S(2)}) collective-permute-start(bf16[16,176,128]{2,1,0:T(8,128)(2,1)} %all-to-all-done.1), channel_id=1, source_target_pairs={{0,1},{1,0},{2,3},{3,2},{4,5},{5,4},{6,7},{7,6},{8,9},{9,8},{10,11... | collective-permute-start | bytes 2162696 | tf_op jit(solution)/shard_map/ppermute | solution.py:29
  49.2 25.0 %copy-start.51 = (pred[96,2,16]{0,2,1:T(8,128)(4,1)}, pred[96,2,16]{0,2,1:T(8,128)(4,1)S(1)}, u32[]{:S(2)}) copy-start(pred[96,2,16]{0,2,1:T(8,128)(4,1)S(1)} %broadcast_and_fusion) | copy-start | bytes 9220
  77.7 4.4 %copy-start.3 = (bf16[32,512]{1,0:T(8,128)(2,1)S(1)}, bf16[32,512]{1,0:T(8,128)(2,1)}, u32[]{:S(2)}) copy-start(bf16[32,512]{1,0:T(8,128)(2,1)} %param.19) | copy-start | bytes 98308
  77.7 4.5 %copy-start.36 = (s32[1,1,8,16]{3,2,1,0:T(8,128)S(1)}, s32[1,1,8,16]{3,2,1,0:T(8,128)}, u32[]{:S(2)}) copy-start(s32[1,1,8,16]{3,2,1,0:T(8,128)} %param.17) | copy-start | bytes 1540
  82.1 17.5 %copy-start.14 = (bf16[32,512]{1,0:T(8,128)(2,1)}, bf16[32,512]{1,0:T(8,128)(2,1)S(1)}, u32[]{:S(2)}) copy-start(bf16[32,512]{1,0:T(8,128)(2,1)S(1)} %get-tuple-element.25) | copy-start | bytes 98308
  85.0 13.3 %all-to-all-start.3 = ((f32[8,32,128]{2,1,0:T(8,128)}), f32[8,32,128]{2,1,0:T(8,128)S(1)}, u32[]{:S(2)}, u32[]{:S(2)}) async-start(f32[8,32,128]{2,1,0:T(8,128)} %select_maximum_fusion.6), calls=%async_computation.3 | async-start | bytes 262144 | tf_op jit(solution)/shard_map/all_to_all | solution.py:18
  114.6 3.9 %collective-permute-start.1 = (bf16[16,176,128]{2,1,0:T(8,128)(2,1)S(1)}, bf16[16,176,128]{2,1,0:T(8,128)(2,1)S(1)}, u32[]{:S(2)}, u32[]{:S(2)}) collective-permute-start(bf16[16,176,128]{2,1,0:T(8,128)(2,1)S(1)} %all_to_all.70), channel_id=1, source_target_pairs={{0,1},{1,0},{2,3},{3,2},{4,5},{5,4},{6,7},{7,6},{8,9},{9,8},{10,11... | collective-permute-start | bytes 2162696 | tf_op jit(solution)/shard_map/ppermute | solution.py:29
  124.0 33.8 %copy-start.16 = (bf16[32,512]{1,0:T(8,128)(2,1)}, bf16[32,512]{1,0:T(8,128)(2,1)S(1)}, u32[]{:S(2)}) copy-start(bf16[32,512]{1,0:T(8,128)(2,1)S(1)} %get-tuple-element.27) | copy-start | bytes 98308
  127.5 11.8 %all-to-all-start.5 = ((f32[8,32,128]{2,1,0:T(8,128)}), f32[8,32,128]{2,1,0:T(8,128)S(1)}, u32[]{:S(2)}, u32[]{:S(2)}) async-start(f32[8,32,128]{2,1,0:T(8,128)} %select_maximum_fusion.5), calls=%async_computation.5 | async-start | bytes 262144 | tf_op jit(solution)/shard_map/all_to_all | solution.py:18
  141.1 19.9 %slice-start = ((f32[176,128]{1,0:T(8,128)}), f32[128,128]{1,0:T(8,128)S(1)}, s32[]{:S(2)}) async-start(f32[176,128]{1,0:T(8,128)} %copy-done.22), calls=%async_computation.14 | async-start | bytes 131072 | tf_op jit(solution)/shard_map/slice | solution.py:154
  157.8 6.2 %collective-permute-start.2 = (bf16[16,176,128]{2,1,0:T(8,128)(2,1)}, bf16[16,176,128]{2,1,0:T(8,128)(2,1)}, u32[]{:S(2)}, u32[]{:S(2)}) collective-permute-start(bf16[16,176,128]{2,1,0:T(8,128)(2,1)} %all_to_all.71), channel_id=1, source_target_pairs={{0,1},{1,0},{2,3},{3,2},{4,5},{5,4},{6,7},{7,6},{8,9},{9,8},{10,11... | collective-permute-start | bytes 2162696 | tf_op jit(solution)/shard_map/ppermute | solution.py:29
  161.0 4.3 %copy-start.49 = (pred[96,2,11]{0,2,1:T(8,128)(4,1)S(1)}, pred[96,2,11]{0,2,1:T(8,128)(4,1)}, u32[]{:S(2)}) copy-start(pred[96,2,11]{0,2,1:T(8,128)(4,1)} %copy-done.47) | copy-start | bytes 6340
  167.8 4.4 %copy-start.4 = (bf16[32,512]{1,0:T(8,128)(2,1)S(1)}, bf16[32,512]{1,0:T(8,128)(2,1)}, u32[]{:S(2)}) copy-start(bf16[32,512]{1,0:T(8,128)(2,1)} %param.19) | copy-start | bytes 98308
  171.6 13.7 %copy-start.12 = (bf16[32,512]{1,0:T(8,128)(2,1)}, bf16[32,512]{1,0:T(8,128)(2,1)S(1)}, u32[]{:S(2)}) copy-start(bf16[32,512]{1,0:T(8,128)(2,1)S(1)} %get-tuple-element.31) | copy-start | bytes 98308
  178.8 6.1 %copy-start.37 = (s32[1,1,8,16]{3,2,1,0:T(8,128)S(1)}, s32[1,1,8,16]{3,2,1,0:T(8,128)}, u32[]{:S(2)}) copy-start(s32[1,1,8,16]{3,2,1,0:T(8,128)} %param.17) | copy-start | bytes 1540
  178.8 26.5 %all-to-all-start.7 = ((bf16[32,176,128]{2,1,0:T(8,128)(2,1)}), bf16[32,176,128]{2,1,0:T(8,128)(2,1)}, u32[]{:S(2)}, u32[]{:S(2)}) async-start(bf16[32,176,128]{2,1,0:T(8,128)(2,1)} %pad_maximum_fusion.1), calls=%async_computation.7 | async-start | bytes 2883584 | tf_op jit(solution)/shard_map/all_to_all | solution.py:22
  211.6 12.9 %all-to-all-start.8 = ((f32[8,32,128]{2,1,0:T(8,128)}), f32[8,32,128]{2,1,0:T(8,128)S(1)}, u32[]{:S(2)}, u32[]{:S(2)}) async-start(f32[8,32,128]{2,1,0:T(8,128)} %select_maximum_fusion.2), calls=%async_computation.8 | async-start | bytes 262144 | tf_op jit(solution)/shard_map/all_to_all | solution.py:18
  228.7 8.2 %copy-start.20 = (bf16[32,512]{1,0:T(8,128)(2,1)}, bf16[32,512]{1,0:T(8,128)(2,1)S(1)}, u32[]{:S(2)}) copy-start(bf16[32,512]{1,0:T(8,128)(2,1)S(1)} %get-tuple-element.33) | copy-start | bytes 98308
  231.9 14.8 %all-to-all-start.9 = ((bf16[16,176,128]{2,1,0:T(8,128)(2,1)}), bf16[16,176,128]{2,1,0:T(8,128)(2,1)}, u32[]{:S(2)}, u32[]{:S(2)}) async-start(bf16[16,176,128]{2,1,0:T(8,128)(2,1)} %broadcast_in_dim.78), calls=%async_computation.9 | async-start | bytes 1441792 | tf_op jit(solution)/shard_map/all_to_all | solution.py:28
  241.0 14.7 %copy-start.13 = (bf16[32,512]{1,0:T(8,128)(2,1)S(1)}, bf16[32,512]{1,0:T(8,128)(2,1)}, u32[]{:S(2)}) copy-start(bf16[32,512]{1,0:T(8,128)(2,1)} %copy-done.12) | copy-start | bytes 98308
  241.0 14.8 %copy-start.17 = (bf16[32,512]{1,0:T(8,128)(2,1)S(1)}, bf16[32,512]{1,0:T(8,128)(2,1)}, u32[]{:S(2)}) copy-start(bf16[32,512]{1,0:T(8,128)(2,1)} %copy-done.16) | copy-start | bytes 98308
  241.0 14.8 %copy-start.35 = (bf16[32,32]{0,1:T(8,128)(2,1)S(1)}, bf16[32,32]{0,1:T(8,128)(2,1)}, u32[]{:S(2)}) copy-start(bf16[32,32]{0,1:T(8,128)(2,1)} %copy.428) | copy-start | bytes 6148
  246.8 28.9 %all-to-all-start.10 = ((bf16[32,176,128]{2,1,0:T(8,128)(2,1)}), bf16[32,176,128]{2,1,0:T(8,128)(2,1)}, u32[]{:S(2)}, u32[]{:S(2)}) async-start(bf16[32,176,128]{2,1,0:T(8,128)(2,1)} %pad_maximum_fusion.2), calls=%async_computation.10 | async-start | bytes 2883584 | tf_op jit(solution)/shard_map/all_to_all | solution.py:22
  255.3 22.6 %collective-permute-start.3 = (bf16[16,176,128]{2,1,0:T(8,128)(2,1)}, bf16[16,176,128]{2,1,0:T(8,128)(2,1)}, u32[]{:S(2)}, u32[]{:S(2)}) collective-permute-start(bf16[16,176,128]{2,1,0:T(8,128)(2,1)} %all-to-all-done.9), channel_id=1, source_target_pairs={{0,1},{1,0},{2,3},{3,2},{4,5},{5,4},{6,7},{7,6},{8,9},{9,8},{10,11... | collective-permute-start | bytes 2162696 | tf_op jit(solution)/shard_map/ppermute | solution.py:29
  281.2 16.1 %copy-start.6 = (f32[32,512]{1,0:T(8,128)S(1)}, f32[32,512]{1,0:T(8,128)}, u32[]{:S(2)}) copy-start(f32[32,512]{1,0:T(8,128)} %get-tuple-element.26) | copy-start | bytes 196612
  281.2 13.7 %all-to-all-start.11 = ((f32[8,32,128]{2,1,0:T(8,128)}), f32[8,32,128]{2,1,0:T(8,128)}, u32[]{:S(2)}, u32[]{:S(2)}) async-start(f32[8,32,128]{2,1,0:T(8,128)} %select_maximum_fusion.1), calls=%async_computation.11 | async-start | bytes 262144 | tf_op jit(solution)/shard_map/all_to_all | solution.py:18
  303.3 6.3 %copy-start.11 = (bf16[32,512]{1,0:T(8,128)(2,1)S(1)}, bf16[32,512]{1,0:T(8,128)(2,1)}, u32[]{:S(2)}) copy-start(bf16[32,512]{1,0:T(8,128)(2,1)} %copy-done.10) | copy-start | bytes 98308
  303.3 6.5 %copy-start.19 = (bf16[32,512]{1,0:T(8,128)(2,1)S(1)}, bf16[32,512]{1,0:T(8,128)(2,1)}, u32[]{:S(2)}) copy-start(bf16[32,512]{1,0:T(8,128)(2,1)} %copy-done.18) | copy-start | bytes 98308
  303.3 6.5 %copy-start.32 = (bf16[32,32]{1,0:T(8,128)(2,1)S(1)}, bf16[32,32]{1,0:T(8,128)(2,1)}, u32[]{:S(2)}) copy-start(bf16[32,32]{1,0:T(8,128)(2,1)} %copy-done.31) | copy-start | bytes 6148
  303.3 6.6 %copy-start.21 = (bf16[32,512]{1,0:T(8,128)(2,1)S(1)}, bf16[32,512]{1,0:T(8,128)(2,1)}, u32[]{:S(2)}) copy-start(bf16[32,512]{1,0:T(8,128)(2,1)} %copy-done.20) | copy-start | bytes 98308
  303.3 6.6 %copy-start.30 = (bf16[32,32]{1,0:T(8,128)(2,1)S(1)}, bf16[32,32]{1,0:T(8,128)(2,1)}, u32[]{:S(2)}) copy-start(bf16[32,32]{1,0:T(8,128)(2,1)} %copy-done.29) | copy-start | bytes 6148
  303.3 7.4 %copy-start.50 = (pred[96,2,11]{0,2,1:T(8,128)(4,1)S(1)}, pred[96,2,11]{0,2,1:T(8,128)(4,1)}, u32[]{:S(2)}) copy-start(pred[96,2,11]{0,2,1:T(8,128)(4,1)} %copy-done.47) | copy-start | bytes 6340
  303.4 7.4 %copy-start.54 = (pred[96,2,16]{0,2,1:T(8,128)(4,1)S(1)}, pred[96,2,16]{0,2,1:T(8,128)(4,1)}, u32[]{:S(2)}) copy-start(pred[96,2,16]{0,2,1:T(8,128)(4,1)} %copy-done.51) | copy-start | bytes 9220
  303.4 26.6 %all-to-all-start.12 = ((bf16[32,176,128]{2,1,0:T(8,128)(2,1)}), bf16[32,176,128]{2,1,0:T(8,128)(2,1)}, u32[]{:S(2)}, u32[]{:S(2)}) async-start(bf16[32,176,128]{2,1,0:T(8,128)(2,1)} %pad_maximum_fusion.3), calls=%async_computation.12 | async-start | bytes 2883584 | tf_op jit(solution)/shard_map/all_to_all | solution.py:22
  313.9 22.2 %copy-start.15 = (bf16[32,512]{1,0:T(8,128)(2,1)S(1)}, bf16[32,512]{1,0:T(8,128)(2,1)}, u32[]{:S(2)}) copy-start(bf16[32,512]{1,0:T(8,128)(2,1)} %copy-done.14) | copy-start | bytes 98308
  314.0 22.2 %copy-start.26 = (f32[32,512]{1,0:T(8,128)S(1)}, f32[32,512]{1,0:T(8,128)}, u32[]{:S(2)}) copy-start(f32[32,512]{1,0:T(8,128)} %convolution_add_fusion.2) | copy-start | bytes 196612
  314.0 22.2 %copy-start.34 = (bf16[32,32]{0,1:T(8,128)(2,1)S(1)}, bf16[32,32]{0,1:T(8,128)(2,1)}, u32[]{:S(2)}) copy-start(bf16[32,32]{0,1:T(8,128)(2,1)} %copy-done.33) | copy-start | bytes 6148
  314.0 22.3 %copy-start.28 = (bf16[32,32]{1,0:T(8,128)(2,1)S(1)}, bf16[32,32]{1,0:T(8,128)(2,1)}, u32[]{:S(2)}) copy-start(bf16[32,32]{1,0:T(8,128)(2,1)} %copy-done.27) | copy-start | bytes 6148
  314.7 31.0 %copy-start.25 = (bf16[32,512]{1,0:T(8,128)(2,1)S(1)}, bf16[32,512]{1,0:T(8,128)(2,1)}, u32[]{:S(2)}) copy-start(bf16[32,512]{1,0:T(8,128)(2,1)} %copy-done.24) | copy-start | bytes 98308
  332.7 12.9 %all-to-all-start.13 = ((f32[8,32,128]{2,1,0:T(8,128)}), f32[8,32,128]{2,1,0:T(8,128)S(1)}, u32[]{:S(2)}, u32[]{:S(2)}) async-start(f32[8,32,128]{2,1,0:T(8,128)} %select_maximum_fusion), calls=%async_computation.13 | async-start | bytes 262144 | tf_op jit(solution)/shard_map/all_to_all | solution.py:18
  (25 other events, 47.9 us)

commit v3 on v2

--- a/solution.py
+++ b/solution.py
@@ -87,6 +87,7 @@
     ).astype(jnp.bfloat16)
     border_to_row = (chosen[:, None] == jnp.arange(own_rows, dtype=jnp.int32)[None, :]).astype(jnp.float32)
     row_to_border = border_to_row.T.astype(jnp.bfloat16).reshape(own_rows, groups, sent)
+    border_split = jnp.eye(bound_cols, dtype=jnp.float32).reshape(bound_cols, groups, sent)
     polarity = (2 * excitatory - 1).astype(jnp.float32)
     drive_f = drive.astype(jnp.float32)
 
@@ -152,10 +153,10 @@
         pair_sums = everything[tile_rows:].reshape(batch_rows, 2 * rank)
         group_coeff = pair_sums[:, :rank] + pair_sums[:, rank:]
         own_part = jnp.moveaxis(summed[:own_tiles], 0, 1).reshape(batch_rows, own_rows)
-        border = summed[own_tiles:].reshape(batch_rows, groups, sent)
-        chunks = jnp.concatenate(
-            [jnp.moveaxis(border, 1, 0), jnp.broadcast_to(group_coeff, (groups, batch_rows, rank))], axis=2
-        )
+        border = jnp.einsum(
+            "bc,cgk->gbk", summed[own_tiles], border_split, precision=lax.Precision.HIGHEST
+        )
+        chunks = jnp.concatenate([border, jnp.broadcast_to(group_coeff, (groups, batch_rows, rank))], axis=2)
         return own_part, chunks
 
     def adjoint_end(adjoint, own_part, back, rates):

time: 350 us -> 351 us (level)
    all_to_all x6, waiting for transfers between devices: 42 us -> 37.6 us  [from_each_region(): return lax.all_to_all(padded, 'region', 0, 0, tiled=True)[..., :width]]
where the time goes in v3:
time: 351 us; the launch traced here: 347 us
  waiting for transfers between devices  120 us (34%)
  starting transfers between devices  75.7 us (22%)
  matrix products  47.2 us (13%)
  local copies, waits for them, and re-layouts  38.9 us (11%)
  other arithmetic  33 us (9%)
  blocking collectives  30.4 us (9%)
    all_to_all x4, waiting for transfers between devices, from_each_lane(): return lax.all_to_all(slots, ROW, 0, 0, tiled=True)  69.2 us
    all_to_all x6, waiting for transfers between devices, from_each_region(): return lax.all_to_all(padded, 'region', 0, 0, tiled=True)[..., :width]  37.6 us
    all_to_all x4, starting transfers between devices, from_each_lane(): return lax.all_to_all(slots, ROW, 0, 0, tiled=True)  30.5 us
    all_to_all x2, blocking collectives, from_every_lane(): mine = lax.all_to_all(copies, chips, 0, 0, tiled=True)  30.4 us
    all_to_all x6, starting transfers between devices, from_each_region(): return lax.all_to_all(padded, 'region', 0, 0, tiled=True)[..., :width]  28.5 us
    all_to_all x2, waiting for transfers between devices, from_every_lane(): mine = lax.all_to_all(copies, chips, 0, 0, tiled=True)  11.8 us
    all_to_all x2, starting transfers between devices, from_every_lane(): mine = lax.all_to_all(copies, chips, 0, 0, tiled=True)  11.2 us
    another operation x8, local copies, waits for them, and re-layouts, from_every_lane(): return jnp.stack([mine, sibling])  10.8 us
  transfers between devices with their start and end apart: 16, of which 13 were waited for; matrix products, arithmetic and copies ran while one was open for 13% of the time, Pallas kernels for 0%

profile of v3, /device:TPU:9, one launch (start us, length us, event | category | flops | bytes accessed | tf_op | source)
XLA Modules:
  0.0 347.2 jit_solution(10946314775303632258)
XLA Ops:
  5.2 8.2 %all-to-all-start = ((f32[8,32,128]{2,1,0:T(8,128)}), f32[8,32,128]{2,1,0:T(8,128)S(1)}, u32[]{:S(2)}, u32[]{:S(2)}) async-start(f32[8,32,128]{2,1,0:T(8,128)} %select_maximum_fusion.9), calls=%async_computation | async-start | bytes 262144 | tf_op jit(solution)/shard_map/all_to_all | solution.py:18
  16.4 3.3 convolution_convert_fusion.3
  22.7 6.8 %all-to-all-start.1 = ((bf16[16,176,128]{2,1,0:T(8,128)(2,1)}), bf16[16,176,128]{2,1,0:T(8,128)(2,1)}, u32[]{:S(2)}, u32[]{:S(2)}) async-start(bf16[16,176,128]{2,1,0:T(8,128)(2,1)} %broadcast_in_dim.33), calls=%async_computation.1 | async-start | bytes 1441792 | tf_op jit(solution)/shard_map/all_to_all | solution.py:28
  29.7 1.8 copy.221
  32.8 6.0 %all-to-all-done.1 = bf16[16,176,128]{2,1,0:T(8,128)(2,1)} async-done(((bf16[16,176,128]{2,1,0:T(8,128)(2,1)}), bf16[16,176,128]{2,1,0:T(8,128)(2,1)}, u32[]{:S(2)}, u32[]{:S(2)}) %all-to-all-start.1) | async-done | bytes 720928 | tf_op jit(solution)/shard_map/all_to_all | solution.py:28
  38.8 9.8 %all-to-all-start.2 = ((bf16[32,176,128]{2,1,0:T(8,128)(2,1)}), bf16[32,176,128]{2,1,0:T(8,128)(2,1)}, u32[]{:S(2)}, u32[]{:S(2)}) async-start(bf16[32,176,128]{2,1,0:T(8,128)(2,1)} %pad_maximum_fusion), calls=%async_computation.2 | async-start | bytes 2883584 | tf_op jit(solution)/shard_map/all_to_all | solution.py:22
  49.2 2.2 copy.214
  51.4 17.7 %all-to-all-done.2 = bf16[32,176,128]{2,1,0:T(8,128)(2,1)} async-done(((bf16[32,176,128]{2,1,0:T(8,128)(2,1)}), bf16[32,176,128]{2,1,0:T(8,128)(2,1)}, u32[]{:S(2)}, u32[]{:S(2)}) %all-to-all-start.2) | async-done | bytes 1441824 | tf_op jit(solution)/shard_map/all_to_all | solution.py:22
  69.0 1.6 convert_reduce_fusion.3
  73.7 1.7 fusion.8
  75.4 1.8 convolution_bitcast_fusion.13
  80.0 1.6 multiply_convert_fusion.2
  82.8 1.7 select_maximum_fusion.6
  84.6 6.0 %all-to-all-start.3 = ((f32[8,32,128]{2,1,0:T(8,128)}), f32[8,32,128]{2,1,0:T(8,128)S(1)}, u32[]{:S(2)}, u32[]{:S(2)}) async-start(f32[8,32,128]{2,1,0:T(8,128)} %select_maximum_fusion.6), calls=%async_computation.3 | async-start | bytes 262144 | tf_op jit(solution)/shard_map/all_to_all | solution.py:18
  90.5 9.6 %all-to-all-done.3 = f32[8,32,128]{2,1,0:T(8,128)S(1)} async-done(((f32[8,32,128]{2,1,0:T(8,128)}), f32[8,32,128]{2,1,0:T(8,128)S(1)}, u32[]{:S(2)}, u32[]{:S(2)}) %all-to-all-start.3) | async-done | bytes 131104 | tf_op jit(solution)/shard_map/all_to_all | solution.py:18
  101.5 15.0 %all_to_all.70 = bf16[16,176,128]{2,1,0:T(8,128)(2,1)S(1)} all-to-all(bf16[16,176,128]{2,1,0:T(8,128)(2,1)S(1)} %broadcast_in_dim.72), channel_id=1, replica_groups=mesh['region'=8,'row_0'=4,'row_1'=4,'row_2'=2] {'row_0','row_1'}, dimensions={0} | all-to-all | bytes 1441792 | tf_op jit(solution)/shard_map/all_to_all | solution.py:28
  116.4 2.0 collective-permute-start.1
  118.6 1.6 collective-permute-done.1
  121.1 1.8 convolution_bitcast_fusion.10
  129.3 3.5 %all-to-all-start.5 = ((f32[8,32,128]{2,1,0:T(8,128)}), f32[8,32,128]{2,1,0:T(8,128)S(1)}, u32[]{:S(2)}, u32[]{:S(2)}) async-start(f32[8,32,128]{2,1,0:T(8,128)} %select_maximum_fusion.5), calls=%async_computation.5 | async-start | bytes 262144 | tf_op jit(solution)/shard_map/all_to_all | solution.py:18
  133.5 7.7 %all-to-all-done.5 = f32[8,32,128]{2,1,0:T(8,128)S(1)} async-done(((f32[8,32,128]{2,1,0:T(8,128)}), f32[8,32,128]{2,1,0:T(8,128)S(1)}, u32[]{:S(2)}, u32[]{:S(2)}) %all-to-all-start.5) | async-done | bytes 131104 | tf_op jit(solution)/shard_map/all_to_all | solution.py:18
  144.7 15.5 %all_to_all.71 = bf16[16,176,128]{2,1,0:T(8,128)(2,1)} all-to-all(bf16[16,176,128]{2,1,0:T(8,128)(2,1)S(1)} %broadcast_in_dim.74), channel_id=1, replica_groups=mesh['region'=8,'row_0'=4,'row_1'=4,'row_2'=2] {'row_0','row_1'}, dimensions={0} | all-to-all | bytes 1441792 | tf_op jit(solution)/shard_map/all_to_all | solution.py:28
  160.2 2.5 collective-permute-start.2
  167.8 1.8 convolution_bitcast_fusion.8
  174.0 1.7 fusion.133
  176.6 2.2 convolution_convert_fusion.2
  180.6 6.0 %all-to-all-start.7 = ((bf16[32,176,128]{2,1,0:T(8,128)(2,1)}), bf16[32,176,128]{2,1,0:T(8,128)(2,1)}, u32[]{:S(2)}, u32[]{:S(2)}) async-start(bf16[32,176,128]{2,1,0:T(8,128)(2,1)} %pad_maximum_fusion.1), calls=%async_computation.7 | async-start | bytes 2883584 | tf_op jit(solution)/shard_map/all_to_all | solution.py:22
  187.7 19.3 %all-to-all-done.7 = bf16[32,176,128]{2,1,0:T(8,128)(2,1)} async-done(((bf16[32,176,128]{2,1,0:T(8,128)(2,1)}), bf16[32,176,128]{2,1,0:T(8,128)(2,1)}, u32[]{:S(2)}, u32[]{:S(2)}) %all-to-all-start.7) | async-done | bytes 1441824 | tf_op jit(solution)/shard_map/all_to_all | solution.py:22
  213.4 3.4 all-to-all-start.8
  219.1 7.3 %all-to-all-done.8 = f32[8,32,128]{2,1,0:T(8,128)S(1)} async-done(((f32[8,32,128]{2,1,0:T(8,128)}), f32[8,32,128]{2,1,0:T(8,128)S(1)}, u32[]{:S(2)}, u32[]{:S(2)}) %all-to-all-start.8) | async-done | bytes 131104 | tf_op jit(solution)/shard_map/all_to_all | solution.py:18
  227.6 1.7 fusion.134
  232.5 4.4 %all-to-all-start.9 = ((bf16[16,176,128]{2,1,0:T(8,128)(2,1)}), bf16[16,176,128]{2,1,0:T(8,128)(2,1)}, u32[]{:S(2)}, u32[]{:S(2)}) async-start(bf16[16,176,128]{2,1,0:T(8,128)(2,1)} %broadcast_in_dim.78), calls=%async_computation.9 | async-start | bytes 1441792 | tf_op jit(solution)/shard_map/all_to_all | solution.py:28
  237.5 2.2 convolution_convert_fusion.1
  241.5 5.8 %all-to-all-done.9 = bf16[16,176,128]{2,1,0:T(8,128)(2,1)} async-done(((bf16[16,176,128]{2,1,0:T(8,128)(2,1)}), bf16[16,176,128]{2,1,0:T(8,128)(2,1)}, u32[]{:S(2)}, u32[]{:S(2)}) %all-to-all-start.9) | async-done | bytes 720928 | tf_op jit(solution)/shard_map/all_to_all | solution.py:28
  247.3 8.5 %all-to-all-start.10 = ((bf16[32,176,128]{2,1,0:T(8,128)(2,1)}), bf16[32,176,128]{2,1,0:T(8,128)(2,1)}, u32[]{:S(2)}, u32[]{:S(2)}) async-start(bf16[32,176,128]{2,1,0:T(8,128)(2,1)} %pad_maximum_fusion.2), calls=%async_computation.10 | async-start | bytes 2883584 | tf_op jit(solution)/shard_map/all_to_all | solution.py:22
  257.2 2.1 copy.255
  259.3 16.9 %all-to-all-done.10 = bf16[32,176,128]{2,1,0:T(8,128)(2,1)} async-done(((bf16[32,176,128]{2,1,0:T(8,128)(2,1)}), bf16[32,176,128]{2,1,0:T(8,128)(2,1)}, u32[]{:S(2)}, u32[]{:S(2)}) %all-to-all-start.10) | async-done | bytes 1441824 | tf_op jit(solution)/shard_map/all_to_all | solution.py:22
  276.2 1.6 convert_reduce_fusion.1
  278.7 2.2 copy.256
  281.9 4.0 %all-to-all-start.11 = ((f32[8,32,128]{2,1,0:T(8,128)}), f32[8,32,128]{2,1,0:T(8,128)}, u32[]{:S(2)}, u32[]{:S(2)}) async-start(f32[8,32,128]{2,1,0:T(8,128)} %select_maximum_fusion.1), calls=%async_computation.11 | async-start | bytes 262144 | tf_op jit(solution)/shard_map/all_to_all | solution.py:18
  290.8 4.7 %all-to-all-done.11 = f32[8,32,128]{2,1,0:T(8,128)} async-done(((f32[8,32,128]{2,1,0:T(8,128)}), f32[8,32,128]{2,1,0:T(8,128)}, u32[]{:S(2)}, u32[]{:S(2)}) %all-to-all-start.11) | async-done | bytes 131104 | tf_op jit(solution)/shard_map/all_to_all | solution.py:18
  299.8 2.2 convolution_convert_fusion
  303.9 6.2 %all-to-all-start.12 = ((bf16[32,176,128]{2,1,0:T(8,128)(2,1)}), bf16[32,176,128]{2,1,0:T(8,128)(2,1)}, u32[]{:S(2)}, u32[]{:S(2)}) async-start(bf16[32,176,128]{2,1,0:T(8,128)(2,1)} %pad_maximum_fusion.3), calls=%async_computation.12 | async-start | bytes 2883584 | tf_op jit(solution)/shard_map/all_to_all | solution.py:22
  311.3 1.9 fusion.17
  315.3 15.2 %all-to-all-done.12 = bf16[32,176,128]{2,1,0:T(8,128)(2,1)} async-done(((bf16[32,176,128]{2,1,0:T(8,128)(2,1)}), bf16[32,176,128]{2,1,0:T(8,128)(2,1)}, u32[]{:S(2)}, u32[]{:S(2)}) %all-to-all-start.12) | async-done | bytes 1441824 | tf_op jit(solution)/shard_map/all_to_all | solution.py:22
  333.4 3.4 all-to-all-start.13
  336.9 1.6 convolution_add_fusion.3
  338.6 7.7 %all-to-all-done.13 = f32[8,32,128]{2,1,0:T(8,128)S(1)} async-done(((f32[8,32,128]{2,1,0:T(8,128)}), f32[8,32,128]{2,1,0:T(8,128)S(1)}, u32[]{:S(2)}, u32[]{:S(2)}) %all-to-all-start.13) | async-done | bytes 131104 | tf_op jit(solution)/shard_map/all_to_all | solution.py:18
  (318 shorter events, 81.7 us)
Async XLA Ops:
  0.6 15.2 %copy-start = (bf16[4,24,128,128]{3,2,1,0:T(8,128)(2,1)S(1)}, bf16[4,24,128,128]{3,2,1,0:T(8,128)(2,1)}, u32[]{:S(2)}) copy-start(bf16[4,24,128,128]{3,2,1,0:T(8,128)(2,1)} %param.14) | copy-start | bytes 9437188
  5.2 16.0 %all-to-all-start = ((f32[8,32,128]{2,1,0:T(8,128)}), f32[8,32,128]{2,1,0:T(8,128)S(1)}, u32[]{:S(2)}, u32[]{:S(2)}) async-start(f32[8,32,128]{2,1,0:T(8,128)} %select_maximum_fusion.9), calls=%async_computation | async-start | bytes 262144 | tf_op jit(solution)/shard_map/all_to_all | solution.py:18
  21.2 8.3 %copy-start.40 = (bf16[32,32]{1,0:T(8,128)(2,1)S(1)}, bf16[32,32]{1,0:T(8,128)(2,1)}, u32[]{:S(2)}) copy-start(bf16[32,32]{1,0:T(8,128)(2,1)} %get-tuple-element.20) | copy-start | bytes 6148
  22.7 16.1 %all-to-all-start.1 = ((bf16[16,176,128]{2,1,0:T(8,128)(2,1)}), bf16[16,176,128]{2,1,0:T(8,128)(2,1)}, u32[]{:S(2)}, u32[]{:S(2)}) async-start(bf16[16,176,128]{2,1,0:T(8,128)(2,1)} %broadcast_in_dim.33), calls=%async_computation.1 | async-start | bytes 1441792 | tf_op jit(solution)/shard_map/all_to_all | solution.py:28
  38.8 30.2 %all-to-all-start.2 = ((bf16[32,176,128]{2,1,0:T(8,128)(2,1)}), bf16[32,176,128]{2,1,0:T(8,128)(2,1)}, u32[]{:S(2)}, u32[]{:S(2)}) async-start(bf16[32,176,128]{2,1,0:T(8,128)(2,1)} %pad_maximum_fusion), calls=%async_computation.2 | async-start | bytes 2883584 | tf_op jit(solution)/shard_map/all_to_all | solution.py:22
  48.7 25.0 %copy-start.54 = (pred[96,2,11]{0,2,1:T(8,128)(4,1)}, pred[96,2,11]{0,2,1:T(8,128)(4,1)S(1)}, u32[]{:S(2)}) copy-start(pred[96,2,11]{0,2,1:T(8,128)(4,1)S(1)} %iota_compare_fusion.12) | copy-start | bytes 6340
  48.7 25.0 %copy-start.58 = (pred[96,2,16]{0,2,1:T(8,128)(4,1)}, pred[96,2,16]{0,2,1:T(8,128)(4,1)S(1)}, u32[]{:S(2)}) copy-start(pred[96,2,16]{0,2,1:T(8,128)(4,1)S(1)} %broadcast_and_fusion) | copy-start | bytes 9220
  48.7 23.6 %collective-permute-start = (bf16[16,176,128]{2,1,0:T(8,128)(2,1)}, bf16[16,176,128]{2,1,0:T(8,128)(2,1)}, u32[]{:S(2)}, u32[]{:S(2)}) collective-permute-start(bf16[16,176,128]{2,1,0:T(8,128)(2,1)} %all-to-all-done.1), channel_id=1, source_target_pairs={{0,1},{1,0},{2,3},{3,2},{4,5},{5,4},{6,7},{7,6},{8,9},{9,8},{10,11... | collective-permute-start | bytes 2162696 | tf_op jit(solution)/shard_map/ppermute | solution.py:29
  51.4 22.3 %copy-start.48 = (pred[96]{0:T(512)(128)(4,1)S(1)}, pred[96]{0:T(512)(128)(4,1)}, u32[]{:S(2)}) copy-start(pred[96]{0:T(512)(128)(4,1)} %copy-done.47) | copy-start | bytes 292
  70.6 4.8 %copy-start.22 = (f32[176,128]{1,0:T(8,128)}, f32[176,128]{1,0:T(8,128)S(1)}, u32[]{:S(2)}) copy-start(f32[176,128]{1,0:T(8,128)S(1)} %convert_reduce_fusion.3) | copy-start | bytes 270340
  77.2 4.5 %copy-start.39 = (s32[1,1,8,16]{3,2,1,0:T(8,128)S(1)}, s32[1,1,8,16]{3,2,1,0:T(8,128)}, u32[]{:S(2)}) copy-start(s32[1,1,8,16]{3,2,1,0:T(8,128)} %param.17) | copy-start | bytes 1540
  81.6 19.8 %copy-start.14 = (bf16[32,512]{1,0:T(8,128)(2,1)}, bf16[32,512]{1,0:T(8,128)(2,1)S(1)}, u32[]{:S(2)}) copy-start(bf16[32,512]{1,0:T(8,128)(2,1)S(1)} %get-tuple-element.25) | copy-start | bytes 98308
  84.6 15.6 %all-to-all-start.3 = ((f32[8,32,128]{2,1,0:T(8,128)}), f32[8,32,128]{2,1,0:T(8,128)S(1)}, u32[]{:S(2)}, u32[]{:S(2)}) async-start(f32[8,32,128]{2,1,0:T(8,128)} %select_maximum_fusion.6), calls=%async_computation.3 | async-start | bytes 262144 | tf_op jit(solution)/shard_map/all_to_all | solution.py:18
  116.4 3.9 %collective-permute-start.1 = (bf16[16,176,128]{2,1,0:T(8,128)(2,1)S(1)}, bf16[16,176,128]{2,1,0:T(8,128)(2,1)S(1)}, u32[]{:S(2)}, u32[]{:S(2)}) collective-permute-start(bf16[16,176,128]{2,1,0:T(8,128)(2,1)S(1)} %all_to_all.70), channel_id=1, source_target_pairs={{0,1},{1,0},{2,3},{3,2},{4,5},{5,4},{6,7},{7,6},{8,9},{9,8},{10,11... | collective-permute-start | bytes 2162696 | tf_op jit(solution)/shard_map/ppermute | solution.py:29
  125.9 34.3 %copy-start.16 = (bf16[32,512]{1,0:T(8,128)(2,1)}, bf16[32,512]{1,0:T(8,128)(2,1)S(1)}, u32[]{:S(2)}) copy-start(bf16[32,512]{1,0:T(8,128)(2,1)S(1)} %get-tuple-element.27) | copy-start | bytes 98308
  129.3 11.9 %all-to-all-start.5 = ((f32[8,32,128]{2,1,0:T(8,128)}), f32[8,32,128]{2,1,0:T(8,128)S(1)}, u32[]{:S(2)}, u32[]{:S(2)}) async-start(f32[8,32,128]{2,1,0:T(8,128)} %select_maximum_fusion.5), calls=%async_computation.5 | async-start | bytes 262144 | tf_op jit(solution)/shard_map/all_to_all | solution.py:18
  143.6 19.2 %slice-start = ((f32[176,128]{1,0:T(8,128)}), f32[128,128]{1,0:T(8,128)S(1)}, s32[]{:S(2)}) async-start(f32[176,128]{1,0:T(8,128)} %copy-done.22), calls=%async_computation.14 | async-start | bytes 131072 | tf_op jit(solution)/shard_map/slice | solution.py:155
  143.7 19.1 %copy-start.41 = (bf16[32,32]{1,0:T(8,128)(2,1)S(1)}, bf16[32,32]{1,0:T(8,128)(2,1)}, u32[]{:S(2)}) copy-start(bf16[32,32]{1,0:T(8,128)(2,1)} %get-tuple-element.5) | copy-start | bytes 6148
  160.2 5.6 %collective-permute-start.2 = (bf16[16,176,128]{2,1,0:T(8,128)(2,1)}, bf16[16,176,128]{2,1,0:T(8,128)(2,1)}, u32[]{:S(2)}, u32[]{:S(2)}) collective-permute-start(bf16[16,176,128]{2,1,0:T(8,128)(2,1)} %all_to_all.71), channel_id=1, source_target_pairs={{0,1},{1,0},{2,3},{3,2},{4,5},{5,4},{6,7},{7,6},{8,9},{9,8},{10,11... | collective-permute-start | bytes 2162696 | tf_op jit(solution)/shard_map/ppermute | solution.py:29
  169.6 4.4 %copy-start.4 = (bf16[32,512]{1,0:T(8,128)(2,1)S(1)}, bf16[32,512]{1,0:T(8,128)(2,1)}, u32[]{:S(2)}) copy-start(bf16[32,512]{1,0:T(8,128)(2,1)} %param.19) | copy-start | bytes 98308
  173.3 13.6 %copy-start.12 = (bf16[32,512]{1,0:T(8,128)(2,1)}, bf16[32,512]{1,0:T(8,128)(2,1)S(1)}, u32[]{:S(2)}) copy-start(bf16[32,512]{1,0:T(8,128)(2,1)S(1)} %get-tuple-element.31) | copy-start | bytes 98308
  180.6 26.4 %all-to-all-start.7 = ((bf16[32,176,128]{2,1,0:T(8,128)(2,1)}), bf16[32,176,128]{2,1,0:T(8,128)(2,1)}, u32[]{:S(2)}, u32[]{:S(2)}) async-start(bf16[32,176,128]{2,1,0:T(8,128)(2,1)} %pad_maximum_fusion.1), calls=%async_computation.7 | async-start | bytes 2883584 | tf_op jit(solution)/shard_map/all_to_all | solution.py:22
  213.4 12.9 %all-to-all-start.8 = ((f32[8,32,128]{2,1,0:T(8,128)}), f32[8,32,128]{2,1,0:T(8,128)S(1)}, u32[]{:S(2)}, u32[]{:S(2)}) async-start(f32[8,32,128]{2,1,0:T(8,128)} %select_maximum_fusion.2), calls=%async_computation.8 | async-start | bytes 262144 | tf_op jit(solution)/shard_map/all_to_all | solution.py:18
  229.2 8.2 %copy-start.20 = (bf16[32,512]{1,0:T(8,128)(2,1)}, bf16[32,512]{1,0:T(8,128)(2,1)S(1)}, u32[]{:S(2)}) copy-start(bf16[32,512]{1,0:T(8,128)(2,1)S(1)} %get-tuple-element.33) | copy-start | bytes 98308
  232.5 14.8 %all-to-all-start.9 = ((bf16[16,176,128]{2,1,0:T(8,128)(2,1)}), bf16[16,176,128]{2,1,0:T(8,128)(2,1)}, u32[]{:S(2)}, u32[]{:S(2)}) async-start(bf16[16,176,128]{2,1,0:T(8,128)(2,1)} %broadcast_in_dim.78), calls=%async_computation.9 | async-start | bytes 1441792 | tf_op jit(solution)/shard_map/all_to_all | solution.py:28
  241.5 14.8 %copy-start.13 = (bf16[32,512]{1,0:T(8,128)(2,1)S(1)}, bf16[32,512]{1,0:T(8,128)(2,1)}, u32[]{:S(2)}) copy-start(bf16[32,512]{1,0:T(8,128)(2,1)} %copy-done.12) | copy-start | bytes 98308
  241.5 14.8 %copy-start.36 = (bf16[32,32]{0,1:T(8,128)(2,1)S(1)}, bf16[32,32]{0,1:T(8,128)(2,1)}, u32[]{:S(2)}) copy-start(bf16[32,32]{0,1:T(8,128)(2,1)} %copy.298) | copy-start | bytes 6148
  241.5 14.9 %copy-start.17 = (bf16[32,512]{1,0:T(8,128)(2,1)S(1)}, bf16[32,512]{1,0:T(8,128)(2,1)}, u32[]{:S(2)}) copy-start(bf16[32,512]{1,0:T(8,128)(2,1)} %copy-done.16) | copy-start | bytes 98308
  241.5 14.9 %copy-start.38 = (bf16[32,32]{0,1:T(8,128)(2,1)S(1)}, bf16[32,32]{0,1:T(8,128)(2,1)}, u32[]{:S(2)}) copy-start(bf16[32,32]{0,1:T(8,128)(2,1)} %copy-done.37) | copy-start | bytes 6148
  247.3 28.9 %all-to-all-start.10 = ((bf16[32,176,128]{2,1,0:T(8,128)(2,1)}), bf16[32,176,128]{2,1,0:T(8,128)(2,1)}, u32[]{:S(2)}, u32[]{:S(2)}) async-start(bf16[32,176,128]{2,1,0:T(8,128)(2,1)} %pad_maximum_fusion.2), calls=%async_computation.10 | async-start | bytes 2883584 | tf_op jit(solution)/shard_map/all_to_all | solution.py:22
  255.8 22.9 %collective-permute-start.3 = (bf16[16,176,128]{2,1,0:T(8,128)(2,1)}, bf16[16,176,128]{2,1,0:T(8,128)(2,1)}, u32[]{:S(2)}, u32[]{:S(2)}) collective-permute-start(bf16[16,176,128]{2,1,0:T(8,128)(2,1)} %all-to-all-done.9), channel_id=1, source_target_pairs={{0,1},{1,0},{2,3},{3,2},{4,5},{5,4},{6,7},{7,6},{8,9},{9,8},{10,11... | collective-permute-start | bytes 2162696 | tf_op jit(solution)/shard_map/ppermute | solution.py:29
  281.9 13.6 %all-to-all-start.11 = ((f32[8,32,128]{2,1,0:T(8,128)}), f32[8,32,128]{2,1,0:T(8,128)}, u32[]{:S(2)}, u32[]{:S(2)}) async-start(f32[8,32,128]{2,1,0:T(8,128)} %select_maximum_fusion.1), calls=%async_computation.11 | async-start | bytes 262144 | tf_op jit(solution)/shard_map/all_to_all | solution.py:18
  285.9 12.0 %copy-start.6 = (f32[32,512]{1,0:T(8,128)S(1)}, f32[32,512]{1,0:T(8,128)}, u32[]{:S(2)}) copy-start(f32[32,512]{1,0:T(8,128)} %get-tuple-element.26) | copy-start | bytes 196612
  303.8 6.3 %copy-start.11 = (bf16[32,512]{1,0:T(8,128)(2,1)S(1)}, bf16[32,512]{1,0:T(8,128)(2,1)}, u32[]{:S(2)}) copy-start(bf16[32,512]{1,0:T(8,128)(2,1)} %copy-done.10) | copy-start | bytes 98308
  303.8 6.3 %copy-start.27 = (bf16[32,32]{1,0:T(8,128)(2,1)S(1)}, bf16[32,32]{1,0:T(8,128)(2,1)}, u32[]{:S(2)}) copy-start(bf16[32,32]{1,0:T(8,128)(2,1)} %add_reduce_fusion) | copy-start | bytes 6148
  303.8 6.5 %copy-start.19 = (bf16[32,512]{1,0:T(8,128)(2,1)S(1)}, bf16[32,512]{1,0:T(8,128)(2,1)}, u32[]{:S(2)}) copy-start(bf16[32,512]{1,0:T(8,128)(2,1)} %copy-done.18) | copy-start | bytes 98308
  303.8 6.5 %copy-start.33 = (bf16[32,32]{1,0:T(8,128)(2,1)S(1)}, bf16[32,32]{1,0:T(8,128)(2,1)}, u32[]{:S(2)}) copy-start(bf16[32,32]{1,0:T(8,128)(2,1)} %copy-done.32) | copy-start | bytes 6148
  303.8 6.7 %copy-start.21 = (bf16[32,512]{1,0:T(8,128)(2,1)S(1)}, bf16[32,512]{1,0:T(8,128)(2,1)}, u32[]{:S(2)}) copy-start(bf16[32,512]{1,0:T(8,128)(2,1)} %copy-done.20) | copy-start | bytes 98308
  303.8 6.7 %copy-start.31 = (bf16[32,32]{1,0:T(8,128)(2,1)S(1)}, bf16[32,32]{1,0:T(8,128)(2,1)}, u32[]{:S(2)}) copy-start(bf16[32,32]{1,0:T(8,128)(2,1)} %copy-done.30) | copy-start | bytes 6148
  303.9 7.5 %copy-start.57 = (pred[96,2,11]{0,2,1:T(8,128)(4,1)S(1)}, pred[96,2,11]{0,2,1:T(8,128)(4,1)}, u32[]{:S(2)}) copy-start(pred[96,2,11]{0,2,1:T(8,128)(4,1)} %copy-done.54) | copy-start | bytes 6340
  303.9 7.5 %copy-start.61 = (pred[96,2,16]{0,2,1:T(8,128)(4,1)S(1)}, pred[96,2,16]{0,2,1:T(8,128)(4,1)}, u32[]{:S(2)}) copy-start(pred[96,2,16]{0,2,1:T(8,128)(4,1)} %copy-done.58) | copy-start | bytes 9220
  303.9 26.7 %all-to-all-start.12 = ((bf16[32,176,128]{2,1,0:T(8,128)(2,1)}), bf16[32,176,128]{2,1,0:T(8,128)(2,1)}, u32[]{:S(2)}, u32[]{:S(2)}) async-start(bf16[32,176,128]{2,1,0:T(8,128)(2,1)} %pad_maximum_fusion.3), calls=%async_computation.12 | async-start | bytes 2883584 | tf_op jit(solution)/shard_map/all_to_all | solution.py:22
  314.5 22.3 %copy-start.15 = (bf16[32,512]{1,0:T(8,128)(2,1)S(1)}, bf16[32,512]{1,0:T(8,128)(2,1)}, u32[]{:S(2)}) copy-start(bf16[32,512]{1,0:T(8,128)(2,1)} %copy-done.14) | copy-start | bytes 98308
  314.5 22.3 %copy-start.26 = (f32[32,512]{1,0:T(8,128)S(1)}, f32[32,512]{1,0:T(8,128)}, u32[]{:S(2)}) copy-start(f32[32,512]{1,0:T(8,128)} %convolution_add_fusion.2) | copy-start | bytes 196612
  314.5 22.3 %copy-start.35 = (bf16[32,32]{0,1:T(8,128)(2,1)S(1)}, bf16[32,32]{0,1:T(8,128)(2,1)}, u32[]{:S(2)}) copy-start(bf16[32,32]{0,1:T(8,128)(2,1)} %copy-done.34) | copy-start | bytes 6148
  314.5 22.4 %copy-start.29 = (bf16[32,32]{1,0:T(8,128)(2,1)S(1)}, bf16[32,32]{1,0:T(8,128)(2,1)}, u32[]{:S(2)}) copy-start(bf16[32,32]{1,0:T(8,128)(2,1)} %copy-done.28) | copy-start | bytes 6148
  315.3 31.1 %copy-start.25 = (bf16[32,512]{1,0:T(8,128)(2,1)S(1)}, bf16[32,512]{1,0:T(8,128)(2,1)}, u32[]{:S(2)}) copy-start(bf16[32,512]{1,0:T(8,128)(2,1)} %copy-done.24) | copy-start | bytes 98308
  333.4 12.9 %all-to-all-start.13 = ((f32[8,32,128]{2,1,0:T(8,128)}), f32[8,32,128]{2,1,0:T(8,128)S(1)}, u32[]{:S(2)}, u32[]{:S(2)}) async-start(f32[8,32,128]{2,1,0:T(8,128)} %select_maximum_fusion), calls=%async_computation.13 | async-start | bytes 262144 | tf_op jit(solution)/shard_map/all_to_all | solution.py:18
  (31 other events, 68.5 us)

commit v4 on v2

--- a/solution.py
+++ b/solution.py
@@ -34,6 +34,18 @@
     high = x.astype(jnp.bfloat16)
     low = (x - high.astype(jnp.float32)).astype(jnp.bfloat16)
     return jnp.concatenate([high, low], axis=-1)
+
+
+def pair_rows(x):
+    flat = x.reshape(-1, 128)
+    high = flat.astype(jnp.bfloat16)
+    low = (flat - high.astype(jnp.float32)).astype(jnp.bfloat16)
+    return jnp.concatenate([high, low], axis=0)
+
+
+def joined_rows(x, shape):
+    half = x.shape[-2] // 2
+    return (x[..., :half, :].astype(jnp.float32) + x[..., half:, :].astype(jnp.float32)).reshape(*x.shape[:-2], *shape)
 
 
 def joined_pair(x):
@@ -111,15 +123,14 @@
             [
                 jnp.moveaxis(signed.reshape(batch_rows, own_tiles, 128), 1, 0).reshape(-1, 128),
                 incoming.reshape(batch_rows, -1),
-                split_pair(lane_latent).reshape(-1, 128),
+                pair_rows(lane_latent),
             ],
             axis=0,
         )
         return slots
 
     def forward_end(state, gathered):
-        pair_rows = gathered[:, :, tile_rows:].reshape(lanes, batch_rows, 2 * rank)
-        latent = jnp.sum(joined_pair(pair_rows), axis=0)
+        latent = jnp.sum(joined_rows(gathered[:, :, tile_rows:], (batch_rows, rank)), axis=(0, 1))
         stacked = gathered.reshape(*gathered.shape[:2], -1, half_rows, 128)
         blocks = jnp.einsum("shpcm,pcmrk->shrk", picks_fwd, stacked, preferred_element_type=jnp.bfloat16)
         blocks = blocks.reshape(row_tiles, -1, batch_rows, 128)
@@ -141,16 +152,15 @@
         columns = jnp.einsum(
             "lts,bsk->ltbk", picks, spread.reshape(batch_rows, -1, 128), precision=lax.Precision.HIGHEST
         )
-        pair_rows = split_pair(part_coeff).reshape(-1, 128)
-        coeff_rows = jnp.broadcast_to(pair_rows, (lanes, *pair_rows.shape))
+        coeff_pair = pair_rows(part_coeff)
+        coeff_rows = jnp.broadcast_to(coeff_pair, (lanes, *coeff_pair.shape))
         tiles_rows = columns.astype(jnp.bfloat16).reshape(lanes, tile_rows, 128)
         return scaled_b, jnp.concatenate([tiles_rows, coeff_rows], axis=1)
 
     def adjoint_middle(got):
         everything = jnp.sum(got.astype(jnp.float32), axis=0)
         summed = everything[:tile_rows].reshape(per_lane, batch_rows, 128)
-        pair_sums = everything[tile_rows:].reshape(batch_rows, 2 * rank)
-        group_coeff = pair_sums[:, :rank] + pair_sums[:, rank:]
+        group_coeff = joined_rows(everything[tile_rows:], (batch_rows, rank))
         own_part = jnp.moveaxis(summed[:own_tiles], 0, 1).reshape(batch_rows, own_rows)
         border = summed[own_tiles:].reshape(batch_rows, groups, sent)
         chunks = jnp.concatenate(

time: 350 us -> 364 us (1.040)
  local copies, waits for them, and re-layouts: 37.7 us -> 55 us
  waiting for transfers between devices: 122 us -> 116 us
    all_to_all x6, waiting for transfers between devices: 42 us -> 31.8 us  [from_each_region(): return lax.all_to_all(padded, 'region', 0, 0, tiled=True)[..., :width]]
    another operation x4 -> x0, other arithmetic: 5.28 us -> none  [from_every_lane(): return jnp.stack([mine, sibling])]
    all_to_all x2, waiting for transfers between devices: 8.75 us -> 13.9 us  [from_every_lane(): mine = lax.all_to_all(copies, chips, 0, 0, tiled=True)]
    all_to_all x6, starting transfers between devices: 26.3 us -> 30.9 us  [from_each_region(): return lax.all_to_all(padded, 'region', 0, 0, tiled=True)[..., :width]]
  transfers between devices with their start and end apart: 16 -> 16, of which waited for: 13 -> 12; matrix products, arithmetic and copies ran while one was open for 13% -> 15% of each run, Pallas kernels for 0% -> 0%
where the time goes in v4:
time: 364 us; the launch traced here: 360 us
  waiting for transfers between devices  116 us (32%)
  starting transfers between devices  76.8 us (21%)
  local copies, waits for them, and re-layouts  55 us (15%)
  matrix products  47 us (13%)
  other arithmetic  33 us (9%)
  blocking collectives  30.6 us (8%)
    all_to_all x4, waiting for transfers between devices, from_each_lane(): return lax.all_to_all(slots, ROW, 0, 0, tiled=True)  69.3 us
    all_to_all x6, waiting for transfers between devices, from_each_region(): return lax.all_to_all(padded, 'region', 0, 0, tiled=True)[..., :width]  31.8 us
    all_to_all x6, starting transfers between devices, from_each_region(): return lax.all_to_all(padded, 'region', 0, 0, tiled=True)[..., :width]  30.9 us
    all_to_all x2, blocking collectives, from_every_lane(): mine = lax.all_to_all(copies, chips, 0, 0, tiled=True)  30.6 us
    all_to_all x4, starting transfers between devices, from_each_lane(): return lax.all_to_all(slots, ROW, 0, 0, tiled=True)  29.4 us
    all_to_all x2, waiting for transfers between devices, from_every_lane(): mine = lax.all_to_all(copies, chips, 0, 0, tiled=True)  13.9 us
    another operation x8, local copies, waits for them, and re-layouts, from_every_lane(): return jnp.stack([mine, sibling])  13.7 us
    all_to_all x2, starting transfers between devices, from_every_lane(): mine = lax.all_to_all(copies, chips, 0, 0, tiled=True)  11.1 us
  transfers between devices with their start and end apart: 16, of which 12 were waited for; matrix products, arithmetic and copies ran while one was open for 15% of the time, Pallas kernels for 0%

profile of v4, /device:TPU:9, one launch (start us, length us, event | category | flops | bytes accessed | tf_op | source)
XLA Modules:
  0.0 359.8 jit_solution(2920433227829251259)
XLA Ops:
  5.2 8.2 %all-to-all-start = ((f32[8,32,128]{2,1,0:T(8,128)}), f32[8,32,128]{2,1,0:T(8,128)S(1)}, u32[]{:S(2)}, u32[]{:S(2)}) async-start(f32[8,32,128]{2,1,0:T(8,128)} %select_maximum_fusion.9), calls=%async_computation | async-start | bytes 262144 | tf_op jit(solution)/shard_map/all_to_all | solution.py:18
  16.4 3.3 convolution_convert_fusion.3
  19.9 2.9 copy.344
  24.2 6.8 %all-to-all-start.1 = ((bf16[16,176,128]{2,1,0:T(8,128)(2,1)}), bf16[16,176,128]{2,1,0:T(8,128)(2,1)}, u32[]{:S(2)}, u32[]{:S(2)}) async-start(bf16[16,176,128]{2,1,0:T(8,128)(2,1)} %broadcast_in_dim.33), calls=%async_computation.1 | async-start | bytes 1441792 | tf_op jit(solution)/shard_map/all_to_all | solution.py:28
  31.1 2.5 pad_maximum_fusion
  33.7 8.1 %all-to-all-done.1 = bf16[16,176,128]{2,1,0:T(8,128)(2,1)} async-done(((bf16[16,176,128]{2,1,0:T(8,128)(2,1)}), bf16[16,176,128]{2,1,0:T(8,128)(2,1)}, u32[]{:S(2)}, u32[]{:S(2)}) %all-to-all-start.1) | async-done | bytes 720928 | tf_op jit(solution)/shard_map/all_to_all | solution.py:28
  41.8 8.3 %all-to-all-start.2 = ((bf16[32,176,128]{2,1,0:T(8,128)(2,1)}), bf16[32,176,128]{2,1,0:T(8,128)(2,1)}, u32[]{:S(2)}, u32[]{:S(2)}) async-start(bf16[32,176,128]{2,1,0:T(8,128)(2,1)} %pad_maximum_fusion), calls=%async_computation.2 | async-start | bytes 2883584 | tf_op jit(solution)/shard_map/all_to_all | solution.py:22
  50.7 2.2 copy.337
  52.9 17.7 %all-to-all-done.2 = bf16[32,176,128]{2,1,0:T(8,128)(2,1)} async-done(((bf16[32,176,128]{2,1,0:T(8,128)(2,1)}), bf16[32,176,128]{2,1,0:T(8,128)(2,1)}, u32[]{:S(2)}, u32[]{:S(2)}) %all-to-all-start.2) | async-done | bytes 1441824 | tf_op jit(solution)/shard_map/all_to_all | solution.py:22
  75.9 1.7 fusion.8
  82.2 1.7 select_maximum_fusion.6
  83.9 6.6 %all-to-all-start.3 = ((f32[8,32,128]{2,1,0:T(8,128)}), f32[8,32,128]{2,1,0:T(8,128)S(1)}, u32[]{:S(2)}, u32[]{:S(2)}) async-start(f32[8,32,128]{2,1,0:T(8,128)} %select_maximum_fusion.6), calls=%async_computation.3 | async-start | bytes 262144 | tf_op jit(solution)/shard_map/all_to_all | solution.py:18
  91.2 9.0 %all-to-all-done.3 = f32[8,32,128]{2,1,0:T(8,128)S(1)} async-done(((f32[8,32,128]{2,1,0:T(8,128)}), f32[8,32,128]{2,1,0:T(8,128)S(1)}, u32[]{:S(2)}, u32[]{:S(2)}) %all-to-all-start.3) | async-done | bytes 131104 | tf_op jit(solution)/shard_map/all_to_all | solution.py:18
  103.4 15.0 %all_to_all.70 = bf16[16,176,128]{2,1,0:T(8,128)(2,1)S(1)} all-to-all(bf16[16,176,128]{2,1,0:T(8,128)(2,1)S(1)} %broadcast_in_dim.72), channel_id=1, replica_groups=mesh['region'=8,'row_0'=4,'row_1'=4,'row_2'=2] {'row_0','row_1'}, dimensions={0} | all-to-all | bytes 1441792 | tf_op jit(solution)/shard_map/all_to_all | solution.py:28
  118.3 2.0 collective-permute-start.1
  124.5 1.7 fusion.11
  132.3 3.4 all-to-all-start.5
  137.0 6.9 %all-to-all-done.5 = f32[8,32,128]{2,1,0:T(8,128)S(1)} async-done(((f32[8,32,128]{2,1,0:T(8,128)}), f32[8,32,128]{2,1,0:T(8,128)S(1)}, u32[]{:S(2)}, u32[]{:S(2)}) %all-to-all-start.5) | async-done | bytes 131104 | tf_op jit(solution)/shard_map/all_to_all | solution.py:18
  148.6 15.6 %all_to_all.71 = bf16[16,176,128]{2,1,0:T(8,128)(2,1)} all-to-all(bf16[16,176,128]{2,1,0:T(8,128)(2,1)S(1)} %broadcast_in_dim.74), channel_id=1, replica_groups=mesh['region'=8,'row_0'=4,'row_1'=4,'row_2'=2] {'row_0','row_1'}, dimensions={0} | all-to-all | bytes 1441792 | tf_op jit(solution)/shard_map/all_to_all | solution.py:28
  164.2 2.5 collective-permute-start.2
  167.5 1.7 fusion.41
  169.2 2.2 copy.362
  173.7 1.7 fusion.14
  178.5 2.2 convolution_convert_fusion.2
  182.5 6.1 %all-to-all-start.7 = ((bf16[32,176,128]{2,1,0:T(8,128)(2,1)}), bf16[32,176,128]{2,1,0:T(8,128)(2,1)}, u32[]{:S(2)}, u32[]{:S(2)}) async-start(bf16[32,176,128]{2,1,0:T(8,128)(2,1)} %pad_maximum_fusion.1), calls=%async_computation.7 | async-start | bytes 2883584 | tf_op jit(solution)/shard_map/all_to_all | solution.py:22
  191.9 17.1 %all-to-all-done.7 = bf16[32,176,128]{2,1,0:T(8,128)(2,1)} async-done(((bf16[32,176,128]{2,1,0:T(8,128)(2,1)}), bf16[32,176,128]{2,1,0:T(8,128)(2,1)}, u32[]{:S(2)}, u32[]{:S(2)}) %all-to-all-start.7) | async-done | bytes 1441824 | tf_op jit(solution)/shard_map/all_to_all | solution.py:22
  209.0 1.6 convert_reduce_fusion.2
  214.6 1.6 copy.375
  217.7 1.7 select_maximum_fusion.2
  219.4 3.4 all-to-all-start.8
  225.6 6.7 %all-to-all-done.8 = f32[8,32,128]{2,1,0:T(8,128)S(1)} async-done(((f32[8,32,128]{2,1,0:T(8,128)}), f32[8,32,128]{2,1,0:T(8,128)S(1)}, u32[]{:S(2)}, u32[]{:S(2)}) %all-to-all-start.8) | async-done | bytes 131104 | tf_op jit(solution)/shard_map/all_to_all | solution.py:18
  235.6 1.7 fusion.121
  243.4 4.3 %all-to-all-start.9 = ((bf16[16,176,128]{2,1,0:T(8,128)(2,1)}), bf16[16,176,128]{2,1,0:T(8,128)(2,1)}, u32[]{:S(2)}, u32[]{:S(2)}) async-start(bf16[16,176,128]{2,1,0:T(8,128)(2,1)} %broadcast_in_dim.78), calls=%async_computation.9 | async-start | bytes 1441792 | tf_op jit(solution)/shard_map/all_to_all | solution.py:28
  248.4 2.2 convolution_convert_fusion.1
  252.4 5.8 %all-to-all-done.9 = bf16[16,176,128]{2,1,0:T(8,128)(2,1)} async-done(((bf16[16,176,128]{2,1,0:T(8,128)(2,1)}), bf16[16,176,128]{2,1,0:T(8,128)(2,1)}, u32[]{:S(2)}, u32[]{:S(2)}) %all-to-all-start.9) | async-done | bytes 720928 | tf_op jit(solution)/shard_map/all_to_all | solution.py:28
  258.2 8.8 %all-to-all-start.10 = ((bf16[32,176,128]{2,1,0:T(8,128)(2,1)}), bf16[32,176,128]{2,1,0:T(8,128)(2,1)}, u32[]{:S(2)}, u32[]{:S(2)}) async-start(bf16[32,176,128]{2,1,0:T(8,128)(2,1)} %pad_maximum_fusion.2), calls=%async_computation.10 | async-start | bytes 2883584 | tf_op jit(solution)/shard_map/all_to_all | solution.py:22
  268.1 19.3 %all-to-all-done.10 = bf16[32,176,128]{2,1,0:T(8,128)(2,1)} async-done(((bf16[32,176,128]{2,1,0:T(8,128)(2,1)}), bf16[32,176,128]{2,1,0:T(8,128)(2,1)}, u32[]{:S(2)}, u32[]{:S(2)}) %all-to-all-start.10) | async-done | bytes 1441824 | tf_op jit(solution)/shard_map/all_to_all | solution.py:22
  292.1 3.4 all-to-all-start.11
  295.5 1.6 convolution_add_fusion.2
  297.1 2.2 copy.380
  301.4 2.2 copy.381
  310.0 2.2 convolution_convert_fusion
  314.0 6.2 %all-to-all-start.12 = ((bf16[32,176,128]{2,1,0:T(8,128)(2,1)}), bf16[32,176,128]{2,1,0:T(8,128)(2,1)}, u32[]{:S(2)}, u32[]{:S(2)}) async-start(bf16[32,176,128]{2,1,0:T(8,128)(2,1)} %pad_maximum_fusion.3), calls=%async_computation.12 | async-start | bytes 2883584 | tf_op jit(solution)/shard_map/all_to_all | solution.py:22
  321.4 1.9 fusion.17
  325.4 15.3 %all-to-all-done.12 = bf16[32,176,128]{2,1,0:T(8,128)(2,1)} async-done(((bf16[32,176,128]{2,1,0:T(8,128)(2,1)}), bf16[32,176,128]{2,1,0:T(8,128)(2,1)}, u32[]{:S(2)}, u32[]{:S(2)}) %all-to-all-start.12) | async-done | bytes 1441824 | tf_op jit(solution)/shard_map/all_to_all | solution.py:22
  343.3 6.0 %all-to-all-start.13 = ((f32[8,32,128]{2,1,0:T(8,128)}), f32[8,32,128]{2,1,0:T(8,128)S(1)}, u32[]{:S(2)}, u32[]{:S(2)}) async-start(f32[8,32,128]{2,1,0:T(8,128)} %select_maximum_fusion), calls=%async_computation.13 | async-start | bytes 262144 | tf_op jit(solution)/shard_map/all_to_all | solution.py:18
  349.3 1.6 convolution_add_fusion.3
  351.1 7.8 %all-to-all-done.13 = f32[8,32,128]{2,1,0:T(8,128)S(1)} async-done(((f32[8,32,128]{2,1,0:T(8,128)}), f32[8,32,128]{2,1,0:T(8,128)S(1)}, u32[]{:S(2)}, u32[]{:S(2)}) %all-to-all-start.13) | async-done | bytes 131104 | tf_op jit(solution)/shard_map/all_to_all | solution.py:18
  (297 shorter events, 93.5 us)
Async XLA Ops:
  0.6 15.2 %copy-start = (bf16[4,24,128,128]{3,2,1,0:T(8,128)(2,1)S(1)}, bf16[4,24,128,128]{3,2,1,0:T(8,128)(2,1)}, u32[]{:S(2)}) copy-start(bf16[4,24,128,128]{3,2,1,0:T(8,128)(2,1)} %param.14) | copy-start | bytes 9437188
  5.2 17.7 %all-to-all-start = ((f32[8,32,128]{2,1,0:T(8,128)}), f32[8,32,128]{2,1,0:T(8,128)S(1)}, u32[]{:S(2)}, u32[]{:S(2)}) async-start(f32[8,32,128]{2,1,0:T(8,128)} %select_maximum_fusion.9), calls=%async_computation | async-start | bytes 262144 | tf_op jit(solution)/shard_map/all_to_all | solution.py:18
  14.2 61.7 %copy-start.46 = (pred[96]{0:T(512)(128)(4,1)}, pred[96]{0:T(512)(128)(4,1)S(1)}, u32[]{:S(2)}) copy-start(pred[96]{0:T(512)(128)(4,1)S(1)} %lt.39) | copy-start | bytes 292
  14.9 35.2 %copy-start.42 = (s32[96]{0:T(128)}, s32[96]{0:T(128)S(1)}, u32[]{:S(2)}) copy-start(s32[96]{0:T(128)S(1)} %reshape.431) | copy-start | bytes 1156
  15.8 3.9 %copy-start.9 = (bf16[32,512]{1,0:T(8,128)(2,1)}, bf16[32,512]{1,0:T(8,128)(2,1)S(1)}, u32[]{:S(2)}) copy-start(bf16[32,512]{1,0:T(8,128)(2,1)S(1)} %multiply_convert_fusion.4) | copy-start | bytes 98308
  16.4 3.3 copy-start.2
  24.2 17.6 %all-to-all-start.1 = ((bf16[16,176,128]{2,1,0:T(8,128)(2,1)}), bf16[16,176,128]{2,1,0:T(8,128)(2,1)}, u32[]{:S(2)}, u32[]{:S(2)}) async-start(bf16[16,176,128]{2,1,0:T(8,128)(2,1)} %broadcast_in_dim.33), calls=%async_computation.1 | async-start | bytes 1441792 | tf_op jit(solution)/shard_map/all_to_all | solution.py:28
  41.8 28.7 %all-to-all-start.2 = ((bf16[32,176,128]{2,1,0:T(8,128)(2,1)}), bf16[32,176,128]{2,1,0:T(8,128)(2,1)}, u32[]{:S(2)}, u32[]{:S(2)}) async-start(bf16[32,176,128]{2,1,0:T(8,128)(2,1)} %pad_maximum_fusion), calls=%async_computation.2 | async-start | bytes 2883584 | tf_op jit(solution)/shard_map/all_to_all | solution.py:22
  50.2 25.7 %copy-start.51 = (pred[96,2,11]{0,2,1:T(8,128)(4,1)}, pred[96,2,11]{0,2,1:T(8,128)(4,1)S(1)}, u32[]{:S(2)}) copy-start(pred[96,2,11]{0,2,1:T(8,128)(4,1)S(1)} %iota_compare_fusion.7) | copy-start | bytes 6340
  50.2 23.4 %collective-permute-start = (bf16[16,176,128]{2,1,0:T(8,128)(2,1)}, bf16[16,176,128]{2,1,0:T(8,128)(2,1)}, u32[]{:S(2)}, u32[]{:S(2)}) collective-permute-start(bf16[16,176,128]{2,1,0:T(8,128)(2,1)} %all-to-all-done.1), channel_id=1, source_target_pairs={{0,1},{1,0},{2,3},{3,2},{4,5},{5,4},{6,7},{7,6},{8,9},{9,8},{10,11... | collective-permute-start | bytes 2162696 | tf_op jit(solution)/shard_map/ppermute | solution.py:29
  50.7 25.2 %copy-start.55 = (pred[96,2,16]{0,2,1:T(8,128)(4,1)}, pred[96,2,16]{0,2,1:T(8,128)(4,1)S(1)}, u32[]{:S(2)}) copy-start(pred[96,2,16]{0,2,1:T(8,128)(4,1)S(1)} %broadcast_and_fusion) | copy-start | bytes 9220
  74.5 4.3 %copy-start.30 = (bf16[32,32]{1,0:T(8,128)(2,1)}, bf16[32,32]{1,0:T(8,128)(2,1)S(1)}, u32[]{:S(2)}) copy-start(bf16[32,32]{1,0:T(8,128)(2,1)S(1)} %convert_element_type.253) | copy-start | bytes 6148
  79.0 24.4 %copy-start.13 = (bf16[32,512]{1,0:T(8,128)(2,1)}, bf16[32,512]{1,0:T(8,128)(2,1)S(1)}, u32[]{:S(2)}) copy-start(bf16[32,512]{1,0:T(8,128)(2,1)S(1)} %get-tuple-element.25) | copy-start | bytes 98308
  83.9 16.2 %all-to-all-start.3 = ((f32[8,32,128]{2,1,0:T(8,128)}), f32[8,32,128]{2,1,0:T(8,128)S(1)}, u32[]{:S(2)}, u32[]{:S(2)}) async-start(f32[8,32,128]{2,1,0:T(8,128)} %select_maximum_fusion.6), calls=%async_computation.3 | async-start | bytes 262144 | tf_op jit(solution)/shard_map/all_to_all | solution.py:18
  118.3 3.9 %collective-permute-start.1 = (bf16[16,176,128]{2,1,0:T(8,128)(2,1)S(1)}, bf16[16,176,128]{2,1,0:T(8,128)(2,1)S(1)}, u32[]{:S(2)}, u32[]{:S(2)}) collective-permute-start(bf16[16,176,128]{2,1,0:T(8,128)(2,1)S(1)} %all_to_all.70), channel_id=1, source_target_pairs={{0,1},{1,0},{2,3},{3,2},{4,5},{5,4},{6,7},{7,6},{8,9},{9,8},{10,11... | collective-permute-start | bytes 2162696 | tf_op jit(solution)/shard_map/ppermute | solution.py:29
  123.2 4.2 %copy-start.32 = (bf16[32,32]{1,0:T(8,128)(2,1)}, bf16[32,32]{1,0:T(8,128)(2,1)S(1)}, u32[]{:S(2)}) copy-start(bf16[32,32]{1,0:T(8,128)(2,1)S(1)} %convert_element_type.270) | copy-start | bytes 6148
  132.3 11.7 %all-to-all-start.5 = ((f32[8,32,128]{2,1,0:T(8,128)}), f32[8,32,128]{2,1,0:T(8,128)S(1)}, u32[]{:S(2)}, u32[]{:S(2)}) async-start(f32[8,32,128]{2,1,0:T(8,128)} %select_maximum_fusion.5), calls=%async_computation.5 | async-start | bytes 262144 | tf_op jit(solution)/shard_map/all_to_all | solution.py:18
  146.7 20.8 %slice-start = ((f32[176,128]{1,0:T(8,128)}), f32[128,128]{1,0:T(8,128)S(1)}, s32[]{:S(2)}) async-start(f32[176,128]{1,0:T(8,128)} %copy-done.21), calls=%async_computation.14 | async-start | bytes 131072 | tf_op jit(solution)/shard_map/slice | solution.py:164
  164.2 7.2 %collective-permute-start.2 = (bf16[16,176,128]{2,1,0:T(8,128)(2,1)}, bf16[16,176,128]{2,1,0:T(8,128)(2,1)}, u32[]{:S(2)}, u32[]{:S(2)}) collective-permute-start(bf16[16,176,128]{2,1,0:T(8,128)(2,1)} %all_to_all.71), channel_id=1, source_target_pairs={{0,1},{1,0},{2,3},{3,2},{4,5},{5,4},{6,7},{7,6},{8,9},{9,8},{10,11... | collective-permute-start | bytes 2162696 | tf_op jit(solution)/shard_map/ppermute | solution.py:29
  172.4 4.3 %copy-start.34 = (bf16[32,32]{1,0:T(8,128)(2,1)}, bf16[32,32]{1,0:T(8,128)(2,1)S(1)}, u32[]{:S(2)}) copy-start(bf16[32,32]{1,0:T(8,128)(2,1)S(1)} %convert_element_type.280) | copy-start | bytes 6148
  176.8 11.8 %copy-start.11 = (bf16[32,512]{1,0:T(8,128)(2,1)}, bf16[32,512]{1,0:T(8,128)(2,1)S(1)}, u32[]{:S(2)}) copy-start(bf16[32,512]{1,0:T(8,128)(2,1)S(1)} %get-tuple-element.31) | copy-start | bytes 98308
  182.5 6.1 %copy-start.41 = (s32[1,1,8,16]{3,2,1,0:T(8,128)S(1)}, s32[1,1,8,16]{3,2,1,0:T(8,128)}, u32[]{:S(2)}) copy-start(s32[1,1,8,16]{3,2,1,0:T(8,128)} %param.17) | copy-start | bytes 1540
  182.5 26.5 %all-to-all-start.7 = ((bf16[32,176,128]{2,1,0:T(8,128)(2,1)}), bf16[32,176,128]{2,1,0:T(8,128)(2,1)}, u32[]{:S(2)}, u32[]{:S(2)}) async-start(bf16[32,176,128]{2,1,0:T(8,128)(2,1)} %pad_maximum_fusion.1), calls=%async_computation.7 | async-start | bytes 2883584 | tf_op jit(solution)/shard_map/all_to_all | solution.py:22
  219.4 12.9 %all-to-all-start.8 = ((f32[8,32,128]{2,1,0:T(8,128)}), f32[8,32,128]{2,1,0:T(8,128)S(1)}, u32[]{:S(2)}, u32[]{:S(2)}) async-start(f32[8,32,128]{2,1,0:T(8,128)} %select_maximum_fusion.2), calls=%async_computation.8 | async-start | bytes 262144 | tf_op jit(solution)/shard_map/all_to_all | solution.py:18
  241.4 6.3 %copy-start.38 = (f32[32,32]{1,0:T(8,128)S(1)}, f32[32,32]{1,0:T(8,128)}, u32[]{:S(2)}) copy-start(f32[32,32]{1,0:T(8,128)} %fusion.129) | copy-start | bytes 12292
  241.4 6.3 %copy-start.29 = (bf16[32,4,128]{2,1,0:T(4,128)(2,1)S(1)}, bf16[32,4,128]{2,1,0:T(4,128)(2,1)}, u32[]{:S(2)}) copy-start(bf16[32,4,128]{2,1,0:T(4,128)(2,1)} %reshape.466) | copy-start | bytes 98308
  243.4 14.8 %all-to-all-start.9 = ((bf16[16,176,128]{2,1,0:T(8,128)(2,1)}), bf16[16,176,128]{2,1,0:T(8,128)(2,1)}, u32[]{:S(2)}, u32[]{:S(2)}) async-start(bf16[16,176,128]{2,1,0:T(8,128)(2,1)} %broadcast_in_dim.78), calls=%async_computation.9 | async-start | bytes 1441792 | tf_op jit(solution)/shard_map/all_to_all | solution.py:28
  252.4 14.6 %copy-start.12 = (bf16[32,512]{1,0:T(8,128)(2,1)S(1)}, bf16[32,512]{1,0:T(8,128)(2,1)}, u32[]{:S(2)}) copy-start(bf16[32,512]{1,0:T(8,128)(2,1)} %copy-done.11) | copy-start | bytes 98308
  258.2 29.2 %all-to-all-start.10 = ((bf16[32,176,128]{2,1,0:T(8,128)(2,1)}), bf16[32,176,128]{2,1,0:T(8,128)(2,1)}, u32[]{:S(2)}, u32[]{:S(2)}) async-start(bf16[32,176,128]{2,1,0:T(8,128)(2,1)} %pad_maximum_fusion.2), calls=%async_computation.10 | async-start | bytes 2883584 | tf_op jit(solution)/shard_map/all_to_all | solution.py:22
  267.0 28.5 %copy-start.16 = (bf16[32,512]{1,0:T(8,128)(2,1)S(1)}, bf16[32,512]{1,0:T(8,128)(2,1)}, u32[]{:S(2)}) copy-start(bf16[32,512]{1,0:T(8,128)(2,1)} %copy-done.15) | copy-start | bytes 98308
  267.7 27.7 %copy-start.37 = (bf16[32,32]{0,1:T(8,128)(2,1)S(1)}, bf16[32,32]{0,1:T(8,128)(2,1)}, u32[]{:S(2)}) copy-start(bf16[32,32]{0,1:T(8,128)(2,1)} %copy.428) | copy-start | bytes 6148
  267.7 31.5 %collective-permute-start.3 = (bf16[16,176,128]{2,1,0:T(8,128)(2,1)}, bf16[16,176,128]{2,1,0:T(8,128)(2,1)}, u32[]{:S(2)}, u32[]{:S(2)}) collective-permute-start(bf16[16,176,128]{2,1,0:T(8,128)(2,1)} %all-to-all-done.9), channel_id=1, source_target_pairs={{0,1},{1,0},{2,3},{3,2},{4,5},{5,4},{6,7},{7,6},{8,9},{9,8},{10,11... | collective-permute-start | bytes 2162696 | tf_op jit(solution)/shard_map/ppermute | solution.py:29
  292.1 12.9 %all-to-all-start.11 = ((f32[8,32,128]{2,1,0:T(8,128)}), f32[8,32,128]{2,1,0:T(8,128)S(1)}, u32[]{:S(2)}, u32[]{:S(2)}) async-start(f32[8,32,128]{2,1,0:T(8,128)} %select_maximum_fusion.1), calls=%async_computation.11 | async-start | bytes 262144 | tf_op jit(solution)/shard_map/all_to_all | solution.py:18
  299.2 7.8 %slice-start.1 = ((f32[176,128]{1,0:T(8,128)}), f32[128,128]{1,0:T(8,128)S(1)}, s32[]{:S(2)}) async-start(f32[176,128]{1,0:T(8,128)} %copy-done.23), calls=%async_computation.15 | async-start | bytes 131072 | tf_op jit(solution)/shard_map/slice | solution.py:164
  314.0 6.3 %copy-start.10 = (bf16[32,512]{1,0:T(8,128)(2,1)S(1)}, bf16[32,512]{1,0:T(8,128)(2,1)}, u32[]{:S(2)}) copy-start(bf16[32,512]{1,0:T(8,128)(2,1)} %copy-done.9) | copy-start | bytes 98308
  314.0 6.5 %copy-start.18 = (bf16[32,512]{1,0:T(8,128)(2,1)S(1)}, bf16[32,512]{1,0:T(8,128)(2,1)}, u32[]{:S(2)}) copy-start(bf16[32,512]{1,0:T(8,128)(2,1)} %copy-done.17) | copy-start | bytes 98308
  314.0 6.5 %copy-start.35 = (bf16[32,32]{1,0:T(8,128)(2,1)S(1)}, bf16[32,32]{1,0:T(8,128)(2,1)}, u32[]{:S(2)}) copy-start(bf16[32,32]{1,0:T(8,128)(2,1)} %copy-done.34) | copy-start | bytes 6148
  314.0 6.6 %copy-start.20 = (bf16[32,512]{1,0:T(8,128)(2,1)S(1)}, bf16[32,512]{1,0:T(8,128)(2,1)}, u32[]{:S(2)}) copy-start(bf16[32,512]{1,0:T(8,128)(2,1)} %copy-done.19) | copy-start | bytes 98308
  314.0 6.6 %copy-start.33 = (bf16[32,32]{1,0:T(8,128)(2,1)S(1)}, bf16[32,32]{1,0:T(8,128)(2,1)}, u32[]{:S(2)}) copy-start(bf16[32,32]{1,0:T(8,128)(2,1)} %copy-done.32) | copy-start | bytes 6148
  314.0 7.4 %copy-start.54 = (pred[96,2,11]{0,2,1:T(8,128)(4,1)S(1)}, pred[96,2,11]{0,2,1:T(8,128)(4,1)}, u32[]{:S(2)}) copy-start(pred[96,2,11]{0,2,1:T(8,128)(4,1)} %copy-done.51) | copy-start | bytes 6340
  314.0 7.4 %copy-start.58 = (pred[96,2,16]{0,2,1:T(8,128)(4,1)S(1)}, pred[96,2,16]{0,2,1:T(8,128)(4,1)}, u32[]{:S(2)}) copy-start(pred[96,2,16]{0,2,1:T(8,128)(4,1)} %copy-done.55) | copy-start | bytes 9220
  314.0 26.6 %all-to-all-start.12 = ((bf16[32,176,128]{2,1,0:T(8,128)(2,1)}), bf16[32,176,128]{2,1,0:T(8,128)(2,1)}, u32[]{:S(2)}, u32[]{:S(2)}) async-start(bf16[32,176,128]{2,1,0:T(8,128)(2,1)} %pad_maximum_fusion.3), calls=%async_computation.12 | async-start | bytes 2883584 | tf_op jit(solution)/shard_map/all_to_all | solution.py:22
  324.6 24.8 %copy-start.31 = (bf16[32,32]{1,0:T(8,128)(2,1)S(1)}, bf16[32,32]{1,0:T(8,128)(2,1)}, u32[]{:S(2)}) copy-start(bf16[32,32]{1,0:T(8,128)(2,1)} %copy-done.30) | copy-start | bytes 6148
  324.6 26.4 %copy-start.14 = (bf16[32,512]{1,0:T(8,128)(2,1)S(1)}, bf16[32,512]{1,0:T(8,128)(2,1)}, u32[]{:S(2)}) copy-start(bf16[32,512]{1,0:T(8,128)(2,1)} %copy-done.13) | copy-start | bytes 98308
  324.6 26.4 %copy-start.26 = (f32[32,512]{1,0:T(8,128)S(1)}, f32[32,512]{1,0:T(8,128)}, u32[]{:S(2)}) copy-start(f32[32,512]{1,0:T(8,128)} %convolution_add_fusion.2) | copy-start | bytes 196612
  325.4 25.6 %copy-start.36 = (bf16[32,32]{0,1:T(8,128)(2,1)S(1)}, bf16[32,32]{0,1:T(8,128)(2,1)}, u32[]{:S(2)}) copy-start(bf16[32,32]{0,1:T(8,128)(2,1)} %copy.429) | copy-start | bytes 6148
  325.4 33.6 %copy-start.25 = (bf16[32,512]{1,0:T(8,128)(2,1)S(1)}, bf16[32,512]{1,0:T(8,128)(2,1)}, u32[]{:S(2)}) copy-start(bf16[32,512]{1,0:T(8,128)(2,1)} %copy-done.24) | copy-start | bytes 98308
  343.3 15.6 %all-to-all-start.13 = ((f32[8,32,128]{2,1,0:T(8,128)}), f32[8,32,128]{2,1,0:T(8,128)S(1)}, u32[]{:S(2)}, u32[]{:S(2)}) async-start(f32[8,32,128]{2,1,0:T(8,128)} %select_maximum_fusion), calls=%async_computation.13 | async-start | bytes 262144 | tf_op jit(solution)/shard_map/all_to_all | solution.py:18
  (29 other events, 41.6 us)

commit v5 on v2

--- a/solution.py
+++ b/solution.py
@@ -138,8 +138,14 @@
             tile_vals,
             preferred_element_type=jnp.float32,
         )
+        rest = spread.reshape(batch_rows, -1, 128)
+        parts = []
+        for _ in range(3):
+            part = rest.astype(jnp.bfloat16)
+            rest = rest - part.astype(jnp.float32)
+            parts.append(part)
         columns = jnp.einsum(
-            "lts,bsk->ltbk", picks, spread.reshape(batch_rows, -1, 128), precision=lax.Precision.HIGHEST
+            "lts,pbsk->ltbk", picks.astype(jnp.bfloat16), jnp.stack(parts), preferred_element_type=jnp.float32
         )
         pair_rows = split_pair(part_coeff).reshape(-1, 128)
         coeff_rows = jnp.broadcast_to(pair_rows, (lanes, *pair_rows.shape))

time: 350 us -> 357 us (1.020)
  other arithmetic: 32.9 us -> 44.1 us
  matrix products: 48.5 us -> 39.8 us
  local copies, waits for them, and re-layouts: 37.7 us -> 43.7 us
  waiting for transfers between devices: 122 us -> 118 us
    dot_general x4, matrix products: 10.2 us -> 3.36 us  [adjoint_start(): jnp.einsum('lts,pbsk->ltbk', picks.astype(jnp.bfloat16), jnp.stack(parts)...]
    reshape x4, local copies, waits for them, and re-layouts: 2.04 us -> 7.64 us  [adjoint_start(): tiles_rows = columns.astype(jnp.bfloat16).reshape(lanes, tile_rows, 128)]
    concatenate x4, other arithmetic: 4.89 us -> 10.3 us  [adjoint_start(): return (scaled_b, jnp.concatenate([tiles_rows, coeff_rows], axis=1))]
    all_to_all x6, waiting for transfers between devices: 42 us -> 36.8 us  [from_each_region(): return lax.all_to_all(padded, 'region', 0, 0, tiled=True)[..., :width]]
    convert_element_type x0 -> x8, other arithmetic: none -> 3.7 us  [adjoint_start(): part = rest.astype(jnp.bfloat16)]
  transfers between devices with their start and end apart: 16 -> 16, of which waited for: 13 -> 12; matrix products, arithmetic and copies ran while one was open for 13% -> 14% of each run, Pallas kernels for 0% -> 0%
where the time goes in v5:
time: 357 us; the launch traced here: 354 us
  waiting for transfers between devices  118 us (33%)
  starting transfers between devices  75.4 us (21%)
  other arithmetic  44.1 us (12%)
  local copies, waits for them, and re-layouts  43.7 us (12%)
  matrix products  39.8 us (11%)
  blocking collectives  30.4 us (9%)
    all_to_all x4, waiting for transfers between devices, from_each_lane(): return lax.all_to_all(slots, ROW, 0, 0, tiled=True)  69.2 us
    all_to_all x6, waiting for transfers between devices, from_each_region(): return lax.all_to_all(padded, 'region', 0, 0, tiled=True)[..., :width]  36.8 us
    all_to_all x2, blocking collectives, from_every_lane(): mine = lax.all_to_all(copies, chips, 0, 0, tiled=True)  30.4 us
    all_to_all x4, starting transfers between devices, from_each_lane(): return lax.all_to_all(slots, ROW, 0, 0, tiled=True)  29.5 us
    all_to_all x6, starting transfers between devices, from_each_region(): return lax.all_to_all(padded, 'region', 0, 0, tiled=True)[..., :width]  29.3 us
    all_to_all x2, starting transfers between devices, from_every_lane(): mine = lax.all_to_all(copies, chips, 0, 0, tiled=True)  11.3 us
    another operation x8, local copies, waits for them, and re-layouts, from_every_lane(): return jnp.stack([mine, sibling])  10.8 us
    all_to_all x2, waiting for transfers between devices, from_every_lane(): mine = lax.all_to_all(copies, chips, 0, 0, tiled=True)  10.7 us
  transfers between devices with their start and end apart: 16, of which 12 were waited for; matrix products, arithmetic and copies ran while one was open for 14% of the time, Pallas kernels for 0%

profile of v5, /device:TPU:9, one launch (start us, length us, event | category | flops | bytes accessed | tf_op | source)
XLA Modules:
  0.0 353.7 jit_solution(14738562493341407841)
XLA Ops:
  5.2 8.2 %all-to-all-start = ((f32[8,32,128]{2,1,0:T(8,128)}), f32[8,32,128]{2,1,0:T(8,128)S(1)}, u32[]{:S(2)}, u32[]{:S(2)}) async-start(f32[8,32,128]{2,1,0:T(8,128)} %select_maximum_fusion.9), calls=%async_computation | async-start | bytes 262144 | tf_op jit(solution)/shard_map/all_to_all | solution.py:18
  17.2 1.7 convolution_convert_fusion.3
  18.9 2.9 copy.332
  23.4 6.8 %all-to-all-start.1 = ((bf16[16,176,128]{2,1,0:T(8,128)(2,1)}), bf16[16,176,128]{2,1,0:T(8,128)(2,1)}, u32[]{:S(2)}, u32[]{:S(2)}) async-start(bf16[16,176,128]{2,1,0:T(8,128)(2,1)} %broadcast_in_dim.33), calls=%async_computation.1 | async-start | bytes 1441792 | tf_op jit(solution)/shard_map/all_to_all | solution.py:28
  30.6 2.6 pad_maximum_fusion
  33.1 7.3 %all-to-all-done.1 = bf16[16,176,128]{2,1,0:T(8,128)(2,1)} async-done(((bf16[16,176,128]{2,1,0:T(8,128)(2,1)}), bf16[16,176,128]{2,1,0:T(8,128)(2,1)}, u32[]{:S(2)}, u32[]{:S(2)}) %all-to-all-start.1) | async-done | bytes 720928 | tf_op jit(solution)/shard_map/all_to_all | solution.py:28
  40.4 8.8 %all-to-all-start.2 = ((bf16[32,176,128]{2,1,0:T(8,128)(2,1)}), bf16[32,176,128]{2,1,0:T(8,128)(2,1)}, u32[]{:S(2)}, u32[]{:S(2)}) async-start(bf16[32,176,128]{2,1,0:T(8,128)(2,1)} %pad_maximum_fusion), calls=%async_computation.2 | async-start | bytes 2883584 | tf_op jit(solution)/shard_map/all_to_all | solution.py:22
  49.8 2.2 copy.325
  52.0 17.7 %all-to-all-done.2 = bf16[32,176,128]{2,1,0:T(8,128)(2,1)} async-done(((bf16[32,176,128]{2,1,0:T(8,128)(2,1)}), bf16[32,176,128]{2,1,0:T(8,128)(2,1)}, u32[]{:S(2)}, u32[]{:S(2)}) %all-to-all-start.2) | async-done | bytes 1441824 | tf_op jit(solution)/shard_map/all_to_all | solution.py:22
  74.8 1.7 fusion.8
  76.6 1.8 convolution_bitcast_fusion.9
  84.0 1.7 select_maximum_fusion.6
  85.8 6.6 %all-to-all-start.3 = ((f32[8,32,128]{2,1,0:T(8,128)}), f32[8,32,128]{2,1,0:T(8,128)S(1)}, u32[]{:S(2)}, u32[]{:S(2)}) async-start(f32[8,32,128]{2,1,0:T(8,128)} %select_maximum_fusion.6), calls=%async_computation.3 | async-start | bytes 262144 | tf_op jit(solution)/shard_map/all_to_all | solution.py:18
  92.4 9.6 %all-to-all-done.3 = f32[8,32,128]{2,1,0:T(8,128)S(1)} async-done(((f32[8,32,128]{2,1,0:T(8,128)}), f32[8,32,128]{2,1,0:T(8,128)S(1)}, u32[]{:S(2)}, u32[]{:S(2)}) %all-to-all-start.3) | async-done | bytes 131104 | tf_op jit(solution)/shard_map/all_to_all | solution.py:18
  103.3 15.0 %all_to_all.70 = bf16[16,176,128]{2,1,0:T(8,128)(2,1)S(1)} all-to-all(bf16[16,176,128]{2,1,0:T(8,128)(2,1)S(1)} %broadcast_in_dim.72), channel_id=1, replica_groups=mesh['region'=8,'row_0'=4,'row_1'=4,'row_2'=2] {'row_0','row_1'}, dimensions={0} | all-to-all | bytes 1441792 | tf_op jit(solution)/shard_map/all_to_all | solution.py:28
  118.3 2.0 collective-permute-start.1
  120.5 1.6 collective-permute-done.1
  123.0 1.8 convolution_bitcast_fusion.7
  131.2 3.4 all-to-all-start.5
  135.2 7.7 %all-to-all-done.5 = f32[8,32,128]{2,1,0:T(8,128)S(1)} async-done(((f32[8,32,128]{2,1,0:T(8,128)}), f32[8,32,128]{2,1,0:T(8,128)S(1)}, u32[]{:S(2)}, u32[]{:S(2)}) %all-to-all-start.5) | async-done | bytes 131104 | tf_op jit(solution)/shard_map/all_to_all | solution.py:18
  145.8 15.5 %all_to_all.71 = bf16[16,176,128]{2,1,0:T(8,128)(2,1)} all-to-all(bf16[16,176,128]{2,1,0:T(8,128)(2,1)S(1)} %broadcast_in_dim.74), channel_id=1, replica_groups=mesh['region'=8,'row_0'=4,'row_1'=4,'row_2'=2] {'row_0','row_1'}, dimensions={0} | all-to-all | bytes 1441792 | tf_op jit(solution)/shard_map/all_to_all | solution.py:28
  161.3 2.5 collective-permute-start.2
  164.6 1.7 fusion.41
  169.6 1.8 convolution_bitcast_fusion.5
  175.8 1.7 fusion.134
  181.4 2.6 pad_maximum_fusion.1
  184.0 6.0 %all-to-all-start.7 = ((bf16[32,176,128]{2,1,0:T(8,128)(2,1)}), bf16[32,176,128]{2,1,0:T(8,128)(2,1)}, u32[]{:S(2)}, u32[]{:S(2)}) async-start(bf16[32,176,128]{2,1,0:T(8,128)(2,1)} %pad_maximum_fusion.1), calls=%async_computation.7 | async-start | bytes 2883584 | tf_op jit(solution)/shard_map/all_to_all | solution.py:22
  191.0 19.3 %all-to-all-done.7 = bf16[32,176,128]{2,1,0:T(8,128)(2,1)} async-done(((bf16[32,176,128]{2,1,0:T(8,128)(2,1)}), bf16[32,176,128]{2,1,0:T(8,128)(2,1)}, u32[]{:S(2)}, u32[]{:S(2)}) %all-to-all-start.7) | async-done | bytes 1441824 | tf_op jit(solution)/shard_map/all_to_all | solution.py:22
  218.0 3.4 all-to-all-start.8
  223.6 7.3 %all-to-all-done.8 = f32[8,32,128]{2,1,0:T(8,128)S(1)} async-done(((f32[8,32,128]{2,1,0:T(8,128)}), f32[8,32,128]{2,1,0:T(8,128)S(1)}, u32[]{:S(2)}, u32[]{:S(2)}) %all-to-all-start.8) | async-done | bytes 131104 | tf_op jit(solution)/shard_map/all_to_all | solution.py:18
  233.4 1.7 fusion.135
  239.6 4.4 %all-to-all-start.9 = ((bf16[16,176,128]{2,1,0:T(8,128)(2,1)}), bf16[16,176,128]{2,1,0:T(8,128)(2,1)}, u32[]{:S(2)}, u32[]{:S(2)}) async-start(bf16[16,176,128]{2,1,0:T(8,128)(2,1)} %broadcast_in_dim.78), calls=%async_computation.9 | async-start | bytes 1441792 | tf_op jit(solution)/shard_map/all_to_all | solution.py:28
  244.0 2.0 convert_reduce_fusion.1
  248.5 2.6 pad_maximum_fusion.2
  251.1 3.4 all-to-all-done.9
  254.6 8.5 %all-to-all-start.10 = ((bf16[32,176,128]{2,1,0:T(8,128)(2,1)}), bf16[32,176,128]{2,1,0:T(8,128)(2,1)}, u32[]{:S(2)}, u32[]{:S(2)}) async-start(bf16[32,176,128]{2,1,0:T(8,128)(2,1)} %pad_maximum_fusion.2), calls=%async_computation.10 | async-start | bytes 2883584 | tf_op jit(solution)/shard_map/all_to_all | solution.py:22
  264.3 2.2 copy.368
  266.5 17.0 %all-to-all-done.10 = bf16[32,176,128]{2,1,0:T(8,128)(2,1)} async-done(((bf16[32,176,128]{2,1,0:T(8,128)(2,1)}), bf16[32,176,128]{2,1,0:T(8,128)(2,1)}, u32[]{:S(2)}, u32[]{:S(2)}) %all-to-all-start.10) | async-done | bytes 1441824 | tf_op jit(solution)/shard_map/all_to_all | solution.py:22
  286.8 4.3 %all-to-all-start.11 = ((f32[8,32,128]{2,1,0:T(8,128)}), f32[8,32,128]{2,1,0:T(8,128)}, u32[]{:S(2)}, u32[]{:S(2)}) async-start(f32[8,32,128]{2,1,0:T(8,128)} %select_maximum_fusion.1), calls=%async_computation.11 | async-start | bytes 262144 | tf_op jit(solution)/shard_map/all_to_all | solution.py:18
  293.8 2.2 copy.369
  296.1 4.5 %all-to-all-done.11 = f32[8,32,128]{2,1,0:T(8,128)} async-done(((f32[8,32,128]{2,1,0:T(8,128)}), f32[8,32,128]{2,1,0:T(8,128)}, u32[]{:S(2)}, u32[]{:S(2)}) %all-to-all-start.11) | async-done | bytes 131104 | tf_op jit(solution)/shard_map/all_to_all | solution.py:18
  308.0 2.6 pad_maximum_fusion.3
  310.5 6.2 %all-to-all-start.12 = ((bf16[32,176,128]{2,1,0:T(8,128)(2,1)}), bf16[32,176,128]{2,1,0:T(8,128)(2,1)}, u32[]{:S(2)}, u32[]{:S(2)}) async-start(bf16[32,176,128]{2,1,0:T(8,128)(2,1)} %pad_maximum_fusion.3), calls=%async_computation.12 | async-start | bytes 2883584 | tf_op jit(solution)/shard_map/all_to_all | solution.py:22
  318.0 2.0 fusion.17
  321.9 15.3 %all-to-all-done.12 = bf16[32,176,128]{2,1,0:T(8,128)(2,1)} async-done(((bf16[32,176,128]{2,1,0:T(8,128)(2,1)}), bf16[32,176,128]{2,1,0:T(8,128)(2,1)}, u32[]{:S(2)}, u32[]{:S(2)}) %all-to-all-start.12) | async-done | bytes 1441824 | tf_op jit(solution)/shard_map/all_to_all | solution.py:22
  339.9 3.4 all-to-all-start.13
  343.4 1.6 convolution_add_fusion.3
  345.1 7.7 %all-to-all-done.13 = f32[8,32,128]{2,1,0:T(8,128)S(1)} async-done(((f32[8,32,128]{2,1,0:T(8,128)}), f32[8,32,128]{2,1,0:T(8,128)S(1)}, u32[]{:S(2)}, u32[]{:S(2)}) %all-to-all-start.13) | async-done | bytes 131104 | tf_op jit(solution)/shard_map/all_to_all | solution.py:18
  (322 shorter events, 87.5 us)
Async XLA Ops:
  0.6 15.2 %copy-start = (bf16[4,24,128,128]{3,2,1,0:T(8,128)(2,1)S(1)}, bf16[4,24,128,128]{3,2,1,0:T(8,128)(2,1)}, u32[]{:S(2)}) copy-start(bf16[4,24,128,128]{3,2,1,0:T(8,128)(2,1)} %param.14) | copy-start | bytes 9437188
  2.5 13.9 %copy-start.24 = (bf16[32,512]{1,0:T(8,128)(2,1)}, bf16[32,512]{1,0:T(8,128)(2,1)S(1)}, u32[]{:S(2)}) copy-start(bf16[32,512]{1,0:T(8,128)(2,1)S(1)} %multiply_convert_fusion.3) | copy-start | bytes 98308
  5.2 16.6 %all-to-all-start = ((f32[8,32,128]{2,1,0:T(8,128)}), f32[8,32,128]{2,1,0:T(8,128)S(1)}, u32[]{:S(2)}, u32[]{:S(2)}) async-start(f32[8,32,128]{2,1,0:T(8,128)} %select_maximum_fusion.9), calls=%async_computation | async-start | bytes 262144 | tf_op jit(solution)/shard_map/all_to_all | solution.py:18
  14.1 35.1 %copy-start.40 = (s32[96]{0:T(128)}, s32[96]{0:T(128)S(1)}, u32[]{:S(2)}) copy-start(s32[96]{0:T(128)S(1)} %reshape.604) | copy-start | bytes 1156
  15.8 14.4 %copy-start.10 = (bf16[32,512]{1,0:T(8,128)(2,1)}, bf16[32,512]{1,0:T(8,128)(2,1)S(1)}, u32[]{:S(2)}) copy-start(bf16[32,512]{1,0:T(8,128)(2,1)S(1)} %multiply_convert_fusion.4) | copy-start | bytes 98308
  18.9 11.3 %copy-start.1 = (bf16[32,512]{1,0:T(8,128)(2,1)S(1)}, bf16[32,512]{1,0:T(8,128)(2,1)}, u32[]{:S(2)}) copy-start(bf16[32,512]{1,0:T(8,128)(2,1)} %param.18) | copy-start | bytes 98308
  23.4 17.1 %all-to-all-start.1 = ((bf16[16,176,128]{2,1,0:T(8,128)(2,1)}), bf16[16,176,128]{2,1,0:T(8,128)(2,1)}, u32[]{:S(2)}, u32[]{:S(2)}) async-start(bf16[16,176,128]{2,1,0:T(8,128)(2,1)} %broadcast_in_dim.33), calls=%async_computation.1 | async-start | bytes 1441792 | tf_op jit(solution)/shard_map/all_to_all | solution.py:28
  40.4 29.2 %all-to-all-start.2 = ((bf16[32,176,128]{2,1,0:T(8,128)(2,1)}), bf16[32,176,128]{2,1,0:T(8,128)(2,1)}, u32[]{:S(2)}, u32[]{:S(2)}) async-start(bf16[32,176,128]{2,1,0:T(8,128)(2,1)} %pad_maximum_fusion), calls=%async_computation.2 | async-start | bytes 2883584 | tf_op jit(solution)/shard_map/all_to_all | solution.py:22
  49.4 25.5 %copy-start.50 = (pred[96,2,11]{0,2,1:T(8,128)(4,1)}, pred[96,2,11]{0,2,1:T(8,128)(4,1)S(1)}, u32[]{:S(2)}) copy-start(pred[96,2,11]{0,2,1:T(8,128)(4,1)S(1)} %iota_compare_fusion.7) | copy-start | bytes 6340
  49.4 24.2 %collective-permute-start = (bf16[16,176,128]{2,1,0:T(8,128)(2,1)}, bf16[16,176,128]{2,1,0:T(8,128)(2,1)}, u32[]{:S(2)}, u32[]{:S(2)}) collective-permute-start(bf16[16,176,128]{2,1,0:T(8,128)(2,1)} %all-to-all-done.1), channel_id=1, source_target_pairs={{0,1},{1,0},{2,3},{3,2},{4,5},{5,4},{6,7},{7,6},{8,9},{9,8},{10,11... | collective-permute-start | bytes 2162696 | tf_op jit(solution)/shard_map/ppermute | solution.py:29
  49.8 25.0 %copy-start.54 = (pred[96,2,16]{0,2,1:T(8,128)(4,1)}, pred[96,2,16]{0,2,1:T(8,128)(4,1)S(1)}, u32[]{:S(2)}) copy-start(pred[96,2,16]{0,2,1:T(8,128)(4,1)S(1)} %broadcast_and_fusion) | copy-start | bytes 9220
  49.8 25.0 %copy-start.45 = (pred[96]{0:T(512)(128)(4,1)S(1)}, pred[96]{0:T(512)(128)(4,1)}, u32[]{:S(2)}) copy-start(pred[96]{0:T(512)(128)(4,1)} %copy-done.44) | copy-start | bytes 292
  82.8 35.5 %copy-start.14 = (bf16[32,512]{1,0:T(8,128)(2,1)}, bf16[32,512]{1,0:T(8,128)(2,1)S(1)}, u32[]{:S(2)}) copy-start(bf16[32,512]{1,0:T(8,128)(2,1)S(1)} %get-tuple-element.33) | copy-start | bytes 98308
  85.8 16.2 %all-to-all-start.3 = ((f32[8,32,128]{2,1,0:T(8,128)}), f32[8,32,128]{2,1,0:T(8,128)S(1)}, u32[]{:S(2)}, u32[]{:S(2)}) async-start(f32[8,32,128]{2,1,0:T(8,128)} %select_maximum_fusion.6), calls=%async_computation.3 | async-start | bytes 262144 | tf_op jit(solution)/shard_map/all_to_all | solution.py:18
  103.2 19.1 %copy-start.51 = (pred[96,2,11]{0,2,1:T(8,128)(4,1)S(1)}, pred[96,2,11]{0,2,1:T(8,128)(4,1)}, u32[]{:S(2)}) copy-start(pred[96,2,11]{0,2,1:T(8,128)(4,1)} %copy-done.50) | copy-start | bytes 6340
  103.2 19.1 %copy-start.55 = (pred[96,2,16]{0,2,1:T(8,128)(4,1)S(1)}, pred[96,2,16]{0,2,1:T(8,128)(4,1)}, u32[]{:S(2)}) copy-start(pred[96,2,16]{0,2,1:T(8,128)(4,1)} %copy-done.54) | copy-start | bytes 9220
  118.3 3.9 %collective-permute-start.1 = (bf16[16,176,128]{2,1,0:T(8,128)(2,1)S(1)}, bf16[16,176,128]{2,1,0:T(8,128)(2,1)S(1)}, u32[]{:S(2)}, u32[]{:S(2)}) collective-permute-start(bf16[16,176,128]{2,1,0:T(8,128)(2,1)S(1)} %all_to_all.70), channel_id=1, source_target_pairs={{0,1},{1,0},{2,3},{3,2},{4,5},{5,4},{6,7},{7,6},{8,9},{9,8},{10,11... | collective-permute-start | bytes 2162696 | tf_op jit(solution)/shard_map/ppermute | solution.py:29
  127.7 39.9 %copy-start.16 = (bf16[32,512]{1,0:T(8,128)(2,1)}, bf16[32,512]{1,0:T(8,128)(2,1)S(1)}, u32[]{:S(2)}) copy-start(bf16[32,512]{1,0:T(8,128)(2,1)S(1)} %get-tuple-element.35) | copy-start | bytes 98308
  131.2 11.7 %all-to-all-start.5 = ((f32[8,32,128]{2,1,0:T(8,128)}), f32[8,32,128]{2,1,0:T(8,128)S(1)}, u32[]{:S(2)}, u32[]{:S(2)}) async-start(f32[8,32,128]{2,1,0:T(8,128)} %select_maximum_fusion.5), calls=%async_computation.5 | async-start | bytes 262144 | tf_op jit(solution)/shard_map/all_to_all | solution.py:18
  144.7 19.9 %slice-start = ((f32[176,128]{1,0:T(8,128)}), f32[128,128]{1,0:T(8,128)S(1)}, s32[]{:S(2)}) async-start(f32[176,128]{1,0:T(8,128)} %copy-done.22), calls=%async_computation.14 | async-start | bytes 131072 | tf_op jit(solution)/shard_map/slice | solution.py:160
  145.8 23.1 %copy-start.46 = (pred[96]{0:T(512)(128)(4,1)S(1)}, pred[96]{0:T(512)(128)(4,1)}, u32[]{:S(2)}) copy-start(pred[96]{0:T(512)(128)(4,1)} %copy-done.44) | copy-start | bytes 292
  145.8 23.1 %copy-start.52 = (pred[96,2,11]{0,2,1:T(8,128)(4,1)S(1)}, pred[96,2,11]{0,2,1:T(8,128)(4,1)}, u32[]{:S(2)}) copy-start(pred[96,2,11]{0,2,1:T(8,128)(4,1)} %copy-done.50) | copy-start | bytes 6340
  145.8 23.1 %copy-start.56 = (pred[96,2,16]{0,2,1:T(8,128)(4,1)S(1)}, pred[96,2,16]{0,2,1:T(8,128)(4,1)}, u32[]{:S(2)}) copy-start(pred[96,2,16]{0,2,1:T(8,128)(4,1)} %copy-done.54) | copy-start | bytes 9220
  161.3 6.3 %collective-permute-start.2 = (bf16[16,176,128]{2,1,0:T(8,128)(2,1)}, bf16[16,176,128]{2,1,0:T(8,128)(2,1)}, u32[]{:S(2)}, u32[]{:S(2)}) collective-permute-start(bf16[16,176,128]{2,1,0:T(8,128)(2,1)} %all_to_all.71), channel_id=1, source_target_pairs={{0,1},{1,0},{2,3},{3,2},{4,5},{5,4},{6,7},{7,6},{8,9},{9,8},{10,11... | collective-permute-start | bytes 2162696 | tf_op jit(solution)/shard_map/ppermute | solution.py:29
  175.2 15.1 %copy-start.12 = (bf16[32,512]{1,0:T(8,128)(2,1)}, bf16[32,512]{1,0:T(8,128)(2,1)S(1)}, u32[]{:S(2)}) copy-start(bf16[32,512]{1,0:T(8,128)(2,1)S(1)} %get-tuple-element.39) | copy-start | bytes 98308
  184.0 26.4 %all-to-all-start.7 = ((bf16[32,176,128]{2,1,0:T(8,128)(2,1)}), bf16[32,176,128]{2,1,0:T(8,128)(2,1)}, u32[]{:S(2)}, u32[]{:S(2)}) async-start(bf16[32,176,128]{2,1,0:T(8,128)(2,1)} %pad_maximum_fusion.1), calls=%async_computation.7 | async-start | bytes 2883584 | tf_op jit(solution)/shard_map/all_to_all | solution.py:22
  218.0 12.9 %all-to-all-start.8 = ((f32[8,32,128]{2,1,0:T(8,128)}), f32[8,32,128]{2,1,0:T(8,128)S(1)}, u32[]{:S(2)}, u32[]{:S(2)}) async-start(f32[8,32,128]{2,1,0:T(8,128)} %select_maximum_fusion.2), calls=%async_computation.8 | async-start | bytes 262144 | tf_op jit(solution)/shard_map/all_to_all | solution.py:18
  235.1 13.1 %copy-start.20 = (bf16[32,512]{1,0:T(8,128)(2,1)}, bf16[32,512]{1,0:T(8,128)(2,1)S(1)}, u32[]{:S(2)}) copy-start(bf16[32,512]{1,0:T(8,128)(2,1)S(1)} %get-tuple-element.41) | copy-start | bytes 98308
  239.6 15.0 %all-to-all-start.9 = ((bf16[16,176,128]{2,1,0:T(8,128)(2,1)}), bf16[16,176,128]{2,1,0:T(8,128)(2,1)}, u32[]{:S(2)}, u32[]{:S(2)}) async-start(bf16[16,176,128]{2,1,0:T(8,128)(2,1)} %broadcast_in_dim.78), calls=%async_computation.9 | async-start | bytes 1441792 | tf_op jit(solution)/shard_map/all_to_all | solution.py:28
  248.5 14.6 %copy-start.13 = (bf16[32,512]{1,0:T(8,128)(2,1)S(1)}, bf16[32,512]{1,0:T(8,128)(2,1)}, u32[]{:S(2)}) copy-start(bf16[32,512]{1,0:T(8,128)(2,1)} %copy-done.12) | copy-start | bytes 98308
  248.5 15.1 %copy-start.17 = (bf16[32,512]{1,0:T(8,128)(2,1)S(1)}, bf16[32,512]{1,0:T(8,128)(2,1)}, u32[]{:S(2)}) copy-start(bf16[32,512]{1,0:T(8,128)(2,1)} %copy-done.16) | copy-start | bytes 98308
  248.5 15.1 %copy-start.36 = (bf16[32,32]{0,1:T(8,128)(2,1)S(1)}, bf16[32,32]{0,1:T(8,128)(2,1)}, u32[]{:S(2)}) copy-start(bf16[32,32]{0,1:T(8,128)(2,1)} %copy.416) | copy-start | bytes 6148
  254.6 28.9 %all-to-all-start.10 = ((bf16[32,176,128]{2,1,0:T(8,128)(2,1)}), bf16[32,176,128]{2,1,0:T(8,128)(2,1)}, u32[]{:S(2)}, u32[]{:S(2)}) async-start(bf16[32,176,128]{2,1,0:T(8,128)(2,1)} %pad_maximum_fusion.2), calls=%async_computation.10 | async-start | bytes 2883584 | tf_op jit(solution)/shard_map/all_to_all | solution.py:22
  263.2 28.0 %collective-permute-start.3 = (bf16[16,176,128]{2,1,0:T(8,128)(2,1)}, bf16[16,176,128]{2,1,0:T(8,128)(2,1)}, u32[]{:S(2)}, u32[]{:S(2)}) collective-permute-start(bf16[16,176,128]{2,1,0:T(8,128)(2,1)} %all-to-all-done.9), channel_id=1, source_target_pairs={{0,1},{1,0},{2,3},{3,2},{4,5},{5,4},{6,7},{7,6},{8,9},{9,8},{10,11... | collective-permute-start | bytes 2162696 | tf_op jit(solution)/shard_map/ppermute | solution.py:29
  286.8 16.1 %copy-start.6 = (f32[32,512]{1,0:T(8,128)S(1)}, f32[32,512]{1,0:T(8,128)}, u32[]{:S(2)}) copy-start(f32[32,512]{1,0:T(8,128)} %get-tuple-element.34) | copy-start | bytes 196612
  286.8 13.7 %all-to-all-start.11 = ((f32[8,32,128]{2,1,0:T(8,128)}), f32[8,32,128]{2,1,0:T(8,128)}, u32[]{:S(2)}, u32[]{:S(2)}) async-start(f32[8,32,128]{2,1,0:T(8,128)} %select_maximum_fusion.1), calls=%async_computation.11 | async-start | bytes 262144 | tf_op jit(solution)/shard_map/all_to_all | solution.py:18
  307.9 8.9 %copy-start.11 = (bf16[32,512]{1,0:T(8,128)(2,1)S(1)}, bf16[32,512]{1,0:T(8,128)(2,1)}, u32[]{:S(2)}) copy-start(bf16[32,512]{1,0:T(8,128)(2,1)} %copy-done.10) | copy-start | bytes 98308
  307.9 9.0 %copy-start.19 = (bf16[32,512]{1,0:T(8,128)(2,1)S(1)}, bf16[32,512]{1,0:T(8,128)(2,1)}, u32[]{:S(2)}) copy-start(bf16[32,512]{1,0:T(8,128)(2,1)} %copy-done.18) | copy-start | bytes 98308
  307.9 9.0 %copy-start.33 = (bf16[32,32]{1,0:T(8,128)(2,1)S(1)}, bf16[32,32]{1,0:T(8,128)(2,1)}, u32[]{:S(2)}) copy-start(bf16[32,32]{1,0:T(8,128)(2,1)} %copy-done.32) | copy-start | bytes 6148
  307.9 9.2 %copy-start.21 = (bf16[32,512]{1,0:T(8,128)(2,1)S(1)}, bf16[32,512]{1,0:T(8,128)(2,1)}, u32[]{:S(2)}) copy-start(bf16[32,512]{1,0:T(8,128)(2,1)} %copy-done.20) | copy-start | bytes 98308
  307.9 9.2 %copy-start.31 = (bf16[32,32]{1,0:T(8,128)(2,1)S(1)}, bf16[32,32]{1,0:T(8,128)(2,1)}, u32[]{:S(2)}) copy-start(bf16[32,32]{1,0:T(8,128)(2,1)} %copy-done.30) | copy-start | bytes 6148
  310.5 26.6 %all-to-all-start.12 = ((bf16[32,176,128]{2,1,0:T(8,128)(2,1)}), bf16[32,176,128]{2,1,0:T(8,128)(2,1)}, u32[]{:S(2)}, u32[]{:S(2)}) async-start(bf16[32,176,128]{2,1,0:T(8,128)(2,1)} %pad_maximum_fusion.3), calls=%async_computation.12 | async-start | bytes 2883584 | tf_op jit(solution)/shard_map/all_to_all | solution.py:22
  321.1 22.2 %copy-start.15 = (bf16[32,512]{1,0:T(8,128)(2,1)S(1)}, bf16[32,512]{1,0:T(8,128)(2,1)}, u32[]{:S(2)}) copy-start(bf16[32,512]{1,0:T(8,128)(2,1)} %copy-done.14) | copy-start | bytes 98308
  321.1 22.2 %copy-start.26 = (f32[32,512]{1,0:T(8,128)S(1)}, f32[32,512]{1,0:T(8,128)}, u32[]{:S(2)}) copy-start(f32[32,512]{1,0:T(8,128)} %convolution_add_fusion.2) | copy-start | bytes 196612
  321.1 22.2 %copy-start.35 = (bf16[32,32]{0,1:T(8,128)(2,1)S(1)}, bf16[32,32]{0,1:T(8,128)(2,1)}, u32[]{:S(2)}) copy-start(bf16[32,32]{0,1:T(8,128)(2,1)} %copy-done.34) | copy-start | bytes 6148
  321.1 22.3 %copy-start.29 = (bf16[32,32]{1,0:T(8,128)(2,1)S(1)}, bf16[32,32]{1,0:T(8,128)(2,1)}, u32[]{:S(2)}) copy-start(bf16[32,32]{1,0:T(8,128)(2,1)} %copy-done.28) | copy-start | bytes 6148
  321.2 31.8 %copy-start.25 = (bf16[32,512]{1,0:T(8,128)(2,1)S(1)}, bf16[32,512]{1,0:T(8,128)(2,1)}, u32[]{:S(2)}) copy-start(bf16[32,512]{1,0:T(8,128)(2,1)} %copy-done.24) | copy-start | bytes 98308
  339.9 12.9 %all-to-all-start.13 = ((f32[8,32,128]{2,1,0:T(8,128)}), f32[8,32,128]{2,1,0:T(8,128)S(1)}, u32[]{:S(2)}, u32[]{:S(2)}) async-start(f32[8,32,128]{2,1,0:T(8,128)} %select_maximum_fusion), calls=%async_computation.13 | async-start | bytes 262144 | tf_op jit(solution)/shard_map/all_to_all | solution.py:18
  (27 other events, 84.9 us)
